TPU v7x, 256 devices: a whole 4x4x8 slice. The times are simulated.
256 devices in a mesh: heads: 32 (over z_hi, y, x), width: 8 (over z_lo, core).
Axes of the slice: x: 4, y: 4, z: 8 (z_hi: 2, z_lo: 4; z = z_hi * 4 + z_lo), core: 2. Of those that a mesh axis runs over, the one named last changes fastest.
Arguments:
- states: bfloat16 [1536, 6144], P('heads', 'width'), may hold values from -6 to 6
- segment_ids: int32 [1536], replicated, may hold values from 0 to 11, never falling along the last dimension, each value on 1 to 1344 neighbouring positions
- attn_gain: float32 [6144], P('width'), may hold values from 0.1 to 1.9
- attn_shift: float32 [6144], P('width'), may hold values from -3 to 3
- mlp_gain: float32 [6144], P('width'), may hold values from 0.1 to 1.9
- mlp_shift: float32 [6144], P('width'), may hold values from -3 to 3
- qkv_weight: bfloat16 [6144, 18432], P('width', 'heads'), may hold values from -0.078125 to 0.078125
- qkv_bias: float32 [18432], P('heads'), may hold values from -6 to 6
- dense_weight: bfloat16 [6144, 6144], P('heads', 'width'), may hold values from -0.078125 to 0.078125
- dense_bias: float32 [6144], P('width'), may hold values from -2 to 2
- up_weight: bfloat16 [6144, 24576], P('width', 'heads'), may hold values from -0.078125 to 0.078125
- up_bias: float32 [24576], P('heads'), may hold values from -3 to 3
- down_weight: bfloat16 [24576, 6144], P('heads', 'width'), may hold values from -0.0390625 to 0.0390625
- down_bias: float32 [6144], P('width'), may hold values from -2 to 2
Outputs:
- layer_out: bfloat16 [1536, 6144], P('heads', 'width')
- key_cache: bfloat16 [1536, 6144], P('width', 'heads')
- value_cache: bfloat16 [1536, 6144], P('width', 'heads')
Inputs may be any that keep to these rules, and one draw needn't show every extreme that they name: `segment_ids`: document numbers never fall along the tokens; each document has 1 to 1344 tokens and one has exactly 1344.
All inputs are finite; a program needn't handle non-finite values.
Results may differ from a plain program's by a relative error of at most 0.017.
Values may be sent and summed in bfloat16 or wider, within the bound.
No kernel may reach another device: no remote copies, remote signals or barrier semaphores. Data moves between devices by JAX's collectives and lax.ppermute only.
A program may use at most 64 MiB of HBM per device.

v0:
```python
import jax
import jax.numpy as jnp
from jax import lax
from jax.sharding import PartitionSpec as P

HD = 96
ROT = 24
D = 6144


norm_epsilon = 1e-05


def positions_of(segments):
    count = segments.shape[0]
    row_index = jnp.arange(count, dtype=jnp.int32)
    change = jnp.concatenate([jnp.ones((1,), bool), segments[1:] != segments[:-1]])
    first = lax.cummax(jnp.where(change, row_index, 0), axis=0)
    return (row_index - first).astype(jnp.float32)


def rotary(values, positions):
    half_rot = ROT // 2
    inverse = 10000.0 ** (-(jnp.arange(half_rot, dtype=jnp.float32) * 2.0 / ROT))
    angles = positions[:, None] * inverse[None, :]
    cosine = jnp.cos(angles)[:, None, :]
    sine_part = jnp.sin(angles)[:, None, :]
    first_half = values[..., :half_rot]
    second_half = values[..., half_rot:ROT]
    return jnp.concatenate(
        [
            first_half * cosine - second_half * sine_part,
            second_half * cosine + first_half * sine_part,
            values[..., ROT:],
        ],
        axis=-1,
    )


def on_device(
    states,
    segment_ids,
    attn_gain,
    attn_shift,
    mlp_gain,
    mlp_shift,
    qkv_weight,
    qkv_bias,
    dense_weight,
    dense_bias,
    up_weight,
    up_bias,
    down_weight,
    down_bias,
):
    floats = states.astype(jnp.float32)
    row_sums, square_sums = lax.psum((jnp.sum(floats, -1), jnp.sum(floats * floats, -1)), "width")
    row_mean = (row_sums / D)[:, None]
    row_var = (square_sums / D)[:, None] - row_mean * row_mean
    normed = ((floats - row_mean) * lax.rsqrt(row_var + norm_epsilon)).astype(jnp.bfloat16)
    qkv_cols = qkv_weight.shape[1]
    heads_dev = qkv_cols // (3 * HD)
    block_f = lax.all_gather(normed, "heads", axis=0, tiled=True).astype(jnp.float32)
    attn_in = (block_f * attn_gain + attn_shift).astype(jnp.bfloat16)
    mlp_in = (block_f * mlp_gain + mlp_shift).astype(jnp.bfloat16)
    projected = jnp.concatenate(
        [
            jnp.dot(attn_in, qkv_weight, preferred_element_type=jnp.float32),
            jnp.dot(mlp_in, up_weight, preferred_element_type=jnp.float32),
        ],
        axis=1,
    )
    qkv_part = projected[:, :qkv_cols]
    up_part = projected[:, qkv_cols:]
    all_tokens = projected.shape[0]
    own_rows = all_tokens // lax.axis_size("width")
    row_zero = lax.axis_index("width") * own_rows
    positions = positions_of(segment_ids)
    own_segments = lax.dynamic_slice_in_dim(segment_ids, row_zero, own_rows)
    own_index = row_zero + jnp.arange(own_rows, dtype=jnp.int32)
    score_scale = 1.0 / HD**0.5
    own_positions = lax.dynamic_slice_in_dim(positions, row_zero, own_rows)
    qkv_own, up_own = (
        lax.psum_scatter(qkv_part, "width", scatter_dimension=0, tiled=True),
        lax.psum_scatter(up_part, "width", scatter_dimension=0, tiled=True),
    )
    shaped = (qkv_own + qkv_bias).reshape(qkv_own.shape[0], heads_dev, 3, HD)
    queries = rotary(shaped[:, :, 0, :], own_positions).astype(jnp.bfloat16)
    keys_part = rotary(shaped[:, :, 1, :], own_positions).astype(jnp.bfloat16)
    values_part = shaped[:, :, 2, :].astype(jnp.bfloat16)
    width_cols = heads_dev * HD
    key_cache = keys_part.reshape(-1, width_cols)
    value_cache = values_part.reshape(-1, width_cols)
    run_max = jnp.full((heads_dev, own_rows), -1e30, jnp.float32)
    key_rows = lax.all_gather(key_cache, "width", axis=0, tiled=True)
    value_rows = lax.all_gather(value_cache, "width", axis=0, tiled=True)
    count = key_rows.shape[0]
    key_heads = key_rows.reshape(count, heads_dev, HD)
    value_heads = value_rows.reshape(count, heads_dev, HD)
    scores = (
        jnp.einsum("rhd,nhd->hrn", queries, key_heads, preferred_element_type=jnp.float32)
        * score_scale
    )
    key_index = jnp.arange(count, dtype=jnp.int32)
    allowed = (own_segments[:, None] == segment_ids[None, :]) & (
        key_index[None, :] <= own_index[:, None]
    )
    scores = jnp.where(allowed[None], scores, -1e30)
    new_max = jnp.maximum(run_max, jnp.max(scores, -1))
    weights = jnp.where(allowed[None], jnp.exp(scores - new_max[..., None]), 0.0)
    new_sum = jnp.sum(weights, -1)
    mixed = jnp.einsum(
        "hrn,nhd->hrd",
        weights.astype(jnp.bfloat16),
        value_heads,
        preferred_element_type=jnp.float32,
    )
    attended = (
        (mixed / new_sum[..., None])
        .transpose(1, 0, 2)
        .reshape(own_rows, heads_dev * HD)
        .astype(jnp.bfloat16)
    )
    attn_part = jnp.dot(
        lax.all_gather(attended, "width", axis=0, tiled=True),
        dense_weight,
        preferred_element_type=jnp.float32,
    )
    hidden = jax.nn.gelu(up_own + up_bias, approximate=False).astype(jnp.bfloat16)
    mlp_part = jnp.dot(
        lax.all_gather(hidden, "width", axis=0, tiled=True),
        down_weight,
        preferred_element_type=jnp.float32,
    )
    summed = lax.psum_scatter(
        attn_part.astype(jnp.bfloat16), "heads", scatter_dimension=0, tiled=True
    ).astype(jnp.float32) + lax.psum_scatter(
        mlp_part.astype(jnp.bfloat16), "heads", scatter_dimension=0, tiled=True
    ).astype(
        jnp.float32
    )
    layer_out = (floats + summed + dense_bias + down_bias).astype(jnp.bfloat16)
    return (layer_out, key_cache, value_cache)


def solution(mesh):
    in_specs = (
        P("heads", "width"),
        P(),
        P("width"),
        P("width"),
        P("width"),
        P("width"),
        P("width", "heads"),
        P("heads"),
        P("heads", "width"),
        P("width"),
        P("width", "heads"),
        P("heads"),
        P("heads", "width"),
        P("width"),
    )
    out_specs = (P("heads", "width"), P("width", "heads"), P("width", "heads"))
    return jax.shard_map(
        on_device, mesh=mesh, in_specs=in_specs, out_specs=out_specs, check_vma=False
    )
```

profile of v0, /device:TPU:96, one launch (start us, length us, event | category | flops | bytes accessed | tf_op | source)
XLA Modules:
  0.0 822.3 jit_solution(1113341373791377234)
XLA Ops:
  7.2 1.1 convert_reduce_fusion
  8.3 11.1 %all-reduce = (f32[48]{0:T(128)S(1)}, f32[48]{0:T(128)S(1)}) all-reduce(f32[48]{0:T(128)S(1)} %get-tuple-element.13, f32[48]{0:T(128)S(1)} %get-tuple-element.12), channel_id=1, replica_groups=mesh['heads'=32,'width'=8] {'width'}, use_global_device_ids=true, to_apply=%region_3.0 | all-reduce | flops 96 | bytes 768 | tf_op jit(solution)/shard_map/psum | solution.py:57
  19.5 1.6 fusion.41
  21.1 96.7 %all-gather.3.cloned.1.call-done = bf16[1536,768]{1,0:T(8,128)(2,1)} async-done(((bf16[48,768]{1,0:T(8,128)(2,1)}), bf16[1536,768]{1,0:T(8,128)(2,1)}) %all-gather.3.cloned.1.call-update) | async-done | bytes 2359312 | tf_op jit(solution)/shard_map/all_gather | solution.py:63
  117.8 5.8 fusion.5
  123.7 1.6 copy-done.10
  125.3 5.1 fusion.7
  130.5 0.6 copy-done.5
  131.2 0.1 dynamic_slice.6
  131.2 0.1 slice_compare_fusion
  131.3 0.1 add_select_fusion
  131.4 0.3 reduce-window.9
  131.7 0.1 slice.58
  131.8 0.1 slice_reduce_fusion
  131.9 46.0 %reduce-scatter.9.cloned.1.call-done = f32[192,768]{1,0:T(8,128)} async-done(((f32[1536,768]{1,0:T(8,128)}), f32[192,768]{1,0:T(8,128)}) %reduce-scatter.9.cloned.1.call-update) | async-done | bytes 589840 | tf_op jit(solution)/shard_map/reduce_scatter | solution.py:85
  177.9 3.1 fusion.32
  181.1 0.1 fusion.51
  181.2 0.1 multiply_cosine_fusion
  181.4 0.1 copy.40
  181.5 0.1 copy.41
  181.6 0.5 fusion.19
  182.1 49.3 %reduce-scatter.5.cloned.1.call-done = f32[192,576]{1,0:T(8,128)} async-done(((f32[1536,576]{1,0:T(8,128)}), f32[192,576]{1,0:T(8,128)}) %reduce-scatter.5.cloned.1.call-update) | async-done | bytes 442384 | tf_op jit(solution)/shard_map/reduce_scatter | solution.py:84
  231.4 1.1 broadcast_add_fusion
  232.5 0.2 copy.38
  232.8 0.1 copy.51
  232.9 0.8 copy.46
  233.6 0.1 slice.83
  233.7 0.1 copy.52
  233.9 0.1 slice.82
  234.0 0.8 subtract_convert_fusion.1
  234.8 0.1 pad_maximum_fusion
  235.0 0.1 copy.43
  235.1 0.1 copy.44
  235.2 18.6 %all_gather.16 = bf16[1536,192]{1,0:T(8,128)(2,1)S(1)} all-gather(bf16[192,192]{1,0:T(8,128)(2,1)S(1)} %copy.44), channel_id=1, replica_groups=mesh['heads'=32,'width'=8] {'width'}, dimensions={0}, use_global_device_ids=true | all-gather | bytes 663552 | tf_op jit(solution)/shard_map/all_gather | solution.py:95
  253.7 0.3 copy.45
  254.0 19.3 %all_gather.17 = bf16[1536,192]{1,0:T(8,128)(2,1)S(1)} all-gather(bf16[192,192]{1,0:T(8,128)(2,1)S(1)} %copy-done.2), channel_id=1, replica_groups=mesh['heads'=32,'width'=8] {'width'}, dimensions={0}, use_global_device_ids=true | all-gather | bytes 663552 | tf_op jit(solution)/shard_map/all_gather | solution.py:96
  273.4 0.3 copy.47
  273.6 1.8 fusion.55
  275.4 0.7 fusion.13
  276.1 0.7 fusion.27
  276.8 0.1 copy.48
  276.9 16.1 %all_gather.18 = bf16[1536,192]{1,0:T(8,128)(2,1)S(1)} all-gather(bf16[192,192]{1,0:T(8,128)(2,1)S(1)} %copy.48), channel_id=1, replica_groups=mesh['heads'=32,'width'=8] {'width'}, dimensions={0}, use_global_device_ids=true | all-gather | bytes 663552 | tf_op jit(solution)/shard_map/all_gather | solution.py:125
  293.0 2.2 convolution_convert_fusion.1
  295.3 1.2 copy-done.11
  296.5 5.1 convolution_convert_fusion
  301.6 251.7 %reduce-scatter.7.cloned.1.call-done = bf16[48,768]{1,0:T(8,128)(2,1)} async-done(((bf16[1536,768]{1,0:T(8,128)(2,1)}), bf16[48,768]{1,0:T(8,128)(2,1)}) %reduce-scatter.7.cloned.1.call-update) | async-done | bytes 73744 | tf_op jit(solution)/shard_map/reduce_scatter | solution.py:135
  553.4 260.5 %reduce-scatter.11.cloned.1.call-done = bf16[48,768]{1,0:T(8,128)(2,1)} async-done(((bf16[1536,768]{1,0:T(8,128)(2,1)}), bf16[48,768]{1,0:T(8,128)(2,1)}) %reduce-scatter.11.cloned.1.call-update) | async-done | bytes 73744 | tf_op jit(solution)/shard_map/reduce_scatter | solution.py:137
  813.8 1.6 fusion.45
  (46 shorter events, 0.6 us)
Async XLA Ops:
  7.2 110.7 %copy-start = (bf16[768,768]{1,0:T(8,128)(2,1)S(1)}, bf16[768,768]{1,0:T(8,128)(2,1)}, u32[]{:S(2)}) copy-start(bf16[768,768]{1,0:T(8,128)(2,1)} %param.24) | copy-start | bytes 3538948
  7.2 110.6 %all-gather.3.cloned.1.call-start = ((), (), s32[]{:S(2)}) async-start(), calls=%async_computation.4 | async-start | bytes 2433024 | tf_op jit(solution)/shard_map/all_gather | solution.py:63
  21.1 156.8 %reduce-scatter.9.cloned.1.call-start = ((), (), s32[]{:S(2)}) async-start(), calls=%async_computation.7 | async-start | bytes 5308416 | tf_op jit(solution)/shard_map/reduce_scatter | solution.py:85
  123.7 1.7 copy-start.10
  123.7 1.7 copy-start.12
  123.7 1.7 copy-start.13
  123.7 107.7 %reduce-scatter.5.cloned.1.call-start = ((), (), s32[]{:S(2)}) async-start(), calls=%async_computation.5 | async-start | bytes 4423680 | tf_op jit(solution)/shard_map/reduce_scatter | solution.py:84
  130.5 0.7 copy-start.5
  130.5 47.5 %copy-start.6 = (f32[768]{0:T(1024)S(1)}, f32[768]{0:T(1024)}, u32[]{:S(2)}) copy-start(f32[768]{0:T(1024)} %param.25) | copy-start | bytes 9220
  130.5 101.0 %copy-start.7 = (f32[576]{0:T(1024)S(1)}, f32[576]{0:T(1024)}, u32[]{:S(2)}) copy-start(f32[576]{0:T(1024)} %param.21) | copy-start | bytes 6916
  130.5 164.8 %all-gather.5.cloned.1.call-start = ((), (), s32[]{:S(2)}) async-start(), calls=%async_computation.8 | async-start | bytes 2654208 | tf_op jit(solution)/shard_map/all_gather | solution.py:131
  181.0 372.3 %reduce-scatter.7.cloned.1.call-start = ((), (), s32[]{:S(2)}) async-start(), calls=%async_computation.6 | async-start | bytes 2433024 | tf_op jit(solution)/shard_map/reduce_scatter | solution.py:135
  233.9 20.1 %copy-start.2 = (bf16[192,192]{1,0:T(8,128)(2,1)S(1)}, bf16[192,192]{1,0:T(8,128)(2,1)}, u32[]{:S(2)}) copy-start(bf16[192,192]{1,0:T(8,128)(2,1)} %copy.46) | copy-start | bytes 221188
  235.2 18.8 %copy-start.3 = (bf16[192,192]{1,0:T(8,128)(2,1)}, bf16[192,192]{1,0:T(8,128)(2,1)S(1)}, u32[]{:S(2)}) copy-start(bf16[192,192]{1,0:T(8,128)(2,1)S(1)} %copy.44) | copy-start | bytes 221188
  276.1 16.9 %copy-start.4 = (bf16[192,768]{1,0:T(8,128)(2,1)S(1)}, bf16[192,768]{1,0:T(8,128)(2,1)}, u32[]{:S(2)}) copy-start(bf16[192,768]{1,0:T(8,128)(2,1)} %param.22) | copy-start | bytes 884740
  295.2 1.3 copy-start.11
  295.2 518.6 %reduce-scatter.11.cloned.1.call-start = ((), (), s32[]{:S(2)}) async-start(), calls=%async_computation.9 | async-start | bytes 2433024 | tf_op jit(solution)/shard_map/reduce_scatter | solution.py:137
  301.6 512.2 %copy-start.1 = (bf16[48,768]{1,0:T(8,128)(2,1)S(1)}, bf16[48,768]{1,0:T(8,128)(2,1)}, u32[]{:S(2)}) copy-start(bf16[48,768]{1,0:T(8,128)(2,1)} %param.14) | copy-start | bytes 221188
  301.6 512.2 %copy-start.8 = (f32[768]{0:T(1024)S(1)}, f32[768]{0:T(1024)}, u32[]{:S(2)}) copy-start(f32[768]{0:T(1024)} %param.27) | copy-start | bytes 9220
  301.6 512.2 %copy-start.9 = (f32[768]{0:T(1024)S(1)}, f32[768]{0:T(1024)}, u32[]{:S(2)}) copy-start(f32[768]{0:T(1024)} %param.23) | copy-start | bytes 9220
Sparse Core Ops, SparseCore 0:
  21.2 96.5 all-gather.2
  123.8 54.0 reduce-scatter.8
  180.5 50.8 reduce-scatter.4
  233.1 44.6 all-gather.4
  295.3 257.9 reduce-scatter.6
  558.6 255.1 reduce-scatter.10
where the time goes:
time: 826 us; the launch traced here: 822 us
  waiting for transfers between devices  704 us (85%)
  blocking collectives  65.1 us (8%)
  matrix products  20.7 us (3%)
  between operations  14.3 us (2%)
  other arithmetic  11.4 us (1%)
    reduce_scatter x1, waiting for transfers between devices, on_device(): lax.psum_scatter(mlp_part.astype(jnp.bfloat16), 'heads', scatter_dimensio...  260 us
    reduce_scatter x1, waiting for transfers between devices, on_device(): lax.psum_scatter(attn_part.astype(jnp.bfloat16), 'heads', scatter_dimensi...  252 us
    all_gather x1, waiting for transfers between devices, on_device(): lax.all_gather(normed, 'heads', axis=0, tiled=True).astype(jnp.float32)  96.7 us
    reduce_scatter x1, waiting for transfers between devices, on_device(): lax.psum_scatter(qkv_part, 'width', scatter_dimension=0, tiled=True)  49.3 us
    reduce_scatter x1, waiting for transfers between devices, on_device(): lax.psum_scatter(up_part, 'width', scatter_dimension=0, tiled=True)  46 us
    all_gather x1, blocking collectives, on_device(): value_rows = lax.all_gather(value_cache, 'width', axis=0, tiled=True)  19.3 us
    all_gather x1, blocking collectives, on_device(): key_rows = lax.all_gather(key_cache, 'width', axis=0, tiled=True)  18.6 us
  transfers between devices with their start and end apart: 6, of which 5 were waited for; matrix products, arithmetic and copies ran while one was open for 3% of the time, Pallas kernels for 0%

commit v1 on v0

--- a/solution.py
+++ b/solution.py
@@ -60,7 +60,13 @@
     normed = ((floats - row_mean) * lax.rsqrt(row_var + norm_epsilon)).astype(jnp.bfloat16)
     qkv_cols = qkv_weight.shape[1]
     heads_dev = qkv_cols // (3 * HD)
-    block_f = lax.all_gather(normed, "heads", axis=0, tiled=True).astype(jnp.float32)
+    heads_n = lax.axis_size("heads")
+    spread = jnp.broadcast_to(normed[None], (heads_n,) + normed.shape)
+    block_f = (
+        lax.all_to_all(spread, "heads", 0, 0, tiled=False)
+        .reshape(heads_n * normed.shape[0], normed.shape[1])
+        .astype(jnp.float32)
+    )
     attn_in = (block_f * attn_gain + attn_shift).astype(jnp.bfloat16)
     mlp_in = (block_f * mlp_gain + mlp_shift).astype(jnp.bfloat16)
     projected = jnp.concatenate(
@@ -132,12 +138,10 @@
         down_weight,
         preferred_element_type=jnp.float32,
     )
-    summed = lax.psum_scatter(
-        attn_part.astype(jnp.bfloat16), "heads", scatter_dimension=0, tiled=True
-    ).astype(jnp.float32) + lax.psum_scatter(
-        mlp_part.astype(jnp.bfloat16), "heads", scatter_dimension=0, tiled=True
-    ).astype(
-        jnp.float32
+    partial = (attn_part + mlp_part).astype(jnp.bfloat16)
+    pieces = partial.reshape(heads_n, partial.shape[0] // heads_n, partial.shape[1])
+    summed = jnp.sum(
+        lax.all_to_all(pieces, "heads", 0, 0, tiled=False).astype(jnp.float32), 0
     )
     layer_out = (floats + summed + dense_bias + down_bias).astype(jnp.bfloat16)
     return (layer_out, key_cache, value_cache)

time: 826 us -> 351 us (0.42)
  waiting for transfers between devices: 704 us -> 98.6 us
  blocking collectives: 65.1 us -> 203 us
    reduce_scatter x2 -> x0, waiting for transfers between devices: 512 us -> none  [the longest x1 260 us: on_device(): lax.psum_scatter(mlp_part.astype(jnp.bfloat16), 'heads', scatter_dimensio...]
    all_to_all x0 -> x2, blocking collectives: none -> 138 us  [the longest x1 69.9 us: on_device(): lax.all_to_all(spread, 'heads', 0, 0, tiled=False)]
    all_gather x1 -> x0, waiting for transfers between devices: 96.7 us -> none  [on_device(): lax.all_gather(normed, 'heads', axis=0, tiled=True).astype(jnp.float32)]
  transfers between devices with their start and end apart: 6 -> 3, of which waited for: 5 -> 2; matrix products, arithmetic and copies ran while one was open for 3% -> 5% of each run, Pallas kernels for 0% -> 0%
where the time goes in v1:
time: 351 us; the launch traced here: 347 us
  blocking collectives  203 us (58%)
  waiting for transfers between devices  98.6 us (28%)
  matrix products  16.2 us (5%)
  between operations  14 us (4%)
  other arithmetic  10.1 us (3%)
  local copies, waits for them, and re-layouts  4.74 us (1%)
    all_to_all x1, blocking collectives, on_device(): lax.all_to_all(spread, 'heads', 0, 0, tiled=False)  69.9 us
    all_to_all x1, blocking collectives, on_device(): lax.all_to_all(pieces, 'heads', 0, 0, tiled=False).astype(jnp.float32)  68.3 us
    reduce_scatter x1, waiting for transfers between devices, on_device(): lax.psum_scatter(up_part, 'width', scatter_dimension=0, tiled=True)  49.9 us
    reduce_scatter x1, waiting for transfers between devices, on_device(): lax.psum_scatter(qkv_part, 'width', scatter_dimension=0, tiled=True)  48.7 us
    all_gather x1, blocking collectives, on_device(): value_rows = lax.all_gather(value_cache, 'width', axis=0, tiled=True)  19.4 us
    all_gather x1, blocking collectives, on_device(): key_rows = lax.all_gather(key_cache, 'width', axis=0, tiled=True)  18.3 us
    all_gather x1, blocking collectives, on_device(): lax.all_gather(attended, 'width', axis=0, tiled=True)  16.3 us
    psum x1, blocking collectives, on_device(): lax.psum((jnp.sum(floats, -1), jnp.sum(floats * floats, -1)), 'width')  11.1 us
  transfers between devices with their start and end apart: 3, of which 2 were waited for; matrix products, arithmetic and copies ran while one was open for 5% of the time, Pallas kernels for 0%

profile of v1, /device:TPU:96, one launch (start us, length us, event | category | flops | bytes accessed | tf_op | source)
XLA Modules:
  0.0 347.2 jit_solution(5073449171978128970)
XLA Ops:
  7.2 1.1 convert_reduce_fusion.1
  8.3 11.1 %all-reduce = (f32[48]{0:T(128)S(1)}, f32[48]{0:T(128)S(1)}) all-reduce(f32[48]{0:T(128)S(1)} %get-tuple-element.13, f32[48]{0:T(128)S(1)} %get-tuple-element.12), channel_id=1, replica_groups=mesh['heads'=32,'width'=8] {'width'}, use_global_device_ids=true, to_apply=%region_3.0 | all-reduce | flops 96 | bytes 768 | tf_op jit(solution)/shard_map/psum | solution.py:57
  19.5 1.0 fusion.41
  20.4 0.2 broadcast_in_dim.23
  20.6 69.9 %all_to_all.10 = bf16[32,48,768]{2,1,0:T(8,128)(2,1)S(1)} all-to-all(bf16[32,48,768]{2,1,0:T(8,128)(2,1)S(1)} %broadcast_in_dim.23), channel_id=1, replica_groups=mesh['heads'=32,'width'=8] {'heads'}, dimensions={0} | all-to-all | bytes 4718592 | tf_op jit(solution)/shard_map/all_to_all | solution.py:66
  90.5 4.2 %fusion.5 = f32[1536,768]{1,0:T(8,128)} fusion(bf16[768,768]{1,0:T(8,128)(2,1)S(1)} %copy-done, bf16[1536,768]{1,0:T(8,128)(2,1)S(1)} %bitcast.37, f32[768]{0:T(1024)S(1)} %copy-done.11, f32[768]{0:T(1024)S(1)} %copy-done.12), kind=kOutput, calls=%fused_computation.10 | convolution fusion | flops 1816657920 | bytes 8263680 | tf_op jit(solution)/shard_map/dot_general | solution.py:75
  94.7 0.6 copy-done.13
  95.4 5.1 %fusion.7 = f32[1536,576]{1,0:T(8,128)} fusion(bf16[768,576]{0,1:T(8,128)(2,1)} %param.20, bf16[1536,768]{1,0:T(8,128)(2,1)S(1)} %bitcast.38, f32[768]{0:T(1024)S(1)} %copy-done.13, f32[768]{0:T(1024)S(1)} %copy-done.14), kind=kOutput, calls=%fused_computation.11 | convolution fusion | flops 1363673088 | bytes 6789120 | tf_op jit(solution)/shard_map/dot_general | solution.py:74
  100.5 0.6 copy-done.5
  101.2 0.1 slice_compare_fusion
  101.2 49.9 %reduce-scatter.5.cloned.1.call-done = f32[192,768]{1,0:T(8,128)} async-done(((f32[1536,768]{1,0:T(8,128)}), f32[192,768]{1,0:T(8,128)}) %reduce-scatter.5.cloned.1.call-update) | async-done | bytes 589840 | tf_op jit(solution)/shard_map/reduce_scatter | solution.py:91
  151.1 3.1 fusion.32
  154.2 0.1 add_select_fusion
  154.3 0.1 dynamic_slice.6
  154.4 0.3 reduce-window.9
  154.8 0.1 slice_reduce_fusion
  155.0 0.1 fusion.51
  155.1 0.1 multiply_cosine_fusion
  155.2 0.1 copy.40
  155.3 0.1 copy.41
  155.4 0.5 fusion.19
  155.9 48.7 %reduce-scatter.3.cloned.1.call-done = f32[192,576]{1,0:T(8,128)} async-done(((f32[1536,576]{1,0:T(8,128)}), f32[192,576]{1,0:T(8,128)}) %reduce-scatter.3.cloned.1.call-update) | async-done | bytes 442384 | tf_op jit(solution)/shard_map/reduce_scatter | solution.py:90
  204.6 1.1 broadcast_add_fusion
  205.7 0.2 copy.38
  205.9 0.1 copy.51
  206.1 0.8 copy.46
  206.8 0.1 slice.83
  206.9 0.1 copy.52
  207.1 0.1 slice.82
  207.2 0.8 subtract_convert_fusion.1
  208.0 0.1 pad_maximum_fusion
  208.1 0.1 copy.43
  208.2 0.1 copy.44
  208.4 18.3 %all_gather.12 = bf16[1536,192]{1,0:T(8,128)(2,1)S(1)} all-gather(bf16[192,192]{1,0:T(8,128)(2,1)S(1)} %copy.44), channel_id=1, replica_groups=mesh['heads'=32,'width'=8] {'width'}, dimensions={0}, use_global_device_ids=true | all-gather | bytes 663552 | tf_op jit(solution)/shard_map/all_gather | solution.py:101
  226.6 0.3 copy.45
  226.9 19.4 %all_gather.13 = bf16[1536,192]{1,0:T(8,128)(2,1)S(1)} all-gather(bf16[192,192]{1,0:T(8,128)(2,1)S(1)} %copy-done.2), channel_id=1, replica_groups=mesh['heads'=32,'width'=8] {'width'}, dimensions={0}, use_global_device_ids=true | all-gather | bytes 663552 | tf_op jit(solution)/shard_map/all_gather | solution.py:102
  246.4 0.3 copy.47
  246.6 1.7 fusion.55
  248.4 0.7 fusion.13
  249.1 0.7 fusion.27
  249.8 0.1 copy.48
  249.9 16.3 %all_gather.14 = bf16[1536,192]{1,0:T(8,128)(2,1)S(1)} all-gather(bf16[192,192]{1,0:T(8,128)(2,1)S(1)} %copy.48), channel_id=1, replica_groups=mesh['heads'=32,'width'=8] {'width'}, dimensions={0}, use_global_device_ids=true | all-gather | bytes 663552 | tf_op jit(solution)/shard_map/all_gather | solution.py:131
  266.2 3.7 %fusion.56 = f32[1536,768]{1,0:T(8,128)S(1)} fusion(bf16[1536,768]{1,0:T(8,128)(2,1)} %all-gather.2.cloned.1.call-done, bf16[768,768]{1,0:T(8,128)(2,1)S(1)} %copy-done.10), kind=kOutput, calls=%fused_computation.89 | convolution fusion | flops 1811939328 | bytes 8257536 | tf_op jit(solution)/shard_map/dot_general | solution.py:136
  270.0 0.8 add_convert_fusion
  270.8 68.3 %all_to_all.11 = bf16[32,48,768]{2,1,0:T(8,128)(2,1)S(1)} all-to-all(bf16[32,48,768]{2,1,0:T(8,128)(2,1)S(1)} %bitcast.32), channel_id=1, replica_groups=mesh['heads'=32,'width'=8] {'heads'}, dimensions={0} | all-to-all | bytes 4718592 | tf_op jit(solution)/shard_map/all_to_all | solution.py:144
  339.1 0.3 convert_reduce_fusion
  339.4 0.6 copy-done.1
  340.0 0.7 fusion.45
  (43 shorter events, 0.5 us)
Async XLA Ops:
  7.2 83.3 %copy-start = (bf16[768,768]{1,0:T(8,128)(2,1)S(1)}, bf16[768,768]{1,0:T(8,128)(2,1)}, u32[]{:S(2)}) copy-start(bf16[768,768]{1,0:T(8,128)(2,1)} %param.24) | copy-start | bytes 3538948
  7.2 143.9 %reduce-scatter.5.cloned.1.call-start = ((), (), s32[]{:S(2)}) async-start(), calls=%async_computation.5 | async-start | bytes 5308416 | tf_op jit(solution)/shard_map/reduce_scatter | solution.py:91
  20.6 69.9 %copy-start.11 = (f32[768]{0:T(1024)S(1)}, f32[768]{0:T(1024)}, u32[]{:S(2)}) copy-start(f32[768]{0:T(1024)} %param.19) | copy-start | bytes 9220
  20.6 69.9 %copy-start.12 = (f32[768]{0:T(1024)S(1)}, f32[768]{0:T(1024)}, u32[]{:S(2)}) copy-start(f32[768]{0:T(1024)} %param.18) | copy-start | bytes 9220
  94.7 0.7 copy-start.13
  94.7 0.7 copy-start.14
  94.7 109.9 %reduce-scatter.3.cloned.1.call-start = ((), (), s32[]{:S(2)}) async-start(), calls=%async_computation.4 | async-start | bytes 4423680 | tf_op jit(solution)/shard_map/reduce_scatter | solution.py:90
  100.5 0.7 copy-start.5
  100.5 50.7 %copy-start.6 = (f32[768]{0:T(1024)S(1)}, f32[768]{0:T(1024)}, u32[]{:S(2)}) copy-start(f32[768]{0:T(1024)} %param.25) | copy-start | bytes 9220
  100.5 104.1 %copy-start.7 = (f32[576]{0:T(1024)S(1)}, f32[576]{0:T(1024)}, u32[]{:S(2)}) copy-start(f32[576]{0:T(1024)} %param.21) | copy-start | bytes 6916
  100.5 165.7 %all-gather.2.cloned.1.call-start = ((), (), s32[]{:S(2)}) async-start(), calls=%async_computation.6 | async-start | bytes 2654208 | tf_op jit(solution)/shard_map/all_gather | solution.py:137
  207.0 19.9 %copy-start.2 = (bf16[192,192]{1,0:T(8,128)(2,1)S(1)}, bf16[192,192]{1,0:T(8,128)(2,1)}, u32[]{:S(2)}) copy-start(bf16[192,192]{1,0:T(8,128)(2,1)} %copy.46) | copy-start | bytes 221188
  208.3 18.6 %copy-start.3 = (bf16[192,192]{1,0:T(8,128)(2,1)}, bf16[192,192]{1,0:T(8,128)(2,1)S(1)}, u32[]{:S(2)}) copy-start(bf16[192,192]{1,0:T(8,128)(2,1)S(1)} %copy.44) | copy-start | bytes 221188
  249.1 17.1 %copy-start.10 = (bf16[768,768]{1,0:T(8,128)(2,1)S(1)}, bf16[768,768]{1,0:T(8,128)(2,1)}, u32[]{:S(2)}) copy-start(bf16[768,768]{1,0:T(8,128)(2,1)} %param.26) | copy-start | bytes 3538948
  266.2 3.8 %copy-start.4 = (bf16[192,768]{1,0:T(8,128)(2,1)S(1)}, bf16[192,768]{1,0:T(8,128)(2,1)}, u32[]{:S(2)}) copy-start(bf16[192,768]{1,0:T(8,128)(2,1)} %param.22) | copy-start | bytes 884740
  339.1 0.9 copy-start.1
  339.1 0.9 copy-start.8
  339.1 0.9 copy-start.9
Sparse Core Ops, SparseCore 0:
  94.8 56.2 reduce-scatter.4
  153.7 50.8 reduce-scatter.2
  206.4 44.6 all-gather.1

commit v2 on v1

--- a/solution.py
+++ b/solution.py
@@ -86,10 +86,9 @@
     own_index = row_zero + jnp.arange(own_rows, dtype=jnp.int32)
     score_scale = 1.0 / HD**0.5
     own_positions = lax.dynamic_slice_in_dim(positions, row_zero, own_rows)
-    qkv_own, up_own = (
-        lax.psum_scatter(qkv_part, "width", scatter_dimension=0, tiled=True),
-        lax.psum_scatter(up_part, "width", scatter_dimension=0, tiled=True),
-    )
+    qkv_own = lax.psum_scatter(
+        qkv_part.astype(jnp.bfloat16), "width", scatter_dimension=0, tiled=True
+    ).astype(jnp.float32)
     shaped = (qkv_own + qkv_bias).reshape(qkv_own.shape[0], heads_dev, 3, HD)
     queries = rotary(shaped[:, :, 0, :], own_positions).astype(jnp.bfloat16)
     keys_part = rotary(shaped[:, :, 1, :], own_positions).astype(jnp.bfloat16)
@@ -98,8 +97,15 @@
     key_cache = keys_part.reshape(-1, width_cols)
     value_cache = values_part.reshape(-1, width_cols)
     run_max = jnp.full((heads_dev, own_rows), -1e30, jnp.float32)
-    key_rows = lax.all_gather(key_cache, "width", axis=0, tiled=True)
-    value_rows = lax.all_gather(value_cache, "width", axis=0, tiled=True)
+    kv_rows = lax.all_gather(
+        jnp.concatenate([key_cache, value_cache], axis=1), "width", axis=0, tiled=True
+    )
+    kv_rows, up_part = lax.optimization_barrier((kv_rows, up_part))
+    up_own = lax.psum_scatter(
+        up_part.astype(jnp.bfloat16), "width", scatter_dimension=0, tiled=True
+    ).astype(jnp.float32)
+    key_rows = kv_rows[:, :width_cols]
+    value_rows = kv_rows[:, width_cols:]
     count = key_rows.shape[0]
     key_heads = key_rows.reshape(count, heads_dev, HD)
     value_heads = value_rows.reshape(count, heads_dev, HD)

time: 351 us -> 346 us (0.986)
  blocking collectives: 203 us -> 102 us
  waiting for transfers between devices: 98.6 us -> 178 us
  starting transfers between devices: 0.12 us -> 10.5 us
  local copies, waits for them, and re-layouts: 4.74 us -> 10.7 us
    all_to_all x1 -> x0, blocking collectives: 68.3 us -> none  [on_device(): lax.all_to_all(pieces, 'heads', 0, 0, tiled=False).astype(jnp.float32)]
    all_to_all x0 -> x1, waiting for transfers between devices: none -> 52.8 us  [on_device(): lax.all_to_all(pieces, 'heads', 0, 0, tiled=False).astype(jnp.float32)]
    all_gather x2 -> x0, blocking collectives: 37.7 us -> none  [the longest x1 19.4 us: on_device(): value_rows = lax.all_gather(value_cache, 'width', axis=0, tiled=True)]
    all_gather x0 -> x1, waiting for transfers between devices: none -> 31.2 us  [on_device(): lax.all_gather(jnp.concatenate([key_cache, value_cache], axis=1), 'width'...]
    reduce_scatter x2, waiting for transfers between devices: 98.6 us -> 78.3 us  [the longest x1 43.3 us: on_device(): lax.psum_scatter(up_part.astype(jnp.bfloat16), 'width', scatter_dimension...]
    all_gather x1, waiting for transfers between devices: 0.01 us -> 15.3 us  [on_device(): lax.all_gather(hidden, 'width', axis=0, tiled=True)]
    all_to_all x0 -> x1, starting transfers between devices: none -> 10.3 us  [on_device(): lax.all_to_all(pieces, 'heads', 0, 0, tiled=False).astype(jnp.float32)]
    all_gather x1, blocking collectives: 16.3 us -> 20.9 us  [on_device(): lax.all_gather(attended, 'width', axis=0, tiled=True)]
  transfers between devices with their start and end apart: 3 -> 5, of which waited for: 2 -> 5; matrix products, arithmetic and copies ran while one was open for 5% -> 5% of each run, Pallas kernels for 0% -> 0%
where the time goes in v2:
time: 346 us; the launch traced here: 342 us
  waiting for transfers between devices  178 us (51%)
  blocking collectives  102 us (29%)
  matrix products  17.2 us (5%)
  between operations  14.1 us (4%)
  local copies, waits for them, and re-layouts  10.7 us (3%)
  starting transfers between devices  10.5 us (3%)
  other arithmetic  9.39 us (3%)
    all_to_all x1, blocking collectives, on_device(): lax.all_to_all(spread, 'heads', 0, 0, tiled=False)  70 us
    all_to_all x1, waiting for transfers between devices, on_device(): lax.all_to_all(pieces, 'heads', 0, 0, tiled=False).astype(jnp.float32)  52.8 us
    reduce_scatter x1, waiting for transfers between devices, on_device(): lax.psum_scatter(up_part.astype(jnp.bfloat16), 'width', scatter_dimension...  43.3 us
    reduce_scatter x1, waiting for transfers between devices, on_device(): lax.psum_scatter(qkv_part.astype(jnp.bfloat16), 'width', scatter_dimensio...  35 us
    all_gather x1, waiting for transfers between devices, on_device(): lax.all_gather(jnp.concatenate([key_cache, value_cache], axis=1), 'width'...  31.2 us
    all_gather x1, blocking collectives, on_device(): lax.all_gather(attended, 'width', axis=0, tiled=True)  20.9 us
    all_gather x1, waiting for transfers between devices, on_device(): lax.all_gather(hidden, 'width', axis=0, tiled=True)  15.3 us
    psum x1, blocking collectives, on_device(): lax.psum((jnp.sum(floats, -1), jnp.sum(floats * floats, -1)), 'width')  11.1 us
  transfers between devices with their start and end apart: 5, of which 5 were waited for; matrix products, arithmetic and copies ran while one was open for 5% of the time, Pallas kernels for 0%

profile of v2, /device:TPU:96, one launch (start us, length us, event | category | flops | bytes accessed | tf_op | source)
XLA Modules:
  0.0 341.5 jit_solution(11315111861965429610)
XLA Ops:
  7.2 1.1 convert_reduce_fusion.1
  8.3 11.1 %all-reduce = (f32[48]{0:T(128)S(1)}, f32[48]{0:T(128)S(1)}) all-reduce(f32[48]{0:T(128)S(1)} %get-tuple-element.17, f32[48]{0:T(128)S(1)} %get-tuple-element.16), channel_id=1, replica_groups=mesh['heads'=32,'width'=8] {'width'}, use_global_device_ids=true, to_apply=%region_3.0 | all-reduce | flops 96 | bytes 768 | tf_op jit(solution)/shard_map/psum | solution.py:57
  19.5 1.0 fusion.43
  20.4 0.2 broadcast_in_dim.23
  20.6 70.0 %all_to_all.10 = bf16[32,48,768]{2,1,0:T(8,128)(2,1)S(1)} all-to-all(bf16[32,48,768]{2,1,0:T(8,128)(2,1)S(1)} %broadcast_in_dim.23), channel_id=1, replica_groups=mesh['heads'=32,'width'=8] {'heads'}, dimensions={0} | all-to-all | bytes 4718592 | tf_op jit(solution)/shard_map/all_to_all | solution.py:66
  90.6 1.4 copy-done.1
  92.1 3.3 convolution_convert_fusion
  95.7 0.3 reduce-window.9
  96.1 0.1 slice_reduce_fusion
  96.2 0.1 fusion.53
  96.3 0.1 multiply_cosine_fusion
  96.5 0.1 copy.39
  96.6 0.1 copy.40
  96.7 35.0 %reduce-scatter.3.cloned.1.call-done = bf16[192,576]{1,0:T(8,128)(2,1)} async-done(((bf16[1536,576]{1,0:T(8,128)(2,1)}), bf16[192,576]{1,0:T(8,128)(2,1)}) %reduce-scatter.3.cloned.1.call-update) | async-done | bytes 221200 | tf_op jit(solution)/shard_map/reduce_scatter | solution.py:89
  131.7 1.0 convert_add_fusion.1
  132.7 0.2 copy.37
  133.0 0.1 copy.49
  133.1 0.1 copy.50
  133.3 0.1 slice.90
  133.4 0.2 subtract_convert_fusion.1
  133.6 0.1 pad_maximum_fusion.1
  133.7 0.1 copy.42
  133.9 0.8 copy.43
  134.8 5.1 %fusion.5 = bf16[1536,768]{1,0:T(8,128)(2,1)} fusion(bf16[768,768]{1,0:T(8,128)(2,1)S(1)} %copy-done, bf16[1536,768]{1,0:T(8,128)(2,1)} %bitcast.38, f32[768]{0:T(1024)S(1)} %copy-done.14, f32[768]{0:T(1024)S(1)} %copy-done.15), kind=kOutput, calls=%fused_computation.11 | convolution fusion | flops 1816657920 | bytes 5904384 | tf_op jit(solution)/shard_map/dot_general | solution.py:75
  139.9 31.2 %all-gather.3.cloned.1.call-done = bf16[1536,384]{1,0:T(8,128)(2,1)} async-done(((bf16[192,384]{1,0:T(8,128)(2,1)}), bf16[1536,384]{1,0:T(8,128)(2,1)}) %all-gather.3.cloned.1.call-update) | async-done | bytes 1179664 | tf_op jit(solution)/shard_map/all_gather | solution.py:100
  171.2 43.3 %reduce-scatter.5.cloned.1.call-done = bf16[192,768]{1,0:T(8,128)(2,1)} async-done(((bf16[1536,768]{1,0:T(8,128)(2,1)}), bf16[192,768]{1,0:T(8,128)(2,1)}) %reduce-scatter.5.cloned.1.call-update) | async-done | bytes 294928 | tf_op jit(solution)/shard_map/reduce_scatter | solution.py:104
  214.5 3.0 fusion.31
  217.5 0.1 dynamic_slice.6
  217.6 0.5 fusion.18
  218.1 0.1 slice.91
  218.2 1.7 fusion.56
  219.9 1.1 copy.44
  221.0 0.3 copy.45
  221.2 1.9 fusion.58
  223.1 0.7 fusion.12
  223.9 0.7 fusion.26
  224.5 0.1 copy.46
  224.6 20.9 %all_gather.10 = bf16[1536,192]{1,0:T(8,128)(2,1)S(1)} all-gather(bf16[192,192]{1,0:T(8,128)(2,1)S(1)} %copy.46), channel_id=1, replica_groups=mesh['heads'=32,'width'=8] {'width'}, dimensions={0}, use_global_device_ids=true | all-gather | bytes 663552 | tf_op jit(solution)/shard_map/all_gather | solution.py:137
  245.5 15.3 %all-gather.5.cloned.1.call-done = bf16[1536,768]{1,0:T(8,128)(2,1)} async-done(((bf16[192,768]{1,0:T(8,128)(2,1)}), bf16[1536,768]{1,0:T(8,128)(2,1)}) %all-gather.5.cloned.1.call-update) | async-done | bytes 2359312 | tf_op jit(solution)/shard_map/all_gather | solution.py:143
  260.8 4.0 %fusion.59 = f32[1536,768]{1,0:T(8,128)S(1)} fusion(bf16[1536,768]{1,0:T(8,128)(2,1)} %all-gather.5.cloned.1.call-done, bf16[768,768]{1,0:T(8,128)(2,1)} %param.26), kind=kOutput, calls=%fused_computation.94 | convolution fusion | flops 1811939328 | bytes 8257536 | tf_op jit(solution)/shard_map/dot_general | solution.py:142
  264.8 2.2 add_convert_fusion
  267.1 10.3 %all-to-all-start.1 = ((bf16[32,48,768]{2,1,0:T(8,128)(2,1)}), bf16[32,48,768]{2,1,0:T(8,128)(2,1)S(1)}, u32[]{:S(2)}, u32[]{:S(2)}) async-start(bf16[32,48,768]{2,1,0:T(8,128)(2,1)} %bitcast.32), calls=%async_computation.3 | async-start | bytes 4718592 | tf_op jit(solution)/shard_map/all_to_all | solution.py:150
  277.4 1.6 copy.48
  279.0 1.6 copy.47
  280.7 52.8 %all-to-all-done.1 = bf16[32,48,768]{2,1,0:T(8,128)(2,1)S(1)} async-done(((bf16[32,48,768]{2,1,0:T(8,128)(2,1)}), bf16[32,48,768]{2,1,0:T(8,128)(2,1)S(1)}, u32[]{:S(2)}, u32[]{:S(2)}) %all-to-all-start.1) | async-done | bytes 2359328 | tf_op jit(solution)/shard_map/all_to_all | solution.py:150
  333.4 0.3 convert_reduce_fusion
  333.8 0.5 copy-done.4
  334.3 0.7 fusion.47
  (50 shorter events, 0.7 us)
Async XLA Ops:
  7.2 127.6 %copy-start = (bf16[768,768]{1,0:T(8,128)(2,1)S(1)}, bf16[768,768]{1,0:T(8,128)(2,1)}, u32[]{:S(2)}) copy-start(bf16[768,768]{1,0:T(8,128)(2,1)} %param.24) | copy-start | bytes 3538948
  7.2 124.5 %reduce-scatter.3.cloned.1.call-start = ((), (), s32[]{:S(2)}) async-start(), calls=%async_computation.4 | async-start | bytes 2211840 | tf_op jit(solution)/shard_map/reduce_scatter | solution.py:89
  20.6 71.4 %copy-start.11 = (bf16[768,576]{0,1:T(8,128)(2,1)S(1)}, bf16[768,576]{0,1:T(8,128)(2,1)}, u32[]{:S(2)}) copy-start(bf16[768,576]{0,1:T(8,128)(2,1)} %param.20) | copy-start | bytes 2654212
  20.6 71.4 %copy-start.12 = (f32[768]{0:T(1024)S(1)}, f32[768]{0:T(1024)}, u32[]{:S(2)}) copy-start(f32[768]{0:T(1024)} %param.17) | copy-start | bytes 9220
  20.6 71.4 %copy-start.13 = (f32[768]{0:T(1024)S(1)}, f32[768]{0:T(1024)}, u32[]{:S(2)}) copy-start(f32[768]{0:T(1024)} %param.16) | copy-start | bytes 9220
  90.6 1.4 copy-start.1
  92.0 3.4 %copy-start.6 = (s32[1536]{0:T(1024)S(1)}, s32[1536]{0:T(1024)}, u32[]{:S(2)}) copy-start(s32[1536]{0:T(1024)} %param.15) | copy-start | bytes 18436
  95.4 36.3 %copy-start.7 = (f32[576]{0:T(1024)S(1)}, f32[576]{0:T(1024)}, u32[]{:S(2)}) copy-start(f32[576]{0:T(1024)} %param.21) | copy-start | bytes 6916
  95.4 75.7 %all-gather.3.cloned.1.call-start = ((), (), s32[]{:S(2)}) async-start(), calls=%async_computation.5 | async-start | bytes 1327104 | tf_op jit(solution)/shard_map/all_gather | solution.py:100
  132.9 6.9 %copy-start.2 = (bf16[192,2,1,96]{0,3,2,1:T(8,128)(2,1)}, bf16[192,2,1,96]{0,3,2,1:T(8,128)(2,1)S(1)}, u32[]{:S(2)}) copy-start(bf16[192,2,1,96]{0,3,2,1:T(8,128)(2,1)S(1)} %slice.89) | copy-start | bytes 221188
  132.9 1.8 copy-start.14
  132.9 1.8 copy-start.15
  133.8 6.1 %copy-start.3 = (bf16[192,2,96]{0,2,1:T(8,128)(2,1)}, bf16[192,2,96]{0,2,1:T(8,128)(2,1)S(1)}, u32[]{:S(2)}) copy-start(bf16[192,2,96]{0,2,1:T(8,128)(2,1)S(1)} %copy.42) | copy-start | bytes 221188
  134.7 79.8 %reduce-scatter.5.cloned.1.call-start = ((), (), s32[]{:S(2)}) async-start(), calls=%async_computation.6 | async-start | bytes 2654208 | tf_op jit(solution)/shard_map/reduce_scatter | solution.py:104
  139.9 74.6 %copy-start.8 = (f32[768]{0:T(1024)S(1)}, f32[768]{0:T(1024)}, u32[]{:S(2)}) copy-start(f32[768]{0:T(1024)} %param.25) | copy-start | bytes 9220
  171.1 89.7 %all-gather.5.cloned.1.call-start = ((), (), s32[]{:S(2)}) async-start(), calls=%async_computation.7 | async-start | bytes 2654208 | tf_op jit(solution)/shard_map/all_gather | solution.py:143
  245.5 19.3 %copy-start.5 = (bf16[192,768]{1,0:T(8,128)(2,1)S(1)}, bf16[192,768]{1,0:T(8,128)(2,1)}, u32[]{:S(2)}) copy-start(bf16[192,768]{1,0:T(8,128)(2,1)} %param.22) | copy-start | bytes 884740
  267.1 66.4 %all-to-all-start.1 = ((bf16[32,48,768]{2,1,0:T(8,128)(2,1)}), bf16[32,48,768]{2,1,0:T(8,128)(2,1)S(1)}, u32[]{:S(2)}, u32[]{:S(2)}) async-start(bf16[32,48,768]{2,1,0:T(8,128)(2,1)} %bitcast.32), calls=%async_computation.3 | async-start | bytes 4718592 | tf_op jit(solution)/shard_map/all_to_all | solution.py:150
  277.4 56.4 %copy-start.9 = (f32[768]{0:T(1024)S(1)}, f32[768]{0:T(1024)}, u32[]{:S(2)}) copy-start(f32[768]{0:T(1024)} %param.27) | copy-start | bytes 9220
  277.4 56.4 %copy-start.10 = (f32[768]{0:T(1024)S(1)}, f32[768]{0:T(1024)}, u32[]{:S(2)}) copy-start(f32[768]{0:T(1024)} %param.23) | copy-start | bytes 9220
  333.4 0.9 copy-start.4
Sparse Core Ops, SparseCore 0:
  95.6 36.0 reduce-scatter.2
  134.8 36.2 all-gather.2
  173.7 40.7 reduce-scatter.4
  217.6 43.1 all-gather.4

commit v3 on v0

v3 whole, which is shorter than its diff:
```python
import jax
import jax.numpy as jnp
from jax import lax
from jax.sharding import PartitionSpec as P

HD = 96
ROT = 24
D = 6144


norm_epsilon = 1e-05


def positions_of(segments):
    count = segments.shape[0]
    row_index = jnp.arange(count, dtype=jnp.int32)
    change = jnp.concatenate([jnp.ones((1,), bool), segments[1:] != segments[:-1]])
    first = lax.cummax(jnp.where(change, row_index, 0), axis=0)
    return (row_index - first).astype(jnp.float32)


def rotary(values, positions):
    half_rot = ROT // 2
    inverse = 10000.0 ** (-(jnp.arange(half_rot, dtype=jnp.float32) * 2.0 / ROT))
    angles = positions[:, None] * inverse[None, :]
    cosine = jnp.cos(angles)[:, None, :]
    sine_part = jnp.sin(angles)[:, None, :]
    first_half = values[..., :half_rot]
    second_half = values[..., half_rot:ROT]
    return jnp.concatenate(
        [
            first_half * cosine - second_half * sine_part,
            second_half * cosine + first_half * sine_part,
            values[..., ROT:],
        ],
        axis=-1,
    )


HEADS = ("hz", "hy", "hx")
WIDTH = ("wz", "wc")


def gather_heads(block):
    rows, cols = block.shape
    sizes = [lax.axis_size(a) for a in HEADS]
    for axis, size in zip(HEADS, sizes):
        spread = jnp.broadcast_to(block[None], (size,) + block.shape)
        block = lax.all_to_all(spread, axis, 0, 0, tiled=False).reshape(-1, cols)
    block = block.reshape(sizes[2], sizes[1], sizes[0], rows, cols).transpose(2, 1, 0, 3, 4)
    return block.reshape(-1, cols)


def reduce_heads(partial):
    sizes = [lax.axis_size(a) for a in HEADS]
    cols = partial.shape[1]
    rows = partial.shape[0] // (sizes[0] * sizes[1] * sizes[2])
    part = partial.reshape(sizes + [rows, cols]).transpose(2, 0, 1, 3, 4)
    part = lax.all_to_all(part, "hx", 0, 0, tiled=False)
    total = jnp.sum(part.astype(jnp.float32), 0)
    part = total.astype(jnp.bfloat16).transpose(1, 0, 2, 3)
    part = lax.all_to_all(part, "hy", 0, 0, tiled=False)
    total = jnp.sum(part.astype(jnp.float32), 0)
    part = lax.all_to_all(total.astype(jnp.bfloat16), "hz", 0, 0, tiled=False)
    return jnp.sum(part.astype(jnp.float32), 0)


def on_device(
    states,
    segment_ids,
    attn_gain,
    attn_shift,
    mlp_gain,
    mlp_shift,
    qkv_weight,
    qkv_bias,
    dense_weight,
    dense_bias,
    up_weight,
    up_bias,
    down_weight,
    down_bias,
):
    floats = states.astype(jnp.float32)
    stats = lax.psum(jnp.stack([jnp.sum(floats, -1), jnp.sum(floats * floats, -1)]), WIDTH)
    row_mean = (stats[0] / D)[:, None]
    row_var = (stats[1] / D)[:, None] - row_mean * row_mean
    normed = ((floats - row_mean) * lax.rsqrt(row_var + norm_epsilon)).astype(jnp.bfloat16)
    qkv_cols = qkv_weight.shape[1]
    heads_dev = qkv_cols // (3 * HD)
    block_f = gather_heads(normed).astype(jnp.float32)
    attn_in = (block_f * attn_gain + attn_shift).astype(jnp.bfloat16)
    mlp_in = (block_f * mlp_gain + mlp_shift).astype(jnp.bfloat16)
    projected = jnp.concatenate(
        [
            jnp.dot(attn_in, qkv_weight, preferred_element_type=jnp.float32),
            jnp.dot(mlp_in, up_weight, preferred_element_type=jnp.float32),
        ],
        axis=1,
    )
    summed_proj = lax.psum(projected.astype(jnp.bfloat16), WIDTH).astype(jnp.float32)
    all_tokens = projected.shape[0]
    own_rows = all_tokens // lax.axis_size(WIDTH)
    row_zero = lax.axis_index(WIDTH) * own_rows
    positions = positions_of(segment_ids)
    own_segments = lax.dynamic_slice_in_dim(segment_ids, row_zero, own_rows)
    own_index = row_zero + jnp.arange(own_rows, dtype=jnp.int32)
    score_scale = 1.0 / HD**0.5
    own_positions = lax.dynamic_slice_in_dim(positions, row_zero, own_rows)
    shaped = (summed_proj[:, :qkv_cols] + qkv_bias).reshape(all_tokens, heads_dev, 3, HD)
    own_shaped = lax.dynamic_slice_in_dim(shaped, row_zero, own_rows)
    queries = rotary(own_shaped[:, :, 0, :], own_positions).astype(jnp.bfloat16)
    key_heads = rotary(shaped[:, :, 1, :], positions).astype(jnp.bfloat16)
    value_heads = shaped[:, :, 2, :].astype(jnp.bfloat16)
    width_cols = heads_dev * HD
    key_cache = lax.dynamic_slice_in_dim(key_heads, row_zero, own_rows).reshape(-1, width_cols)
    value_cache = lax.dynamic_slice_in_dim(value_heads, row_zero, own_rows).reshape(-1, width_cols)
    run_max = jnp.full((heads_dev, own_rows), -1e30, jnp.float32)
    count = all_tokens
    scores = (
        jnp.einsum("rhd,nhd->hrn", queries, key_heads, preferred_element_type=jnp.float32)
        * score_scale
    )
    key_index = jnp.arange(count, dtype=jnp.int32)
    allowed = (own_segments[:, None] == segment_ids[None, :]) & (
        key_index[None, :] <= own_index[:, None]
    )
    scores = jnp.where(allowed[None], scores, -1e30)
    new_max = jnp.maximum(run_max, jnp.max(scores, -1))
    weights = jnp.where(allowed[None], jnp.exp(scores - new_max[..., None]), 0.0)
    new_sum = jnp.sum(weights, -1)
    mixed = jnp.einsum(
        "hrn,nhd->hrd",
        weights.astype(jnp.bfloat16),
        value_heads,
        preferred_element_type=jnp.float32,
    )
    attended = (
        (mixed / new_sum[..., None])
        .transpose(1, 0, 2)
        .reshape(own_rows, heads_dev * HD)
        .astype(jnp.bfloat16)
    )
    attn_part = jnp.dot(
        lax.all_gather(attended, WIDTH, axis=0, tiled=True),
        dense_weight,
        preferred_element_type=jnp.float32,
    )
    hidden = jax.nn.gelu(summed_proj[:, qkv_cols:] + up_bias, approximate=False).astype(
        jnp.bfloat16
    )
    mlp_part = jnp.dot(hidden, down_weight, preferred_element_type=jnp.float32)
    summed = reduce_heads((attn_part + mlp_part).astype(jnp.bfloat16))
    layer_out = (floats + summed + dense_bias + down_bias).astype(jnp.bfloat16)
    return (layer_out, key_cache, value_cache)


def solution(mesh):
    devices = mesh.devices.reshape(2, 4, 4, 4, 2)
    fine = jax.sharding.Mesh(devices, HEADS + WIDTH)
    in_specs = (
        P(HEADS, WIDTH),
        P(),
        P(WIDTH),
        P(WIDTH),
        P(WIDTH),
        P(WIDTH),
        P(WIDTH, HEADS),
        P(HEADS),
        P(HEADS, WIDTH),
        P(WIDTH),
        P(WIDTH, HEADS),
        P(HEADS),
        P(HEADS, WIDTH),
        P(WIDTH),
    )
    out_specs = (P(HEADS, WIDTH), P(WIDTH, HEADS), P(WIDTH, HEADS))
    return jax.shard_map(
        on_device, mesh=fine, in_specs=in_specs, out_specs=out_specs, check_vma=False
    )
```

time: 826 us -> 311 us (0.38)
  waiting for transfers between devices: 704 us -> 113 us
  blocking collectives: 65.1 us -> 124 us
  starting transfers between devices: 0.25 us -> 9.42 us
    reduce_scatter x4 -> x0, waiting for transfers between devices: 608 us -> none  [the longest x1 260 us: on_device(): lax.psum_scatter(mlp_part.astype(jnp.bfloat16), 'heads', scatter_dimensio...]
    psum x0 -> x1, waiting for transfers between devices: none -> 98.9 us  [on_device(): lax.psum(projected.astype(jnp.bfloat16), WIDTH).astype(jnp.float32)]
    all_to_all x0 -> x4, blocking collectives: none -> 97.1 us  [the longest x3 63.3 us: gather_heads(): block = lax.all_to_all(spread, axis, 0, 0, tiled=False).reshape(-1, cols)]
    all_gather x2 -> x0, waiting for transfers between devices: 96.7 us -> none  [the longest x1 96.7 us: on_device(): lax.all_gather(normed, 'heads', axis=0, tiled=True).astype(jnp.float32)]
    all_gather x3 -> x1, blocking collectives: 54 us -> 15.8 us  [on_device(): lax.all_gather(attended, WIDTH, axis=0, tiled=True)]
    all_to_all x0 -> x2, waiting for transfers between devices: none -> 14.5 us  [the longest x1 7.8 us: reduce_heads(): part = lax.all_to_all(part, 'hy', 0, 0, tiled=False)]
    all_to_all x0 -> x2, starting transfers between devices: none -> 9.38 us  [the longest x1 5.1 us: reduce_heads(): part = lax.all_to_all(total.astype(jnp.bfloat16), 'hz', 0, 0, tiled=False)]
  transfers between devices with their start and end apart: 6 -> 3, of which waited for: 5 -> 3; matrix products, arithmetic and copies ran while one was open for 3% -> 2% of each run, Pallas kernels for 0% -> 0%
where the time goes in v3:
time: 311 us; the launch traced here: 309 us
  blocking collectives  124 us (40%)
  waiting for transfers between devices  113 us (36%)
  matrix products  21 us (7%)
  other arithmetic  14.8 us (5%)
  between operations  14.5 us (5%)
  local copies, waits for them, and re-layouts  11.7 us (4%)
  starting transfers between devices  9.42 us (3%)
    psum x1, waiting for transfers between devices, on_device(): lax.psum(projected.astype(jnp.bfloat16), WIDTH).astype(jnp.float32)  98.9 us
    all_to_all x3, blocking collectives, gather_heads(): block = lax.all_to_all(spread, axis, 0, 0, tiled=False).reshape(-1, cols)  63.3 us
    all_to_all x1, blocking collectives, reduce_heads(): part = lax.all_to_all(part, 'hx', 0, 0, tiled=False)  33.8 us
    all_gather x1, blocking collectives, on_device(): lax.all_gather(attended, WIDTH, axis=0, tiled=True)  15.8 us
    dot_general x1, matrix products, on_device(): mlp_part = jnp.dot(hidden, down_weight, preferred_element_type=jnp.float32)  13.7 us
    psum x1, blocking collectives, on_device(): lax.psum(jnp.stack([jnp.sum(floats, -1), jnp.sum(floats * floats, -1)]),...  11.1 us
    all_to_all x1, waiting for transfers between devices, reduce_heads(): part = lax.all_to_all(part, 'hy', 0, 0, tiled=False)  7.8 us
    all_to_all x1, waiting for transfers between devices, reduce_heads(): part = lax.all_to_all(total.astype(jnp.bfloat16), 'hz', 0, 0, tiled=False)  6.66 us
  transfers between devices with their start and end apart: 3, of which 3 were waited for; matrix products, arithmetic and copies ran while one was open for 2% of the time, Pallas kernels for 0%

profile of v3, /device:TPU:96, one launch (start us, length us, event | category | flops | bytes accessed | tf_op | source)
XLA Modules:
  0.0 308.7 jit_solution(4177761642653803791)
XLA Ops:
  7.2 1.1 convert_reduce_fusion.1
  8.3 11.1 %psum.14 = f32[2,48]{1,0:T(2,128)S(1)} all-reduce(f32[2,48]{1,0:T(2,128)S(1)} %pad_maximum_fusion.2), channel_id=1, replica_groups=mesh['hz'=2,'hy'=4,'hx'=4,'wz'=4,'wc'=2] {'wz','wc'}, use_global_device_ids=true, to_apply=%region_2.0 | all-reduce | flops 96 | bytes 768 | tf_op jit(solution)/shard_map/psum | solution.py:85
  19.5 1.0 fusion.37
  20.5 14.2 %all_to_all.30 = bf16[2,48,768]{2,1,0:T(8,128)(2,1)S(1)} all-to-all(bf16[2,48,768]{2,1,0:T(8,128)(2,1)S(1)} %broadcast_in_dim.31), channel_id=1, replica_groups=mesh['hz'=2,'hy'=4,'hx'=4,'wz'=4,'wc'=2] {'hz'}, dimensions={0} | all-to-all | bytes 294912 | tf_op jit(solution)/shard_map/all_to_all | solution.py:49
  34.7 15.7 %all_to_all.31 = bf16[4,96,768]{2,1,0:T(8,128)(2,1)S(1)} all-to-all(bf16[4,96,768]{2,1,0:T(8,128)(2,1)S(1)} %broadcast_in_dim.33), channel_id=1, replica_groups=mesh['hz'=2,'hy'=4,'hx'=4,'wz'=4,'wc'=2] {'hy'}, dimensions={0} | all-to-all | bytes 1179648 | tf_op jit(solution)/shard_map/all_to_all | solution.py:49
  50.4 0.2 broadcast_in_dim.35
  50.6 33.4 %all_to_all.32 = bf16[4,384,768]{2,1,0:T(8,128)(2,1)S(1)} all-to-all(bf16[4,384,768]{2,1,0:T(8,128)(2,1)S(1)} %broadcast_in_dim.35), channel_id=1, replica_groups=mesh['hz'=2,'hy'=4,'hx'=4,'wz'=4,'wc'=2] {'hx'}, dimensions={0} | all-to-all | bytes 4718592 | tf_op jit(solution)/shard_map/all_to_all | solution.py:49
  84.0 0.6 convert_bitcast_fusion
  84.6 0.4 copy.57
  85.0 0.2 copy-done.8
  85.3 1.1 fusion.4
  86.4 2.1 convolution_convert_fusion
  88.5 1.6 convolution_convert_fusion.1
  90.1 2.2 pad_maximum_fusion
  92.5 0.3 reduce-window.9
  92.9 0.1 slice_reduce_fusion
  93.2 0.1 multiply_cosine_fusion.1
  93.4 0.1 copy.60
  93.5 0.1 copy.59
  93.6 0.4 multiply_cosine_fusion
  94.0 0.5 fusion.23
  94.5 98.9 %all-reduce.2.cloned.1.call-done = bf16[1536,1344]{0,1:T(8,128)(2,1)} async-done(((bf16[1536,1344]{0,1:T(8,128)(2,1)}), bf16[1536,1344]{0,1:T(8,128)(2,1)}) %all-reduce.2.cloned.1.call-update) | async-done | bytes 4128784 | tf_op jit(solution)/shard_map/psum | solution.py:101
  193.4 3.3 %convert_element_type.74 = f32[1536,1344]{0,1:T(8,128)S(1)} convert(bf16[1536,1344]{0,1:T(8,128)(2,1)} %all-reduce.2.cloned.1.call-done) | non-fusion elementwise | flops 2064384 | bytes 12386304 | tf_op jit(solution)/shard_map/convert_element_type | solution.py:101
  196.7 0.3 slice_add_fusion.1
  197.1 2.8 copy-done.2
  200.0 1.1 copy-done.3
  201.2 0.1 copy.69
  201.5 0.1 subtract_convert_fusion.1
  201.7 0.8 fusion.81
  202.5 0.7 fusion.17
  203.3 2.0 fusion.31
  205.3 15.8 %all_gather.3 = bf16[1536,192]{1,0:T(8,128)(2,1)S(1)} all-gather(bf16[192,192]{1,0:T(8,128)(2,1)S(1)} %copy.63), channel_id=1, replica_groups=mesh['hz'=2,'hy'=4,'hx'=4,'wz'=4,'wc'=2] {'wz','wc'}, dimensions={0}, use_global_device_ids=true | all-gather | bytes 663552 | tf_op jit(solution)/shard_map/all_gather | solution.py:145
  221.1 13.7 %fusion.15 = f32[1536,768]{1,0:T(8,128)S(1)} fusion(bf16[768,768]{1,0:T(8,128)(2,1)S(1)} %copy-done.15, f32[1536,1344]{0,1:T(8,128)} %copy-done.2, f32[768]{0:T(1024)S(1)} %copy-done.17), kind=kOutput, calls=%fused_computation.36 | convolution fusion | flops 1889796096 | bytes 10619904 | tf_op jit(solution)/shard_map/dot_general | solution.py:152
  234.9 0.8 add_convert_fusion
  235.7 0.2 copy.82
  235.9 33.8 %all_to_all.33 = bf16[4,2,4,48,768]{4,3,2,1,0:T(8,128)(2,1)S(1)} all-to-all(bf16[4,2,4,48,768]{4,3,2,1,0:T(8,128)(2,1)S(1)} %bitcast.68), channel_id=1, replica_groups=mesh['hz'=2,'hy'=4,'hx'=4,'wz'=4,'wc'=2] {'hx'}, dimensions={0} | all-to-all | bytes 4718592 | tf_op jit(solution)/shard_map/all_to_all | solution.py:59
  269.8 1.3 reduce_sum.63
  271.1 1.9 copy.65
  273.0 4.3 %all-to-all-start.4 = ((bf16[4,2,48,768]{3,2,1,0:T(8,128)(2,1)}), bf16[4,2,48,768]{3,2,1,0:T(8,128)(2,1)S(1)}, u32[]{:S(2)}, u32[]{:S(2)}) async-start(bf16[4,2,48,768]{3,2,1,0:T(8,128)(2,1)} %copy.65), calls=%async_computation.4 | async-start | bytes 1179648 | tf_op jit(solution)/shard_map/all_to_all | solution.py:62
  277.3 1.0 constant_dynamic-slice_fusion.1
  278.3 0.7 copy.66
  279.1 7.8 %all-to-all-done.4 = bf16[4,2,48,768]{3,2,1,0:T(8,128)(2,1)S(1)} async-done(((bf16[4,2,48,768]{3,2,1,0:T(8,128)(2,1)}), bf16[4,2,48,768]{3,2,1,0:T(8,128)(2,1)S(1)}, u32[]{:S(2)}, u32[]{:S(2)}) %all-to-all-start.4) | async-done | bytes 589856 | tf_op jit(solution)/shard_map/all_to_all | solution.py:62
  286.9 0.8 reduce_sum.64
  287.6 5.1 %all-to-all-start.5 = ((bf16[2,48,768]{2,1,0:T(8,128)(2,1)}), bf16[2,48,768]{2,1,0:T(8,128)(2,1)S(1)}, u32[]{:S(2)}, u32[]{:S(2)}) async-start(bf16[2,48,768]{2,1,0:T(8,128)(2,1)} %reduce_sum.64), calls=%async_computation.5 | async-start | bytes 294912 | tf_op jit(solution)/shard_map/all_to_all | solution.py:64
  292.7 1.1 constant_dynamic-slice_fusion
  293.8 0.7 copy.67
  294.5 6.7 %all-to-all-done.5 = bf16[2,48,768]{2,1,0:T(8,128)(2,1)S(1)} async-done(((bf16[2,48,768]{2,1,0:T(8,128)(2,1)}), bf16[2,48,768]{2,1,0:T(8,128)(2,1)S(1)}, u32[]{:S(2)}, u32[]{:S(2)}) %all-to-all-start.5) | async-done | bytes 147488 | tf_op jit(solution)/shard_map/all_to_all | solution.py:64
  301.2 0.7 fusion.40
  (58 shorter events, 1.3 us)
Async XLA Ops:
  7.2 79.2 %copy-start = (bf16[768,768]{1,0:T(8,128)(2,1)S(1)}, bf16[768,768]{1,0:T(8,128)(2,1)}, u32[]{:S(2)}) copy-start(bf16[768,768]{1,0:T(8,128)(2,1)} %param.24) | copy-start | bytes 3538948
  7.2 186.2 %all-reduce.2.cloned.1.call-start = ((), (), s32[]{:S(2)}) async-start(), calls=%async_computation.6 | async-start | bytes 8257536 | tf_op jit(solution)/shard_map/psum | solution.py:101
  84.5 0.7 copy-start.8
  84.5 0.7 copy-start.9
  84.6 0.7 copy-start.10
  84.6 0.7 copy-start.11
  86.3 2.1 copy-start.16
  90.0 2.2 copy-start.7
  94.5 102.2 %copy-start.12 = (f32[576]{0:T(1024)S(1)}, f32[576]{0:T(1024)}, u32[]{:S(2)}) copy-start(f32[576]{0:T(1024)} %param.21) | copy-start | bytes 6916
  196.7 3.2 %copy-start.2 = (f32[1536,1344]{0,1:T(8,128)}, f32[1536,1344]{0,1:T(8,128)S(1)}, u32[]{:S(2)}) copy-start(f32[1536,1344]{0,1:T(8,128)S(1)} %convert_element_type.74) | copy-start | bytes 24772612
  197.0 4.1 %copy-start.3 = (f32[1536,576]{0,1:T(8,128)}, f32[1536,576]{0,1:T(8,128)S(1)}, u32[]{:S(2)}) copy-start(f32[1536,576]{0,1:T(8,128)S(1)} %slice_add_fusion.1) | copy-start | bytes 10616836
  201.7 3.5 %copy-start.4 = (bf16[1536,2,96]{0,2,1:T(8,128)(2,1)}, bf16[1536,2,96]{0,2,1:T(8,128)(2,1)S(1)}, u32[]{:S(2)}) copy-start(bf16[1536,2,96]{0,2,1:T(8,128)(2,1)S(1)} %pad_maximum_fusion.1) | copy-start | bytes 1769476
  202.5 18.6 %copy-start.15 = (bf16[768,768]{1,0:T(8,128)(2,1)S(1)}, bf16[768,768]{1,0:T(8,128)(2,1)}, u32[]{:S(2)}) copy-start(bf16[768,768]{1,0:T(8,128)(2,1)} %param.26) | copy-start | bytes 3538948
  202.5 18.6 %copy-start.17 = (f32[768]{0:T(1024)S(1)}, f32[768]{0:T(1024)}, u32[]{:S(2)}) copy-start(f32[768]{0:T(1024)} %param.25) | copy-start | bytes 9220
  221.1 13.8 %copy-start.6 = (bf16[192,768]{1,0:T(8,128)(2,1)S(1)}, bf16[192,768]{1,0:T(8,128)(2,1)}, u32[]{:S(2)}) copy-start(bf16[192,768]{1,0:T(8,128)(2,1)} %param.22) | copy-start | bytes 884740
  235.9 66.0 %copy-start.1 = (bf16[768,768]{1,0:T(8,128)(2,1)S(1)}, bf16[768,768]{1,0:T(8,128)(2,1)}, u32[]{:S(2)}) copy-start(bf16[768,768]{1,0:T(8,128)(2,1)} %param.24) | copy-start | bytes 3538948
  269.8 31.5 %copy-start.13 = (f32[768]{0:T(1024)S(1)}, f32[768]{0:T(1024)}, u32[]{:S(2)}) copy-start(f32[768]{0:T(1024)} %param.27) | copy-start | bytes 9220
  269.8 31.5 %copy-start.14 = (f32[768]{0:T(1024)S(1)}, f32[768]{0:T(1024)}, u32[]{:S(2)}) copy-start(f32[768]{0:T(1024)} %param.23) | copy-start | bytes 9220
  271.1 30.2 %copy-start.5 = (bf16[48,768]{1,0:T(8,128)(2,1)S(1)}, bf16[48,768]{1,0:T(8,128)(2,1)}, u32[]{:S(2)}) copy-start(bf16[48,768]{1,0:T(8,128)(2,1)} %param.14) | copy-start | bytes 221188
  273.0 13.8 %all-to-all-start.4 = ((bf16[4,2,48,768]{3,2,1,0:T(8,128)(2,1)}), bf16[4,2,48,768]{3,2,1,0:T(8,128)(2,1)S(1)}, u32[]{:S(2)}, u32[]{:S(2)}) async-start(bf16[4,2,48,768]{3,2,1,0:T(8,128)(2,1)} %copy.65), calls=%async_computation.4 | async-start | bytes 1179648 | tf_op jit(solution)/shard_map/all_to_all | solution.py:62
  287.6 13.6 %all-to-all-start.5 = ((bf16[2,48,768]{2,1,0:T(8,128)(2,1)}), bf16[2,48,768]{2,1,0:T(8,128)(2,1)S(1)}, u32[]{:S(2)}, u32[]{:S(2)}) async-start(bf16[2,48,768]{2,1,0:T(8,128)(2,1)} %reduce_sum.64), calls=%async_computation.5 | async-start | bytes 294912 | tf_op jit(solution)/shard_map/all_to_all | solution.py:64
Sparse Core Ops, SparseCore 0:
  92.4 100.9 all-reduce.1

commit v4 on v3

--- a/solution.py
+++ b/solution.py
@@ -149,6 +149,7 @@
     hidden = jax.nn.gelu(summed_proj[:, qkv_cols:] + up_bias, approximate=False).astype(
         jnp.bfloat16
     )
+    hidden = lax.optimization_barrier(hidden)
     mlp_part = jnp.dot(hidden, down_weight, preferred_element_type=jnp.float32)
     summed = reduce_heads((attn_part + mlp_part).astype(jnp.bfloat16))
     layer_out = (floats + summed + dense_bias + down_bias).astype(jnp.bfloat16)

time: 311 us -> 310 us (level)
  blocking collectives: 124 us -> 138 us
  other arithmetic: 14.8 us -> 26.6 us
  matrix products: 21 us -> 10.6 us
  waiting for transfers between devices: 113 us -> 104 us
  starting transfers between devices: 9.42 us -> 5.15 us
    all_to_all x0 -> x1, blocking collectives: none -> 13.6 us  [reduce_heads(): part = lax.all_to_all(part, 'hy', 0, 0, tiled=False)]
    convert_element_type x0 -> x1, other arithmetic: none -> 11.7 us  [on_device(): jax.nn.gelu(summed_proj[:, qkv_cols:] + up_bias, approximate=False)]
    dot_general x1, matrix products: 13.7 us -> 3.4 us  [on_device(): mlp_part = jnp.dot(hidden, down_weight, preferred_element_type=jnp.float32)]
    all_to_all x1 -> x0, waiting for transfers between devices: 7.8 us -> none  [reduce_heads(): part = lax.all_to_all(part, 'hy', 0, 0, tiled=False)]
    all_to_all x1 -> x0, starting transfers between devices: 4.28 us -> none  [reduce_heads(): part = lax.all_to_all(part, 'hy', 0, 0, tiled=False)]
  transfers between devices with their start and end apart: 3 -> 2, of which waited for: 3 -> 2; matrix products, arithmetic and copies ran while one was open for 2% -> 2% of each run, Pallas kernels for 0% -> 0%
where the time goes in v4:
time: 310 us; the launch traced here: 307 us
  blocking collectives  138 us (45%)
  waiting for transfers between devices  104 us (34%)
  other arithmetic  26.6 us (9%)
  between operations  14.4 us (5%)
  matrix products  10.6 us (3%)
  local copies, waits for them, and re-layouts  8.72 us (3%)
  starting transfers between devices  5.15 us (2%)
    psum x1, waiting for transfers between devices, on_device(): lax.psum(projected.astype(jnp.bfloat16), WIDTH).astype(jnp.float32)  98.9 us
    all_to_all x3, blocking collectives, gather_heads(): block = lax.all_to_all(spread, axis, 0, 0, tiled=False).reshape(-1, cols)  63.3 us
    all_to_all x1, blocking collectives, reduce_heads(): part = lax.all_to_all(part, 'hx', 0, 0, tiled=False)  33.8 us
    all_gather x1, blocking collectives, on_device(): lax.all_gather(attended, WIDTH, axis=0, tiled=True)  15.8 us
    all_to_all x1, blocking collectives, reduce_heads(): part = lax.all_to_all(part, 'hy', 0, 0, tiled=False)  13.6 us
    convert_element_type x1, other arithmetic, on_device(): jax.nn.gelu(summed_proj[:, qkv_cols:] + up_bias, approximate=False)  11.7 us
    psum x1, blocking collectives, on_device(): lax.psum(jnp.stack([jnp.sum(floats, -1), jnp.sum(floats * floats, -1)]),...  11.1 us
  transfers between devices with their start and end apart: 2, of which 2 were waited for; matrix products, arithmetic and copies ran while one was open for 2% of the time, Pallas kernels for 0%

profile of v4, /device:TPU:96, one launch (start us, length us, event | category | flops | bytes accessed | tf_op | source)
XLA Modules:
  0.0 307.0 jit_solution(16440178622481553993)
XLA Ops:
  7.2 1.1 convert_reduce_fusion.1
  8.3 11.1 %psum.14 = f32[2,48]{1,0:T(2,128)S(1)} all-reduce(f32[2,48]{1,0:T(2,128)S(1)} %pad_maximum_fusion.2), channel_id=1, replica_groups=mesh['hz'=2,'hy'=4,'hx'=4,'wz'=4,'wc'=2] {'wz','wc'}, use_global_device_ids=true, to_apply=%region_2.0 | all-reduce | flops 96 | bytes 768 | tf_op jit(solution)/shard_map/psum | solution.py:85
  19.5 1.0 fusion.35
  20.5 14.2 %all_to_all.30 = bf16[2,48,768]{2,1,0:T(8,128)(2,1)S(1)} all-to-all(bf16[2,48,768]{2,1,0:T(8,128)(2,1)S(1)} %broadcast_in_dim.31), channel_id=1, replica_groups=mesh['hz'=2,'hy'=4,'hx'=4,'wz'=4,'wc'=2] {'hz'}, dimensions={0} | all-to-all | bytes 294912 | tf_op jit(solution)/shard_map/all_to_all | solution.py:49
  34.7 15.7 %all_to_all.31 = bf16[4,96,768]{2,1,0:T(8,128)(2,1)S(1)} all-to-all(bf16[4,96,768]{2,1,0:T(8,128)(2,1)S(1)} %broadcast_in_dim.33), channel_id=1, replica_groups=mesh['hz'=2,'hy'=4,'hx'=4,'wz'=4,'wc'=2] {'hy'}, dimensions={0} | all-to-all | bytes 1179648 | tf_op jit(solution)/shard_map/all_to_all | solution.py:49
  50.4 0.2 broadcast_in_dim.35
  50.6 33.4 %all_to_all.32 = bf16[4,384,768]{2,1,0:T(8,128)(2,1)S(1)} all-to-all(bf16[4,384,768]{2,1,0:T(8,128)(2,1)S(1)} %broadcast_in_dim.35), channel_id=1, replica_groups=mesh['hz'=2,'hy'=4,'hx'=4,'wz'=4,'wc'=2] {'hx'}, dimensions={0} | all-to-all | bytes 4718592 | tf_op jit(solution)/shard_map/all_to_all | solution.py:49
  84.0 0.6 convert_bitcast_fusion
  84.6 0.4 copy.57
  85.0 0.2 copy-done.8
  85.3 1.1 fusion.4
  86.4 1.6 convolution_convert_fusion.1
  88.0 2.1 convolution_convert_fusion
  90.1 2.2 pad_maximum_fusion
  92.6 0.3 reduce-window.9
  93.0 0.1 slice_reduce_fusion
  93.3 0.2 multiply_cosine_fusion.1
  93.5 0.1 copy.59
  93.6 0.1 copy.60
  93.7 0.4 multiply_cosine_fusion
  94.1 0.5 fusion.21
  94.6 98.9 %all-reduce.2.cloned.1.call-done = bf16[1536,1344]{0,1:T(8,128)(2,1)} async-done(((bf16[1536,1344]{0,1:T(8,128)(2,1)}), bf16[1536,1344]{0,1:T(8,128)(2,1)}) %all-reduce.2.cloned.1.call-update) | async-done | bytes 4128784 | tf_op jit(solution)/shard_map/psum | solution.py:101
  193.5 3.3 %convert_element_type.74 = f32[1536,1344]{0,1:T(8,128)S(1)} convert(bf16[1536,1344]{0,1:T(8,128)(2,1)} %all-reduce.2.cloned.1.call-done) | non-fusion elementwise | flops 2064384 | bytes 12386304 | tf_op jit(solution)/shard_map/convert_element_type | solution.py:101
  196.8 0.3 slice_add_fusion.1
  197.1 0.1 constant_dynamic-slice_fusion.2
  197.3 1.6 copy-done.2
  199.0 11.7 %fusion.2 = bf16[1536,768]{0,1:T(8,128)(2,1)} fusion(f32[1536,1344]{0,1:T(8,128)S(1)} %convert_element_type.74, f32[768]{0:T(1024)S(1)} %copy-done.13), kind=kLoop, calls=%fused_computation.3 | loop fusion | flops 77856768 | bytes 7080960 | tf_op jit(solution)/shard_map/convert_element_type | solution.py:149
  210.7 0.1 copy.69
  211.0 0.1 subtract_convert_fusion.1
  211.3 0.8 fusion.49
  212.1 0.7 fusion.15
  212.8 2.0 fusion.29
  214.9 15.8 %all_gather.3 = bf16[1536,192]{1,0:T(8,128)(2,1)S(1)} all-gather(bf16[192,192]{1,0:T(8,128)(2,1)S(1)} %copy.63), channel_id=1, replica_groups=mesh['hz'=2,'hy'=4,'hx'=4,'wz'=4,'wc'=2] {'wz','wc'}, dimensions={0}, use_global_device_ids=true | all-gather | bytes 663552 | tf_op jit(solution)/shard_map/all_gather | solution.py:145
  230.7 3.4 %fusion.51 = f32[1536,768]{1,0:T(8,128)S(1)} fusion(bf16[1536,768]{0,1:T(8,128)(2,1)S(1)} %copy-done.4, bf16[768,768]{1,0:T(8,128)(2,1)} %param.26), kind=kOutput, calls=%fused_computation.98 | convolution fusion | flops 1811939328 | bytes 8257536 | tf_op jit(solution)/shard_map/dot_general | solution.py:153
  234.1 0.8 add_convert_fusion
  234.9 0.2 copy.82
  235.2 33.8 %all_to_all.33 = bf16[4,2,4,48,768]{4,3,2,1,0:T(8,128)(2,1)S(1)} all-to-all(bf16[4,2,4,48,768]{4,3,2,1,0:T(8,128)(2,1)S(1)} %bitcast.69), channel_id=1, replica_groups=mesh['hz'=2,'hy'=4,'hx'=4,'wz'=4,'wc'=2] {'hx'}, dimensions={0} | all-to-all | bytes 4718592 | tf_op jit(solution)/shard_map/all_to_all | solution.py:59
  269.0 1.3 reduce_sum.63
  270.3 1.1 copy.65
  271.4 13.6 %all_to_all.34 = bf16[4,2,48,768]{3,2,1,0:T(8,128)(2,1)S(1)} all-to-all(bf16[4,2,48,768]{3,2,1,0:T(8,128)(2,1)S(1)} %copy.65), channel_id=1, replica_groups=mesh['hz'=2,'hy'=4,'hx'=4,'wz'=4,'wc'=2] {'hy'}, dimensions={0} | all-to-all | bytes 1179648 | tf_op jit(solution)/shard_map/all_to_all | solution.py:62
  285.1 0.8 reduce_sum.64
  285.8 5.1 %all-to-all-start.5 = ((bf16[2,48,768]{2,1,0:T(8,128)(2,1)}), bf16[2,48,768]{2,1,0:T(8,128)(2,1)S(1)}, u32[]{:S(2)}, u32[]{:S(2)}) async-start(bf16[2,48,768]{2,1,0:T(8,128)(2,1)} %reduce_sum.64), calls=%async_computation.5 | async-start | bytes 294912 | tf_op jit(solution)/shard_map/all_to_all | solution.py:64
  290.9 1.1 constant_dynamic-slice_fusion
  292.0 0.7 copy.67
  292.8 1.0 constant_dynamic-slice_fusion.1
  293.8 0.7 copy.66
  294.5 4.9 %all-to-all-done.5 = bf16[2,48,768]{2,1,0:T(8,128)(2,1)S(1)} async-done(((bf16[2,48,768]{2,1,0:T(8,128)(2,1)}), bf16[2,48,768]{2,1,0:T(8,128)(2,1)S(1)}, u32[]{:S(2)}, u32[]{:S(2)}) %all-to-all-start.5) | async-done | bytes 147488 | tf_op jit(solution)/shard_map/all_to_all | solution.py:64
  299.5 0.7 fusion.38
  (56 shorter events, 1.3 us)
Async XLA Ops:
  7.2 80.9 %copy-start = (bf16[768,768]{1,0:T(8,128)(2,1)S(1)}, bf16[768,768]{1,0:T(8,128)(2,1)}, u32[]{:S(2)}) copy-start(bf16[768,768]{1,0:T(8,128)(2,1)} %param.24) | copy-start | bytes 3538948
  7.2 186.3 %all-reduce.2.cloned.1.call-start = ((), (), s32[]{:S(2)}) async-start(), calls=%async_computation.6 | async-start | bytes 8257536 | tf_op jit(solution)/shard_map/psum | solution.py:101
  84.5 0.7 copy-start.8
  84.5 0.7 copy-start.9
  84.6 0.7 copy-start.10
  84.6 0.7 copy-start.11
  85.3 1.2 copy-start.16
  90.1 2.2 copy-start.7
  94.6 102.2 %copy-start.12 = (f32[576]{0:T(1024)S(1)}, f32[576]{0:T(1024)}, u32[]{:S(2)}) copy-start(f32[576]{0:T(1024)} %param.21) | copy-start | bytes 6916
  196.8 2.2 copy-start.13
  197.1 1.8 copy-start.2
  211.3 3.5 %copy-start.3 = (bf16[1536,2,96]{0,2,1:T(8,128)(2,1)}, bf16[1536,2,96]{0,2,1:T(8,128)(2,1)S(1)}, u32[]{:S(2)}) copy-start(bf16[1536,2,96]{0,2,1:T(8,128)(2,1)S(1)} %pad_maximum_fusion.1) | copy-start | bytes 1769476
  212.1 18.6 %copy-start.4 = (bf16[1536,768]{0,1:T(8,128)(2,1)S(1)}, bf16[1536,768]{0,1:T(8,128)(2,1)}, u32[]{:S(2)}) copy-start(bf16[1536,768]{0,1:T(8,128)(2,1)} %fusion.2) | copy-start | bytes 7077892
  230.7 3.4 %copy-start.6 = (bf16[192,768]{1,0:T(8,128)(2,1)S(1)}, bf16[192,768]{1,0:T(8,128)(2,1)}, u32[]{:S(2)}) copy-start(bf16[192,768]{1,0:T(8,128)(2,1)} %param.22) | copy-start | bytes 884740
  235.1 65.0 %copy-start.1 = (bf16[768,768]{1,0:T(8,128)(2,1)S(1)}, bf16[768,768]{1,0:T(8,128)(2,1)}, u32[]{:S(2)}) copy-start(bf16[768,768]{1,0:T(8,128)(2,1)} %param.24) | copy-start | bytes 3538948
  269.0 30.5 %copy-start.14 = (f32[768]{0:T(1024)S(1)}, f32[768]{0:T(1024)}, u32[]{:S(2)}) copy-start(f32[768]{0:T(1024)} %param.27) | copy-start | bytes 9220
  269.0 30.5 %copy-start.15 = (f32[768]{0:T(1024)S(1)}, f32[768]{0:T(1024)}, u32[]{:S(2)}) copy-start(f32[768]{0:T(1024)} %param.23) | copy-start | bytes 9220
  270.3 29.2 %copy-start.5 = (bf16[48,768]{1,0:T(8,128)(2,1)S(1)}, bf16[48,768]{1,0:T(8,128)(2,1)}, u32[]{:S(2)}) copy-start(bf16[48,768]{1,0:T(8,128)(2,1)} %param.14) | copy-start | bytes 221188
  285.8 13.6 %all-to-all-start.5 = ((bf16[2,48,768]{2,1,0:T(8,128)(2,1)}), bf16[2,48,768]{2,1,0:T(8,128)(2,1)S(1)}, u32[]{:S(2)}, u32[]{:S(2)}) async-start(bf16[2,48,768]{2,1,0:T(8,128)(2,1)} %reduce_sum.64), calls=%async_computation.5 | async-start | bytes 294912 | tf_op jit(solution)/shard_map/all_to_all | solution.py:64
Sparse Core Ops, SparseCore 0:
  92.5 100.9 all-reduce.1

commit v5 on v4

--- a/solution.py
+++ b/solution.py
@@ -43,23 +43,21 @@
 
 def gather_heads(block):
     rows, cols = block.shape
-    sizes = [lax.axis_size(a) for a in HEADS]
-    for axis, size in zip(HEADS, sizes):
-        spread = jnp.broadcast_to(block[None], (size,) + block.shape)
-        block = lax.all_to_all(spread, axis, 0, 0, tiled=False).reshape(-1, cols)
-    block = block.reshape(sizes[2], sizes[1], sizes[0], rows, cols).transpose(2, 1, 0, 3, 4)
+    nz, ny, nx = [lax.axis_size(a) for a in HEADS]
+    spread = jnp.broadcast_to(block[None], (nz,) + block.shape)
+    block = lax.all_to_all(spread, "hz", 0, 0, tiled=False).reshape(-1, cols)
+    spread = jnp.broadcast_to(block[None], (ny * nx,) + block.shape)
+    block = lax.all_to_all(spread, ("hy", "hx"), 0, 0, tiled=False)
+    block = block.reshape(ny, nx, nz, rows, cols).transpose(2, 0, 1, 3, 4)
     return block.reshape(-1, cols)
 
 
 def reduce_heads(partial):
-    sizes = [lax.axis_size(a) for a in HEADS]
+    nz, ny, nx = [lax.axis_size(a) for a in HEADS]
     cols = partial.shape[1]
-    rows = partial.shape[0] // (sizes[0] * sizes[1] * sizes[2])
-    part = partial.reshape(sizes + [rows, cols]).transpose(2, 0, 1, 3, 4)
-    part = lax.all_to_all(part, "hx", 0, 0, tiled=False)
-    total = jnp.sum(part.astype(jnp.float32), 0)
-    part = total.astype(jnp.bfloat16).transpose(1, 0, 2, 3)
-    part = lax.all_to_all(part, "hy", 0, 0, tiled=False)
+    rows = partial.shape[0] // (nz * ny * nx)
+    part = partial.reshape(nz, ny * nx, rows, cols).transpose(1, 0, 2, 3)
+    part = lax.all_to_all(part, ("hy", "hx"), 0, 0, tiled=False)
     total = jnp.sum(part.astype(jnp.float32), 0)
     part = lax.all_to_all(total.astype(jnp.bfloat16), "hz", 0, 0, tiled=False)
     return jnp.sum(part.astype(jnp.float32), 0)

time: 310 us -> 291 us (0.939)
  blocking collectives: 138 us -> 120 us
    all_to_all x5 -> x3, blocking collectives: 111 us -> 93 us  [the longest x1 40.4 us: gather_heads(): block = lax.all_to_all(spread, ('hy', 'hx'), 0, 0, tiled=False)]
where the time goes in v5:
time: 291 us; the launch traced here: 288 us
  blocking collectives  120 us (41%)
  waiting for transfers between devices  104 us (36%)
  other arithmetic  26.4 us (9%)
  between operations  14.4 us (5%)
  matrix products  10.6 us (4%)
  local copies, waits for them, and re-layouts  7.66 us (3%)
  starting transfers between devices  5.14 us (2%)
    psum x1, waiting for transfers between devices, on_device(): lax.psum(projected.astype(jnp.bfloat16), WIDTH).astype(jnp.float32)  99.1 us
    all_to_all x1, blocking collectives, gather_heads(): block = lax.all_to_all(spread, ('hy', 'hx'), 0, 0, tiled=False)  40.4 us
    all_to_all x1, blocking collectives, reduce_heads(): part = lax.all_to_all(part, ('hy', 'hx'), 0, 0, tiled=False)  38.4 us
    all_gather x1, blocking collectives, on_device(): lax.all_gather(attended, WIDTH, axis=0, tiled=True)  15.8 us
    all_to_all x1, blocking collectives, gather_heads(): block = lax.all_to_all(spread, 'hz', 0, 0, tiled=False).reshape(-1, cols)  14.2 us
    convert_element_type x1, other arithmetic, on_device(): jax.nn.gelu(summed_proj[:, qkv_cols:] + up_bias, approximate=False)  11.7 us
    psum x1, blocking collectives, on_device(): lax.psum(jnp.stack([jnp.sum(floats, -1), jnp.sum(floats * floats, -1)]),...  11.1 us
  transfers between devices with their start and end apart: 2, of which 2 were waited for; matrix products, arithmetic and copies ran while one was open for 2% of the time, Pallas kernels for 0%

profile of v5, /device:TPU:96, one launch (start us, length us, event | category | flops | bytes accessed | tf_op | source)
XLA Modules:
  0.0 288.2 jit_solution(13851987181347984685)
XLA Ops:
  7.2 1.1 convert_reduce_fusion.1
  8.3 11.1 %psum.14 = f32[2,48]{1,0:T(2,128)S(1)} all-reduce(f32[2,48]{1,0:T(2,128)S(1)} %pad_maximum_fusion.2), channel_id=1, replica_groups=mesh['hz'=2,'hy'=4,'hx'=4,'wz'=4,'wc'=2] {'wz','wc'}, use_global_device_ids=true, to_apply=%region_2.0 | all-reduce | flops 96 | bytes 768 | tf_op jit(solution)/shard_map/psum | solution.py:83
  19.5 1.0 fusion.35
  20.5 14.2 %all_to_all.20 = bf16[2,48,768]{2,1,0:T(8,128)(2,1)S(1)} all-to-all(bf16[2,48,768]{2,1,0:T(8,128)(2,1)S(1)} %broadcast_in_dim.27), channel_id=1, replica_groups=mesh['hz'=2,'hy'=4,'hx'=4,'wz'=4,'wc'=2] {'hz'}, dimensions={0} | all-to-all | bytes 294912 | tf_op jit(solution)/shard_map/all_to_all | solution.py:48
  34.7 0.2 broadcast_in_dim.29
  34.9 40.4 %all_to_all.21 = bf16[16,96,768]{2,1,0:T(8,128)(2,1)S(1)} all-to-all(bf16[16,96,768]{2,1,0:T(8,128)(2,1)S(1)} %broadcast_in_dim.29), channel_id=1, replica_groups=mesh['hz'=2,'hy'=4,'hx'=4,'wz'=4,'wc'=2] {'hy','hx'}, dimensions={0} | all-to-all | bytes 4718592 | tf_op jit(solution)/shard_map/all_to_all | solution.py:50
  75.2 0.6 convert_bitcast_fusion
  75.9 0.4 copy.47
  76.3 0.2 copy-done.7
  76.6 1.1 fusion.4
  77.6 0.1 copy-done.15
  77.7 1.6 convolution_convert_fusion.1
  79.3 2.1 convolution_convert_fusion
  81.4 2.2 pad_maximum_fusion
  83.7 0.1 dynamic_slice.15
  83.9 0.3 reduce-window.9
  84.3 0.1 slice_reduce_fusion
  84.6 0.2 multiply_cosine_fusion.1
  84.7 0.1 copy.49
  84.9 0.1 copy.50
  85.0 0.4 multiply_cosine_fusion
  85.4 0.5 fusion.21
  85.9 99.1 %all-reduce.2.cloned.1.call-done = bf16[1536,1344]{0,1:T(8,128)(2,1)} async-done(((bf16[1536,1344]{0,1:T(8,128)(2,1)}), bf16[1536,1344]{0,1:T(8,128)(2,1)}) %all-reduce.2.cloned.1.call-update) | async-done | bytes 4128784 | tf_op jit(solution)/shard_map/psum | solution.py:99
  185.0 3.3 %convert_element_type.72 = f32[1536,1344]{0,1:T(8,128)S(1)} convert(bf16[1536,1344]{0,1:T(8,128)(2,1)} %all-reduce.2.cloned.1.call-done) | non-fusion elementwise | flops 2064384 | bytes 12386304 | tf_op jit(solution)/shard_map/convert_element_type | solution.py:99
  188.4 0.3 slice_add_fusion.1
  188.7 0.1 constant_dynamic-slice_fusion.2
  188.8 1.6 copy-done.2
  190.5 11.7 %fusion.2 = bf16[1536,768]{0,1:T(8,128)(2,1)} fusion(f32[1536,1344]{0,1:T(8,128)S(1)} %convert_element_type.72, f32[768]{0:T(1024)S(1)} %copy-done.12), kind=kLoop, calls=%fused_computation.3 | loop fusion | flops 77856768 | bytes 7080960 | tf_op jit(solution)/shard_map/convert_element_type | solution.py:147
  202.3 0.1 copy.58
  202.4 0.1 slice.106
  202.6 0.1 subtract_convert_fusion.1
  202.8 0.8 fusion.49
  203.7 0.7 fusion.15
  204.4 2.0 fusion.29
  206.4 0.1 copy.53
  206.5 15.8 %all_gather.3 = bf16[1536,192]{1,0:T(8,128)(2,1)S(1)} all-gather(bf16[192,192]{1,0:T(8,128)(2,1)S(1)} %copy.53), channel_id=1, replica_groups=mesh['hz'=2,'hy'=4,'hx'=4,'wz'=4,'wc'=2] {'wz','wc'}, dimensions={0}, use_global_device_ids=true | all-gather | bytes 663552 | tf_op jit(solution)/shard_map/all_gather | solution.py:143
  222.3 3.4 %fusion.51 = f32[1536,768]{1,0:T(8,128)S(1)} fusion(bf16[1536,768]{0,1:T(8,128)(2,1)S(1)} %copy-done.4, bf16[768,768]{1,0:T(8,128)(2,1)} %param.26), kind=kOutput, calls=%fused_computation.98 | convolution fusion | flops 1811939328 | bytes 8257536 | tf_op jit(solution)/shard_map/dot_general | solution.py:151
  225.7 0.8 add_convert_fusion
  226.5 0.2 copy.71
  226.8 38.4 %all_to_all.22 = bf16[16,2,48,768]{3,2,1,0:T(8,128)(2,1)S(1)} all-to-all(bf16[16,2,48,768]{3,2,1,0:T(8,128)(2,1)S(1)} %bitcast.67), channel_id=1, replica_groups=mesh['hz'=2,'hy'=4,'hx'=4,'wz'=4,'wc'=2] {'hy','hx'}, dimensions={0} | all-to-all | bytes 4718592 | tf_op jit(solution)/shard_map/all_to_all | solution.py:60
  265.2 1.0 reduce_sum.51
  266.2 5.1 %all-to-all-start.3 = ((bf16[2,48,768]{2,1,0:T(8,128)(2,1)}), bf16[2,48,768]{2,1,0:T(8,128)(2,1)S(1)}, u32[]{:S(2)}, u32[]{:S(2)}) async-start(bf16[2,48,768]{2,1,0:T(8,128)(2,1)} %reduce_sum.51), calls=%async_computation.3 | async-start | bytes 294912 | tf_op jit(solution)/shard_map/all_to_all | solution.py:62
  271.3 1.1 constant_dynamic-slice_fusion
  272.4 0.7 copy.56
  273.1 1.0 constant_dynamic-slice_fusion.1
  274.1 0.7 copy.55
  274.9 4.9 %all-to-all-done.3 = bf16[2,48,768]{2,1,0:T(8,128)(2,1)S(1)} async-done(((bf16[2,48,768]{2,1,0:T(8,128)(2,1)}), bf16[2,48,768]{2,1,0:T(8,128)(2,1)S(1)}, u32[]{:S(2)}, u32[]{:S(2)}) %all-to-all-start.3) | async-done | bytes 147488 | tf_op jit(solution)/shard_map/all_to_all | solution.py:62
  279.8 1.5 fusion.38
  (49 shorter events, 0.9 us)
Async XLA Ops:
  7.2 72.1 %copy-start = (bf16[768,768]{1,0:T(8,128)(2,1)S(1)}, bf16[768,768]{1,0:T(8,128)(2,1)}, u32[]{:S(2)}) copy-start(bf16[768,768]{1,0:T(8,128)(2,1)} %param.24) | copy-start | bytes 3538948
  7.2 177.9 %all-reduce.2.cloned.1.call-start = ((), (), s32[]{:S(2)}) async-start(), calls=%async_computation.4 | async-start | bytes 8257536 | tf_op jit(solution)/shard_map/psum | solution.py:99
  75.8 0.7 copy-start.7
  75.8 0.7 copy-start.8
  75.8 0.7 copy-start.9
  75.9 0.7 copy-start.10
  76.6 1.2 copy-start.15
  81.4 2.2 copy-start.6
  85.9 102.5 %copy-start.11 = (f32[576]{0:T(1024)S(1)}, f32[576]{0:T(1024)}, u32[]{:S(2)}) copy-start(f32[576]{0:T(1024)} %param.21) | copy-start | bytes 6916
  188.4 2.2 copy-start.12
  188.7 1.8 copy-start.2
  202.8 3.5 %copy-start.3 = (bf16[1536,2,96]{0,2,1:T(8,128)(2,1)}, bf16[1536,2,96]{0,2,1:T(8,128)(2,1)S(1)}, u32[]{:S(2)}) copy-start(bf16[1536,2,96]{0,2,1:T(8,128)(2,1)S(1)} %pad_maximum_fusion.1) | copy-start | bytes 1769476
  203.6 18.6 %copy-start.4 = (bf16[1536,768]{0,1:T(8,128)(2,1)S(1)}, bf16[1536,768]{0,1:T(8,128)(2,1)}, u32[]{:S(2)}) copy-start(bf16[1536,768]{0,1:T(8,128)(2,1)} %fusion.2) | copy-start | bytes 7077892
  222.3 3.4 %copy-start.5 = (bf16[192,768]{1,0:T(8,128)(2,1)S(1)}, bf16[192,768]{1,0:T(8,128)(2,1)}, u32[]{:S(2)}) copy-start(bf16[192,768]{1,0:T(8,128)(2,1)} %param.22) | copy-start | bytes 884740
  226.5 54.9 %copy-start.1 = (bf16[768,768]{1,0:T(8,128)(2,1)S(1)}, bf16[768,768]{1,0:T(8,128)(2,1)}, u32[]{:S(2)}) copy-start(bf16[768,768]{1,0:T(8,128)(2,1)} %param.24) | copy-start | bytes 3538948
  226.7 53.1 %copy-start.13 = (f32[768]{0:T(1024)S(1)}, f32[768]{0:T(1024)}, u32[]{:S(2)}) copy-start(f32[768]{0:T(1024)} %param.27) | copy-start | bytes 9220
  226.8 53.1 %copy-start.14 = (f32[768]{0:T(1024)S(1)}, f32[768]{0:T(1024)}, u32[]{:S(2)}) copy-start(f32[768]{0:T(1024)} %param.23) | copy-start | bytes 9220
  266.2 13.6 %all-to-all-start.3 = ((bf16[2,48,768]{2,1,0:T(8,128)(2,1)}), bf16[2,48,768]{2,1,0:T(8,128)(2,1)S(1)}, u32[]{:S(2)}, u32[]{:S(2)}) async-start(bf16[2,48,768]{2,1,0:T(8,128)(2,1)} %reduce_sum.51), calls=%async_computation.3 | async-start | bytes 294912 | tf_op jit(solution)/shard_map/all_to_all | solution.py:62
Sparse Core Ops, SparseCore 0:
  83.8 101.2 all-reduce.1

commit v6 on v5

--- a/solution.py
+++ b/solution.py
@@ -139,16 +139,19 @@
         .reshape(own_rows, heads_dev * HD)
         .astype(jnp.bfloat16)
     )
-    attn_part = jnp.dot(
-        lax.all_gather(attended, WIDTH, axis=0, tiled=True),
-        dense_weight,
-        preferred_element_type=jnp.float32,
-    )
+    width_n = lax.axis_size(WIDTH)
+    shifted = [attended] + [
+        lax.ppermute(attended, WIDTH, [(i, (i + k) % width_n) for i in range(width_n)])
+        for k in range(1, width_n)
+    ]
+    sources = (lax.axis_index(WIDTH) - jnp.arange(width_n)) % width_n
+    gathered = jnp.take(jnp.stack(shifted), sources, axis=0).reshape(-1, attended.shape[1])
     hidden = jax.nn.gelu(summed_proj[:, qkv_cols:] + up_bias, approximate=False).astype(
         jnp.bfloat16
     )
     hidden = lax.optimization_barrier(hidden)
     mlp_part = jnp.dot(hidden, down_weight, preferred_element_type=jnp.float32)
+    attn_part = jnp.dot(gathered, dense_weight, preferred_element_type=jnp.float32)
     summed = reduce_heads((attn_part + mlp_part).astype(jnp.bfloat16))
     layer_out = (floats + summed + dense_bias + down_bias).astype(jnp.bfloat16)
     return (layer_out, key_cache, value_cache)

time: 291 us -> 302 us (1.038)
  blocking collectives: 120 us -> 103 us
  starting transfers between devices: 5.14 us -> 16.2 us
  waiting for transfers between devices: 104 us -> 111 us
  local copies, waits for them, and re-layouts: 7.66 us -> 12.1 us
  matrix products: 10.6 us -> 15 us
    all_gather x1 -> x0, blocking collectives: 15.8 us -> none  [on_device(): lax.all_gather(attended, WIDTH, axis=0, tiled=True)]
    ppermute x0 -> x7, starting transfers between devices: none -> 9.71 us  [on_device(): lax.ppermute(attended, WIDTH, [(i, (i + k) % width_n) for i in range(widt...]
    ppermute x0 -> x7, waiting for transfers between devices: none -> 6.97 us  [on_device(): lax.ppermute(attended, WIDTH, [(i, (i + k) % width_n) for i in range(widt...]
    unnamed x35 -> x42, local copies, waits for them, and re-layouts: 3.69 us -> 7.02 us
  transfers between devices with their start and end apart: 2 -> 9, of which waited for: 2 -> 4; matrix products, arithmetic and copies ran while one was open for 2% -> 8% of each run, Pallas kernels for 0% -> 0%
where the time goes in v6:
time: 302 us; the launch traced here: 298 us
  waiting for transfers between devices  111 us (37%)
  blocking collectives  103 us (34%)
  other arithmetic  26.8 us (9%)
  starting transfers between devices  16.2 us (5%)
  matrix products  15 us (5%)
  between operations  14.5 us (5%)
  local copies, waits for them, and re-layouts  12.1 us (4%)
    psum x1, waiting for transfers between devices, on_device(): lax.psum(projected.astype(jnp.bfloat16), WIDTH).astype(jnp.float32)  99 us
    all_to_all x1, blocking collectives, gather_heads(): block = lax.all_to_all(spread, ('hy', 'hx'), 0, 0, tiled=False)  40.4 us
    all_to_all x1, blocking collectives, reduce_heads(): part = lax.all_to_all(part, ('hy', 'hx'), 0, 0, tiled=False)  37.3 us
    all_to_all x1, blocking collectives, gather_heads(): block = lax.all_to_all(spread, 'hz', 0, 0, tiled=False).reshape(-1, cols)  14.2 us
    convert_element_type x1, other arithmetic, on_device(): jax.nn.gelu(summed_proj[:, qkv_cols:] + up_bias, approximate=False)  12.1 us
    psum x1, blocking collectives, on_device(): lax.psum(jnp.stack([jnp.sum(floats, -1), jnp.sum(floats * floats, -1)]),...  11.1 us
    ppermute x7, starting transfers between devices, on_device(): lax.ppermute(attended, WIDTH, [(i, (i + k) % width_n) for i in range(widt...  9.71 us
    unnamed x42, local copies, waits for them, and re-layouts  7.02 us
  transfers between devices with their start and end apart: 9, of which 4 were waited for; matrix products, arithmetic and copies ran while one was open for 8% of the time, Pallas kernels for 0%

profile of v6, /device:TPU:96, one launch (start us, length us, event | category | flops | bytes accessed | tf_op | source)
XLA Modules:
  0.0 298.4 jit_solution(2308216191753199989)
XLA Ops:
  7.2 1.1 convert_reduce_fusion.1
  8.3 11.1 %psum.14 = f32[2,48]{1,0:T(2,128)S(1)} all-reduce(f32[2,48]{1,0:T(2,128)S(1)} %pad_maximum_fusion.2), channel_id=1, replica_groups=mesh['hz'=2,'hy'=4,'hx'=4,'wz'=4,'wc'=2] {'wz','wc'}, use_global_device_ids=true, to_apply=%region_2.0 | all-reduce | flops 96 | bytes 768 | tf_op jit(solution)/shard_map/psum | solution.py:83
  19.5 1.0 fusion.38
  20.5 14.2 %all_to_all.20 = bf16[2,48,768]{2,1,0:T(8,128)(2,1)S(1)} all-to-all(bf16[2,48,768]{2,1,0:T(8,128)(2,1)S(1)} %broadcast_in_dim.48), channel_id=1, replica_groups=mesh['hz'=2,'hy'=4,'hx'=4,'wz'=4,'wc'=2] {'hz'}, dimensions={0} | all-to-all | bytes 294912 | tf_op jit(solution)/shard_map/all_to_all | solution.py:48
  34.7 0.2 broadcast_in_dim.84
  34.9 40.4 %all_to_all.21 = bf16[16,96,768]{2,1,0:T(8,128)(2,1)S(1)} all-to-all(bf16[16,96,768]{2,1,0:T(8,128)(2,1)S(1)} %broadcast_in_dim.84), channel_id=1, replica_groups=mesh['hz'=2,'hy'=4,'hx'=4,'wz'=4,'wc'=2] {'hy','hx'}, dimensions={0} | all-to-all | bytes 4718592 | tf_op jit(solution)/shard_map/all_to_all | solution.py:50
  75.2 0.6 convert_bitcast_fusion
  75.9 0.4 copy.72
  76.3 0.2 copy-done.7
  76.6 1.1 fusion.4
  77.7 1.6 convolution_convert_fusion.1
  79.3 2.1 convolution_convert_fusion
  81.4 2.2 pad_maximum_fusion
  84.1 0.3 reduce-window.9
  85.2 0.4 multiply_cosine_fusion
  85.6 0.5 fusion.21
  86.1 99.0 %all-reduce.2.cloned.1.call-done = bf16[1536,1344]{0,1:T(8,128)(2,1)} async-done(((bf16[1536,1344]{0,1:T(8,128)(2,1)}), bf16[1536,1344]{0,1:T(8,128)(2,1)}) %all-reduce.2.cloned.1.call-update) | async-done | bytes 4128784 | tf_op jit(solution)/shard_map/psum | solution.py:99
  185.1 3.3 %convert_element_type.82 = f32[1536,1344]{0,1:T(8,128)S(1)} convert(bf16[1536,1344]{0,1:T(8,128)(2,1)} %all-reduce.2.cloned.1.call-done) | non-fusion elementwise | flops 2064384 | bytes 12386304 | tf_op jit(solution)/shard_map/convert_element_type | solution.py:99
  188.4 3.2 %copy-done.2 = f32[1536,1344]{0,1:T(8,128)} copy-done((f32[1536,1344]{0,1:T(8,128)}, f32[1536,1344]{0,1:T(8,128)S(1)}, u32[]{:S(2)}) %copy-start.2) | copy-done | bytes 8257560
  191.6 0.3 slice_add_fusion.1
  192.0 1.7 copy-done.3
  194.4 0.8 fusion.56
  195.2 0.7 fusion.15
  195.9 2.0 fusion.29
  198.0 1.2 collective-permute-start.6
  199.2 0.9 collective-permute-start.5
  200.1 1.4 collective-permute-start.4
  201.4 0.7 collective-permute-start.3
  202.1 1.3 collective-permute-start
  203.4 12.1 %fusion.2 = bf16[1536,768]{0,1:T(8,128)(2,1)S(1)} fusion(f32[1536,1344]{0,1:T(8,128)} %copy-done.2, f32[768]{0:T(1024)S(1)} %copy-done.12), kind=kLoop, calls=%fused_computation.4 | loop fusion | flops 77856768 | bytes 7080960 | tf_op jit(solution)/shard_map/convert_element_type | solution.py:149
  215.6 5.4 %fusion.58 = f32[1536,768]{1,0:T(8,128)} fusion(bf16[1536,768]{0,1:T(8,128)(2,1)S(1)} %fusion.2, bf16[768,768]{1,0:T(8,128)(2,1)} %param.26), kind=kOutput, calls=%fused_computation.124 | convolution fusion | flops 1811939328 | bytes 8257536 | tf_op jit(solution)/shard_map/dot_general | solution.py:153
  221.1 1.4 collective-permute-start.1
  222.4 3.9 %collective-permute-done.1 = bf16[192,192]{1,0:T(8,128)(2,1)S(1)} collective-permute-done((bf16[192,192]{1,0:T(8,128)(2,1)S(1)}, bf16[192,192]{1,0:T(8,128)(2,1)S(1)}, u32[]{:S(2)}, u32[]{:S(2)}) %collective-permute-start.1) | collective-permute-done | bytes 73760 | tf_op jit(solution)/shard_map/ppermute | solution.py:144
  226.4 3.0 collective-permute-start.2
  229.4 3.0 %collective-permute-done.2 = bf16[192,192]{1,0:T(8,128)(2,1)S(1)} collective-permute-done((bf16[192,192]{1,0:T(8,128)(2,1)S(1)}, bf16[192,192]{1,0:T(8,128)(2,1)S(1)}, u32[]{:S(2)}, u32[]{:S(2)}) %collective-permute-start.2) | collective-permute-done | bytes 73760 | tf_op jit(solution)/shard_map/ppermute | solution.py:144
  232.5 0.6 gather_fusion
  233.1 0.3 copy.90
  233.4 3.2 %add_convert_fusion = bf16[1536,768]{1,0:T(8,128)(2,1)S(1)} fusion(f32[1536,768]{1,0:T(8,128)} %fusion.58, bf16[192,768]{1,0:T(8,128)(2,1)S(1)} %copy-done.5, bf16[1536,192]{0,1:T(8,128)(2,1)S(1)} %copy.90, pred[1536]{0:T(1024)(128)(4,1)S(1)} %broadcast_in_dim.42), kind=kOutput, calls=%fused_computation.13 | convolution fusion | flops 455639040 | bytes 7964160 | tf_op jit(solution)/shard_map/dot_general | solution.py:154
  236.6 0.2 copy.105
  236.8 37.3 %all_to_all.22 = bf16[16,2,48,768]{3,2,1,0:T(8,128)(2,1)S(1)} all-to-all(bf16[16,2,48,768]{3,2,1,0:T(8,128)(2,1)S(1)} %bitcast.84), channel_id=1, replica_groups=mesh['hz'=2,'hy'=4,'hx'=4,'wz'=4,'wc'=2] {'hy','hx'}, dimensions={0} | all-to-all | bytes 4718592 | tf_op jit(solution)/shard_map/all_to_all | solution.py:60
  274.1 1.0 reduce_sum.51
  275.1 6.4 %all-to-all-start.3 = ((bf16[2,48,768]{2,1,0:T(8,128)(2,1)}), bf16[2,48,768]{2,1,0:T(8,128)(2,1)S(1)}, u32[]{:S(2)}, u32[]{:S(2)}) async-start(bf16[2,48,768]{2,1,0:T(8,128)(2,1)} %reduce_sum.51), calls=%async_computation.3 | async-start | bytes 294912 | tf_op jit(solution)/shard_map/all_to_all | solution.py:62
  281.5 1.1 constant_dynamic-slice_fusion
  282.6 0.7 copy.89
  283.4 1.0 constant_dynamic-slice_fusion.1
  284.4 0.7 copy.88
  285.1 4.9 %all-to-all-done.3 = bf16[2,48,768]{2,1,0:T(8,128)(2,1)S(1)} async-done(((bf16[2,48,768]{2,1,0:T(8,128)(2,1)}), bf16[2,48,768]{2,1,0:T(8,128)(2,1)S(1)}, u32[]{:S(2)}, u32[]{:S(2)}) %all-to-all-start.3) | async-done | bytes 147488 | tf_op jit(solution)/shard_map/all_to_all | solution.py:62
  290.1 1.5 fusion.41
  (78 shorter events, 2.5 us)
Async XLA Ops:
  7.2 72.1 %copy-start = (bf16[768,768]{1,0:T(8,128)(2,1)S(1)}, bf16[768,768]{1,0:T(8,128)(2,1)}, u32[]{:S(2)}) copy-start(bf16[768,768]{1,0:T(8,128)(2,1)} %param.24) | copy-start | bytes 3538948
  7.2 177.9 %all-reduce.2.cloned.1.call-start = ((), (), s32[]{:S(2)}) async-start(), calls=%async_computation.4 | async-start | bytes 8257536 | tf_op jit(solution)/shard_map/psum | solution.py:99
  75.8 0.7 copy-start.7
  75.8 0.7 copy-start.8
  75.8 0.7 copy-start.9
  75.9 0.7 copy-start.10
  76.6 1.2 copy-start.15
  81.4 2.4 copy-start.6
  86.1 105.5 %copy-start.11 = (f32[576]{0:T(1024)S(1)}, f32[576]{0:T(1024)}, u32[]{:S(2)}) copy-start(f32[576]{0:T(1024)} %param.21) | copy-start | bytes 6916
  188.4 3.2 %copy-start.2 = (f32[1536,1344]{0,1:T(8,128)}, f32[1536,1344]{0,1:T(8,128)S(1)}, u32[]{:S(2)}) copy-start(f32[1536,1344]{0,1:T(8,128)S(1)} %convert_element_type.82) | copy-start | bytes 24772612
  191.9 1.9 copy-start.3
  194.4 3.5 %copy-start.4 = (bf16[1536,2,96]{0,2,1:T(8,128)(2,1)}, bf16[1536,2,96]{0,2,1:T(8,128)(2,1)S(1)}, u32[]{:S(2)}) copy-start(bf16[1536,2,96]{0,2,1:T(8,128)(2,1)S(1)} %pad_maximum_fusion.1) | copy-start | bytes 1769476
  195.2 8.2 %copy-start.12 = (f32[768]{0:T(1024)S(1)}, f32[768]{0:T(1024)}, u32[]{:S(2)}) copy-start(f32[768]{0:T(1024)} %param.25) | copy-start | bytes 9220
  198.0 34.5 %collective-permute-start.6 = (bf16[192,192]{1,0:T(8,128)(2,1)S(1)}, bf16[192,192]{1,0:T(8,128)(2,1)S(1)}, u32[]{:S(2)}, u32[]{:S(2)}) collective-permute-start(bf16[192,192]{1,0:T(8,128)(2,1)S(1)} %copy.78), channel_id=1, source_target_pairs={{0,7},{1,0},{2,1},{3,2},{4,3},{5,4},{6,5},{7,6},{8,15},{9,8},{10,9... | collective-permute-start | bytes 221192 | tf_op jit(solution)/shard_map/ppermute | solution.py:144
  199.2 33.3 %collective-permute-start.5 = (bf16[192,192]{1,0:T(8,128)(2,1)S(1)}, bf16[192,192]{1,0:T(8,128)(2,1)S(1)}, u32[]{:S(2)}, u32[]{:S(2)}) collective-permute-start(bf16[192,192]{1,0:T(8,128)(2,1)S(1)} %copy.78), channel_id=1, source_target_pairs={{0,6},{1,7},{2,0},{3,1},{4,2},{5,3},{6,4},{7,5},{8,14},{9,15},{10,... | collective-permute-start | bytes 221192 | tf_op jit(solution)/shard_map/ppermute | solution.py:144
  200.1 32.4 %collective-permute-start.4 = (bf16[192,192]{1,0:T(8,128)(2,1)S(1)}, bf16[192,192]{1,0:T(8,128)(2,1)S(1)}, u32[]{:S(2)}, u32[]{:S(2)}) collective-permute-start(bf16[192,192]{1,0:T(8,128)(2,1)S(1)} %copy.78), channel_id=1, source_target_pairs={{0,5},{1,6},{2,7},{3,0},{4,1},{5,2},{6,3},{7,4},{8,13},{9,14},{10,... | collective-permute-start | bytes 221192 | tf_op jit(solution)/shard_map/ppermute | solution.py:144
  201.4 31.0 %collective-permute-start.3 = (bf16[192,192]{1,0:T(8,128)(2,1)S(1)}, bf16[192,192]{1,0:T(8,128)(2,1)S(1)}, u32[]{:S(2)}, u32[]{:S(2)}) collective-permute-start(bf16[192,192]{1,0:T(8,128)(2,1)S(1)} %copy.78), channel_id=1, source_target_pairs={{0,4},{1,5},{2,6},{3,7},{4,0},{5,1},{6,2},{7,3},{8,12},{9,13},{10,... | collective-permute-start | bytes 221192 | tf_op jit(solution)/shard_map/ppermute | solution.py:144
  202.1 19.0 %collective-permute-start = (bf16[192,192]{1,0:T(8,128)(2,1)S(1)}, bf16[192,192]{1,0:T(8,128)(2,1)S(1)}, u32[]{:S(2)}, u32[]{:S(2)}) collective-permute-start(bf16[192,192]{1,0:T(8,128)(2,1)S(1)} %copy.78), channel_id=1, source_target_pairs={{0,1},{1,2},{2,3},{3,4},{4,5},{5,6},{6,7},{7,0},{8,9},{9,10},{10,1... | collective-permute-start | bytes 221192 | tf_op jit(solution)/shard_map/ppermute | solution.py:144
  221.0 12.3 %copy-start.5 = (bf16[192,768]{1,0:T(8,128)(2,1)S(1)}, bf16[192,768]{1,0:T(8,128)(2,1)}, u32[]{:S(2)}) copy-start(bf16[192,768]{1,0:T(8,128)(2,1)} %param.22) | copy-start | bytes 884740
  221.1 5.3 %collective-permute-start.1 = (bf16[192,192]{1,0:T(8,128)(2,1)S(1)}, bf16[192,192]{1,0:T(8,128)(2,1)S(1)}, u32[]{:S(2)}, u32[]{:S(2)}) collective-permute-start(bf16[192,192]{1,0:T(8,128)(2,1)S(1)} %copy.78), channel_id=1, source_target_pairs={{0,2},{1,3},{2,4},{3,5},{4,6},{5,7},{6,0},{7,1},{8,10},{9,11},{10,... | collective-permute-start | bytes 221192 | tf_op jit(solution)/shard_map/ppermute | solution.py:144
  226.4 6.0 %collective-permute-start.2 = (bf16[192,192]{1,0:T(8,128)(2,1)S(1)}, bf16[192,192]{1,0:T(8,128)(2,1)S(1)}, u32[]{:S(2)}, u32[]{:S(2)}) collective-permute-start(bf16[192,192]{1,0:T(8,128)(2,1)S(1)} %copy.78), channel_id=1, source_target_pairs={{0,3},{1,4},{2,5},{3,6},{4,7},{5,0},{6,1},{7,2},{8,11},{9,12},{10,... | collective-permute-start | bytes 221192 | tf_op jit(solution)/shard_map/ppermute | solution.py:144
  236.6 55.0 %copy-start.1 = (bf16[768,768]{1,0:T(8,128)(2,1)S(1)}, bf16[768,768]{1,0:T(8,128)(2,1)}, u32[]{:S(2)}) copy-start(bf16[768,768]{1,0:T(8,128)(2,1)} %param.24) | copy-start | bytes 3538948
  236.8 53.2 %copy-start.13 = (f32[768]{0:T(1024)S(1)}, f32[768]{0:T(1024)}, u32[]{:S(2)}) copy-start(f32[768]{0:T(1024)} %param.27) | copy-start | bytes 9220
  236.8 53.2 %copy-start.14 = (f32[768]{0:T(1024)S(1)}, f32[768]{0:T(1024)}, u32[]{:S(2)}) copy-start(f32[768]{0:T(1024)} %param.23) | copy-start | bytes 9220
  275.1 14.9 %all-to-all-start.3 = ((bf16[2,48,768]{2,1,0:T(8,128)(2,1)}), bf16[2,48,768]{2,1,0:T(8,128)(2,1)S(1)}, u32[]{:S(2)}, u32[]{:S(2)}) async-start(bf16[2,48,768]{2,1,0:T(8,128)(2,1)} %reduce_sum.51), calls=%async_computation.3 | async-start | bytes 294912 | tf_op jit(solution)/shard_map/all_to_all | solution.py:62
Sparse Core Ops, SparseCore 0:
  83.8 101.2 all-reduce.1

commit v7 on v5

--- a/solution.py
+++ b/solution.py
@@ -43,12 +43,11 @@
 
 def gather_heads(block):
     rows, cols = block.shape
-    nz, ny, nx = [lax.axis_size(a) for a in HEADS]
-    spread = jnp.broadcast_to(block[None], (nz,) + block.shape)
-    block = lax.all_to_all(spread, "hz", 0, 0, tiled=False).reshape(-1, cols)
+    ny, nx = lax.axis_size("hy"), lax.axis_size("hx")
     spread = jnp.broadcast_to(block[None], (ny * nx,) + block.shape)
     block = lax.all_to_all(spread, ("hy", "hx"), 0, 0, tiled=False)
-    block = block.reshape(ny, nx, nz, rows, cols).transpose(2, 0, 1, 3, 4)
+    nz = lax.axis_size("hz")
+    block = block.reshape(ny, nx, nz, rows // nz, cols).transpose(2, 0, 1, 3, 4)
     return block.reshape(-1, cols)
 
 
@@ -80,13 +79,20 @@
     down_bias,
 ):
     floats = states.astype(jnp.float32)
-    stats = lax.psum(jnp.stack([jnp.sum(floats, -1), jnp.sum(floats * floats, -1)]), WIDTH)
-    row_mean = (stats[0] / D)[:, None]
-    row_var = (stats[1] / D)[:, None] - row_mean * row_mean
-    normed = ((floats - row_mean) * lax.rsqrt(row_var + norm_epsilon)).astype(jnp.bfloat16)
+    nz = lax.axis_size("hz")
+    z = lax.axis_index("hz")
+    swaps = [lax.ppermute(states, "hz", [(i, (i + k) % nz) for i in range(nz)]) for k in range(1, nz)]
+    local = jnp.stack([jnp.sum(floats, -1), jnp.sum(floats * floats, -1)])
+    every = lax.all_gather(local, ("hz",) + WIDTH, axis=0, tiled=False)
+    stats = jnp.sum(every.reshape(nz, -1, 2, local.shape[1]), 1)
+    pair = jnp.stack([states] + swaps)
+    by_z = jnp.take(pair, (z - jnp.arange(nz)) % nz, axis=0).astype(jnp.float32)
+    row_mean = (stats[:, 0] / D)[..., None]
+    row_var = (stats[:, 1] / D)[..., None] - row_mean * row_mean
+    normed = ((by_z - row_mean) * lax.rsqrt(row_var + norm_epsilon)).astype(jnp.bfloat16)
     qkv_cols = qkv_weight.shape[1]
     heads_dev = qkv_cols // (3 * HD)
-    block_f = gather_heads(normed).astype(jnp.float32)
+    block_f = gather_heads(normed.reshape(-1, normed.shape[2])).astype(jnp.float32)
     attn_in = (block_f * attn_gain + attn_shift).astype(jnp.bfloat16)
     mlp_in = (block_f * mlp_gain + mlp_shift).astype(jnp.bfloat16)
     projected = jnp.concatenate(

time: 291 us -> 286 us (0.983)
  blocking collectives: 120 us -> 107 us
  starting transfers between devices: 5.14 us -> 9.72 us
  waiting for transfers between devices: 104 us -> 107 us
    all_to_all x1 -> x0, blocking collectives: 14.2 us -> none  [gather_heads(): block = lax.all_to_all(spread, 'hz', 0, 0, tiled=False).reshape(-1, cols)]
    all_gather x0 -> x1, blocking collectives: none -> 13.9 us  [on_device(): every = lax.all_gather(local, ('hz',) + WIDTH, axis=0, tiled=False)]
    psum x1 -> x0, blocking collectives: 11.1 us -> none  [on_device(): lax.psum(jnp.stack([jnp.sum(floats, -1), jnp.sum(floats * floats, -1)]),...]
    ppermute x0 -> x1, starting transfers between devices: none -> 4.58 us  [on_device(): lax.ppermute(states, 'hz', [(i, (i + k) % nz) for i in range(nz)])]
  transfers between devices with their start and end apart: 2 -> 3, of which waited for: 2 -> 2; matrix products, arithmetic and copies ran while one was open for 2% -> 3% of each run, Pallas kernels for 0% -> 0%
where the time goes in v7:
time: 286 us; the launch traced here: 283 us
  blocking collectives  107 us (37%)
  waiting for transfers between devices  107 us (37%)
  other arithmetic  26.4 us (9%)
  between operations  14.4 us (5%)
  matrix products  10.6 us (4%)
  starting transfers between devices  9.72 us (3%)
  local copies, waits for them, and re-layouts  8.53 us (3%)
    psum x1, waiting for transfers between devices, on_device(): lax.psum(projected.astype(jnp.bfloat16), WIDTH).astype(jnp.float32)  102 us
    all_to_all x1, blocking collectives, gather_heads(): block = lax.all_to_all(spread, ('hy', 'hx'), 0, 0, tiled=False)  38.6 us
    all_to_all x1, blocking collectives, reduce_heads(): part = lax.all_to_all(part, ('hy', 'hx'), 0, 0, tiled=False)  38.4 us
    all_gather x1, blocking collectives, on_device(): lax.all_gather(attended, WIDTH, axis=0, tiled=True)  15.8 us
    all_gather x1, blocking collectives, on_device(): every = lax.all_gather(local, ('hz',) + WIDTH, axis=0, tiled=False)  13.9 us
    convert_element_type x1, other arithmetic, on_device(): jax.nn.gelu(summed_proj[:, qkv_cols:] + up_bias, approximate=False)  11.7 us
  transfers between devices with their start and end apart: 3, of which 2 were waited for; matrix products, arithmetic and copies ran while one was open for 3% of the time, Pallas kernels for 0%

profile of v7, /device:TPU:96, one launch (start us, length us, event | category | flops | bytes accessed | tf_op | source)
XLA Modules:
  0.0 283.2 jit_solution(1064347083924799457)
XLA Ops:
  7.2 4.6 %collective-permute-start = (bf16[48,768]{1,0:T(8,128)(2,1)}, bf16[48,768]{1,0:T(8,128)(2,1)S(1)}, u32[]{:S(2)}, u32[]{:S(2)}) collective-permute-start(bf16[48,768]{1,0:T(8,128)(2,1)} %param.14), channel_id=1, source_target_pairs={{0,128},{128,0},{1,129},{129,1},{2,130},{130,2},{3,131},{131,3},{4... | collective-permute-start | bytes 221192 | tf_op jit(solution)/shard_map/ppermute | solution.py:84
  11.8 1.0 convert_reduce_fusion.1
  13.0 13.9 %all-gather.1 = f32[16,2,48]{2,1,0:T(2,128)S(1)} all-gather(f32[1,2,48]{2,1,0:T(2,128)S(1)} %maximum_bitcast_fusion), channel_id=2, replica_groups=mesh['hz'=2,'hy'=4,'hx'=4,'wz'=4,'wc'=2] {'hz','wz','wc'}, dimensions={0}, use_global_device_ids=true | all-gather | bytes 6528 | tf_op jit(solution)/shard_map/all_gather | solution.py:86
  27.2 0.9 pad_maximum_fusion.2
  28.1 0.6 gather_fusion
  28.7 0.1 multiply_convert_fusion
  28.8 0.2 broadcast_in_dim.45
  29.0 38.6 %all_to_all.15 = bf16[16,96,768]{2,1,0:T(8,128)(2,1)S(1)} all-to-all(bf16[16,96,768]{2,1,0:T(8,128)(2,1)S(1)} %broadcast_in_dim.45), channel_id=1, replica_groups=mesh['hz'=2,'hy'=4,'hx'=4,'wz'=4,'wc'=2] {'hy','hx'}, dimensions={0} | all-to-all | bytes 4718592 | tf_op jit(solution)/shard_map/all_to_all | solution.py:48
  67.6 0.6 convert_bitcast_fusion
  68.2 0.4 copy.47
  68.7 0.2 copy-done.7
  68.9 1.1 fusion.4
  70.0 0.1 copy-done.15
  70.1 1.6 convolution_convert_fusion.1
  71.7 2.1 convolution_convert_fusion
  73.8 2.2 pad_maximum_fusion
  76.3 0.3 reduce-window.9
  76.7 0.1 slice_reduce_fusion
  77.0 0.2 multiply_cosine_fusion.1
  77.1 0.1 copy.49
  77.2 0.1 copy.50
  77.4 0.4 multiply_cosine_fusion
  77.8 0.5 fusion.21
  78.3 101.8 %all-reduce.2.cloned.1.call-done = bf16[1536,1344]{0,1:T(8,128)(2,1)} async-done(((bf16[1536,1344]{0,1:T(8,128)(2,1)}), bf16[1536,1344]{0,1:T(8,128)(2,1)}) %all-reduce.2.cloned.1.call-update) | async-done | bytes 4128784 | tf_op jit(solution)/shard_map/psum | solution.py:105
  180.0 3.3 %convert_element_type.84 = f32[1536,1344]{0,1:T(8,128)S(1)} convert(bf16[1536,1344]{0,1:T(8,128)(2,1)} %all-reduce.2.cloned.1.call-done) | non-fusion elementwise | flops 2064384 | bytes 12386304 | tf_op jit(solution)/shard_map/convert_element_type | solution.py:105
  183.4 0.3 slice_add_fusion.1
  183.7 0.1 constant_dynamic-slice_fusion.2
  183.8 1.6 copy-done.2
  185.5 11.7 %fusion.2 = bf16[1536,768]{0,1:T(8,128)(2,1)} fusion(f32[1536,1344]{0,1:T(8,128)S(1)} %convert_element_type.84, f32[768]{0:T(1024)S(1)} %copy-done.12), kind=kLoop, calls=%fused_computation.4 | loop fusion | flops 77856768 | bytes 7080960 | tf_op jit(solution)/shard_map/convert_element_type | solution.py:153
  197.3 0.1 copy.58
  197.6 0.1 subtract_convert_fusion.1
  197.9 0.8 fusion.50
  198.7 0.7 fusion.15
  199.4 2.0 fusion.29
  201.4 0.1 copy.53
  201.5 15.8 %all_gather.11 = bf16[1536,192]{1,0:T(8,128)(2,1)S(1)} all-gather(bf16[192,192]{1,0:T(8,128)(2,1)S(1)} %copy.53), channel_id=1, replica_groups=mesh['hz'=2,'hy'=4,'hx'=4,'wz'=4,'wc'=2] {'wz','wc'}, dimensions={0}, use_global_device_ids=true | all-gather | bytes 663552 | tf_op jit(solution)/shard_map/all_gather | solution.py:149
  217.3 3.4 %fusion.52 = f32[1536,768]{1,0:T(8,128)S(1)} fusion(bf16[1536,768]{0,1:T(8,128)(2,1)S(1)} %copy-done.4, bf16[768,768]{1,0:T(8,128)(2,1)} %param.26), kind=kOutput, calls=%fused_computation.114 | convolution fusion | flops 1811939328 | bytes 8257536 | tf_op jit(solution)/shard_map/dot_general | solution.py:157
  220.7 0.8 add_convert_fusion
  221.5 0.2 copy.71
  221.8 38.4 %all_to_all.16 = bf16[16,2,48,768]{3,2,1,0:T(8,128)(2,1)S(1)} all-to-all(bf16[16,2,48,768]{3,2,1,0:T(8,128)(2,1)S(1)} %bitcast.68), channel_id=1, replica_groups=mesh['hz'=2,'hy'=4,'hx'=4,'wz'=4,'wc'=2] {'hy','hx'}, dimensions={0} | all-to-all | bytes 4718592 | tf_op jit(solution)/shard_map/all_to_all | solution.py:59
  260.2 1.0 reduce_sum.61
  261.2 5.1 %all-to-all-start.2 = ((bf16[2,48,768]{2,1,0:T(8,128)(2,1)}), bf16[2,48,768]{2,1,0:T(8,128)(2,1)S(1)}, u32[]{:S(2)}, u32[]{:S(2)}) async-start(bf16[2,48,768]{2,1,0:T(8,128)(2,1)} %reduce_sum.61), calls=%async_computation.2 | async-start | bytes 294912 | tf_op jit(solution)/shard_map/all_to_all | solution.py:61
  266.3 1.1 constant_dynamic-slice_fusion
  267.4 0.7 copy.56
  268.2 1.0 constant_dynamic-slice_fusion.1
  269.2 0.7 copy.55
  269.9 4.9 %all-to-all-done.2 = bf16[2,48,768]{2,1,0:T(8,128)(2,1)S(1)} async-done(((bf16[2,48,768]{2,1,0:T(8,128)(2,1)}), bf16[2,48,768]{2,1,0:T(8,128)(2,1)S(1)}, u32[]{:S(2)}, u32[]{:S(2)}) %all-to-all-start.2) | async-done | bytes 147488 | tf_op jit(solution)/shard_map/all_to_all | solution.py:61
  274.9 1.5 fusion.36
  (59 shorter events, 1.5 us)
Async XLA Ops:
  7.2 64.5 %copy-start = (bf16[768,768]{1,0:T(8,128)(2,1)S(1)}, bf16[768,768]{1,0:T(8,128)(2,1)}, u32[]{:S(2)}) copy-start(bf16[768,768]{1,0:T(8,128)(2,1)} %param.24) | copy-start | bytes 3538948
  7.2 172.9 %all-reduce.2.cloned.1.call-start = ((), (), s32[]{:S(2)}) async-start(), calls=%async_computation.3 | async-start | bytes 8257536 | tf_op jit(solution)/shard_map/psum | solution.py:105
  7.2 20.0 %collective-permute-start = (bf16[48,768]{1,0:T(8,128)(2,1)}, bf16[48,768]{1,0:T(8,128)(2,1)S(1)}, u32[]{:S(2)}, u32[]{:S(2)}) collective-permute-start(bf16[48,768]{1,0:T(8,128)(2,1)} %param.14), channel_id=1, source_target_pairs={{0,128},{128,0},{1,129},{129,1},{2,130},{130,2},{3,131},{131,3},{4... | collective-permute-start | bytes 221192 | tf_op jit(solution)/shard_map/ppermute | solution.py:84
  68.2 0.7 copy-start.7
  68.2 0.7 copy-start.8
  68.2 0.7 copy-start.9
  68.2 0.7 copy-start.10
  68.9 1.2 copy-start.15
  73.8 2.2 copy-start.6
  78.2 105.1 %copy-start.11 = (f32[576]{0:T(1024)S(1)}, f32[576]{0:T(1024)}, u32[]{:S(2)}) copy-start(f32[576]{0:T(1024)} %param.21) | copy-start | bytes 6916
  183.4 2.2 copy-start.12
  183.7 1.8 copy-start.2
  197.8 3.5 %copy-start.3 = (bf16[1536,2,96]{0,2,1:T(8,128)(2,1)}, bf16[1536,2,96]{0,2,1:T(8,128)(2,1)S(1)}, u32[]{:S(2)}) copy-start(bf16[1536,2,96]{0,2,1:T(8,128)(2,1)S(1)} %pad_maximum_fusion.1) | copy-start | bytes 1769476
  198.7 18.6 %copy-start.4 = (bf16[1536,768]{0,1:T(8,128)(2,1)S(1)}, bf16[1536,768]{0,1:T(8,128)(2,1)}, u32[]{:S(2)}) copy-start(bf16[1536,768]{0,1:T(8,128)(2,1)} %fusion.2) | copy-start | bytes 7077892
  217.3 3.4 %copy-start.5 = (bf16[192,768]{1,0:T(8,128)(2,1)S(1)}, bf16[192,768]{1,0:T(8,128)(2,1)}, u32[]{:S(2)}) copy-start(bf16[192,768]{1,0:T(8,128)(2,1)} %param.22) | copy-start | bytes 884740
  221.5 54.9 %copy-start.1 = (bf16[768,768]{1,0:T(8,128)(2,1)S(1)}, bf16[768,768]{1,0:T(8,128)(2,1)}, u32[]{:S(2)}) copy-start(bf16[768,768]{1,0:T(8,128)(2,1)} %param.24) | copy-start | bytes 3538948
  221.8 53.1 %copy-start.13 = (f32[768]{0:T(1024)S(1)}, f32[768]{0:T(1024)}, u32[]{:S(2)}) copy-start(f32[768]{0:T(1024)} %param.27) | copy-start | bytes 9220
  221.8 53.1 %copy-start.14 = (f32[768]{0:T(1024)S(1)}, f32[768]{0:T(1024)}, u32[]{:S(2)}) copy-start(f32[768]{0:T(1024)} %param.23) | copy-start | bytes 9220
  261.2 13.6 %all-to-all-start.2 = ((bf16[2,48,768]{2,1,0:T(8,128)(2,1)}), bf16[2,48,768]{2,1,0:T(8,128)(2,1)S(1)}, u32[]{:S(2)}, u32[]{:S(2)}) async-start(bf16[2,48,768]{2,1,0:T(8,128)(2,1)} %reduce_sum.61), calls=%async_computation.2 | async-start | bytes 294912 | tf_op jit(solution)/shard_map/all_to_all | solution.py:61
Sparse Core Ops, SparseCore 0:
  76.2 103.8 all-reduce.1

commit v8 on v7

--- a/solution.py
+++ b/solution.py
@@ -102,7 +102,7 @@
         ],
         axis=1,
     )
-    summed_proj = lax.psum(projected.astype(jnp.bfloat16), WIDTH).astype(jnp.float32)
+    summed_proj = lax.psum(projected.astype(jnp.bfloat16), WIDTH)
     all_tokens = projected.shape[0]
     own_rows = all_tokens // lax.axis_size(WIDTH)
     row_zero = lax.axis_index(WIDTH) * own_rows
@@ -111,7 +111,7 @@
     own_index = row_zero + jnp.arange(own_rows, dtype=jnp.int32)
     score_scale = 1.0 / HD**0.5
     own_positions = lax.dynamic_slice_in_dim(positions, row_zero, own_rows)
-    shaped = (summed_proj[:, :qkv_cols] + qkv_bias).reshape(all_tokens, heads_dev, 3, HD)
+    shaped = (summed_proj[:, :qkv_cols].astype(jnp.float32) + qkv_bias).reshape(all_tokens, heads_dev, 3, HD)
     own_shaped = lax.dynamic_slice_in_dim(shaped, row_zero, own_rows)
     queries = rotary(own_shaped[:, :, 0, :], own_positions).astype(jnp.bfloat16)
     key_heads = rotary(shaped[:, :, 1, :], positions).astype(jnp.bfloat16)
@@ -150,7 +150,7 @@
         dense_weight,
         preferred_element_type=jnp.float32,
     )
-    hidden = jax.nn.gelu(summed_proj[:, qkv_cols:] + up_bias, approximate=False).astype(
+    hidden = jax.nn.gelu(summed_proj[:, qkv_cols:].astype(jnp.float32) + up_bias, approximate=False).astype(
         jnp.bfloat16
     )
     hidden = lax.optimization_barrier(hidden)

time: 286 us -> 286 us (level)
    convert_element_type x2 -> x1, other arithmetic: 15.1 us -> 11.9 us  [on_device(): jax.nn.gelu(summed_proj[:, qkv_cols:].astype(jnp.float32) + up_bias, appr...]
where the time goes in v8:
time: 286 us; the launch traced here: 283 us
  blocking collectives  107 us (37%)
  waiting for transfers between devices  107 us (37%)
  other arithmetic  24.9 us (9%)
  between operations  14.4 us (5%)
  matrix products  11 us (4%)
  starting transfers between devices  9.71 us (3%)
  local copies, waits for them, and re-layouts  9.4 us (3%)
    psum x1, waiting for transfers between devices, on_device(): summed_proj = lax.psum(projected.astype(jnp.bfloat16), WIDTH)  102 us
    all_to_all x1, blocking collectives, gather_heads(): block = lax.all_to_all(spread, ('hy', 'hx'), 0, 0, tiled=False)  38.6 us
    all_to_all x1, blocking collectives, reduce_heads(): part = lax.all_to_all(part, ('hy', 'hx'), 0, 0, tiled=False)  38.3 us
    all_gather x1, blocking collectives, on_device(): lax.all_gather(attended, WIDTH, axis=0, tiled=True)  15.8 us
    all_gather x1, blocking collectives, on_device(): every = lax.all_gather(local, ('hz',) + WIDTH, axis=0, tiled=False)  13.9 us
    convert_element_type x1, other arithmetic, on_device(): jax.nn.gelu(summed_proj[:, qkv_cols:].astype(jnp.float32) + up_bias, appr...  11.9 us
  transfers between devices with their start and end apart: 3, of which 2 were waited for; matrix products, arithmetic and copies ran while one was open for 3% of the time, Pallas kernels for 0%

profile of v8, /device:TPU:96, one launch (start us, length us, event | category | flops | bytes accessed | tf_op | source)
XLA Modules:
  0.0 282.8 jit_solution(10883065932688507212)
XLA Ops:
  7.2 4.6 %collective-permute-start = (bf16[48,768]{1,0:T(8,128)(2,1)}, bf16[48,768]{1,0:T(8,128)(2,1)S(1)}, u32[]{:S(2)}, u32[]{:S(2)}) collective-permute-start(bf16[48,768]{1,0:T(8,128)(2,1)} %param.14), channel_id=1, source_target_pairs={{0,128},{128,0},{1,129},{129,1},{2,130},{130,2},{3,131},{131,3},{4... | collective-permute-start | bytes 221192 | tf_op jit(solution)/shard_map/ppermute | solution.py:84
  11.8 1.0 convert_reduce_fusion.1
  13.0 13.9 %all-gather.1 = f32[16,2,48]{2,1,0:T(2,128)S(1)} all-gather(f32[1,2,48]{2,1,0:T(2,128)S(1)} %maximum_bitcast_fusion), channel_id=2, replica_groups=mesh['hz'=2,'hy'=4,'hx'=4,'wz'=4,'wc'=2] {'hz','wz','wc'}, dimensions={0}, use_global_device_ids=true | all-gather | bytes 6528 | tf_op jit(solution)/shard_map/all_gather | solution.py:86
  27.2 0.9 pad_maximum_fusion.2
  28.1 0.6 gather_fusion
  28.7 0.1 multiply_convert_fusion
  28.8 0.2 broadcast_in_dim.45
  29.0 38.6 %all_to_all.15 = bf16[16,96,768]{2,1,0:T(8,128)(2,1)S(1)} all-to-all(bf16[16,96,768]{2,1,0:T(8,128)(2,1)S(1)} %broadcast_in_dim.45), channel_id=1, replica_groups=mesh['hz'=2,'hy'=4,'hx'=4,'wz'=4,'wc'=2] {'hy','hx'}, dimensions={0} | all-to-all | bytes 4718592 | tf_op jit(solution)/shard_map/all_to_all | solution.py:48
  67.6 0.6 convert_bitcast_fusion
  68.2 0.4 copy.47
  68.7 0.2 copy-done.6
  68.9 1.1 fusion.4
  70.0 0.1 copy-done.15
  70.1 1.6 convolution_convert_fusion.1
  71.7 2.1 convolution_convert_fusion
  73.8 2.2 pad_maximum_fusion
  76.3 0.3 reduce-window.9
  76.7 0.1 slice_reduce_fusion
  77.0 0.2 multiply_cosine_fusion.1
  77.1 0.1 copy.49
  77.3 0.1 copy.50
  77.4 0.4 multiply_cosine_fusion
  77.8 0.5 fusion.24
  78.3 101.8 %all-reduce.2.cloned.1.call-done = bf16[1536,1344]{0,1:T(8,128)(2,1)} async-done(((bf16[1536,1344]{0,1:T(8,128)(2,1)}), bf16[1536,1344]{0,1:T(8,128)(2,1)}) %all-reduce.2.cloned.1.call-update) | async-done | bytes 4128784 | tf_op jit(solution)/shard_map/psum | solution.py:105
  180.1 1.9 convert_add_fusion.1
  182.0 0.1 constant_dynamic-slice_fusion.2
  182.1 1.7 copy-done.1
  183.9 11.9 %fusion.2 = bf16[1536,768]{0,1:T(8,128)(2,1)} fusion(bf16[1536,1344]{0,1:T(8,128)(2,1)S(1)} %copy-done.2, f32[768]{0:T(1024)S(1)} %copy-done.13), kind=kLoop, calls=%fused_computation.4 | loop fusion | flops 79036416 | bytes 4721664 | tf_op jit(solution)/shard_map/convert_element_type | solution.py:153
  195.8 0.1 copy.58
  196.1 0.1 subtract_convert_fusion.1
  196.4 0.8 copy-done.3
  197.2 0.8 fusion.53
  198.0 0.7 fusion.18
  198.7 2.0 fusion.32
  200.7 0.1 copy.53
  200.8 15.8 %all_gather.11 = bf16[1536,192]{1,0:T(8,128)(2,1)S(1)} all-gather(bf16[192,192]{1,0:T(8,128)(2,1)S(1)} %copy.53), channel_id=1, replica_groups=mesh['hz'=2,'hy'=4,'hx'=4,'wz'=4,'wc'=2] {'wz','wc'}, dimensions={0}, use_global_device_ids=true | all-gather | bytes 663552 | tf_op jit(solution)/shard_map/all_gather | solution.py:149
  216.6 3.8 %fusion.55 = f32[1536,768]{1,0:T(8,128)S(1)} fusion(bf16[1536,768]{0,1:T(8,128)(2,1)} %fusion.2, bf16[768,768]{1,0:T(8,128)(2,1)S(1)} %copy-done.14), kind=kOutput, calls=%fused_computation.116 | convolution fusion | flops 1811939328 | bytes 8257536 | tf_op jit(solution)/shard_map/dot_general | solution.py:157
  220.4 0.8 add_convert_fusion
  221.2 0.2 copy.71
  221.5 38.3 %all_to_all.16 = bf16[16,2,48,768]{3,2,1,0:T(8,128)(2,1)S(1)} all-to-all(bf16[16,2,48,768]{3,2,1,0:T(8,128)(2,1)S(1)} %bitcast.68), channel_id=1, replica_groups=mesh['hz'=2,'hy'=4,'hx'=4,'wz'=4,'wc'=2] {'hy','hx'}, dimensions={0} | all-to-all | bytes 4718592 | tf_op jit(solution)/shard_map/all_to_all | solution.py:59
  259.8 1.0 reduce_sum.61
  260.8 5.1 %all-to-all-start.2 = ((bf16[2,48,768]{2,1,0:T(8,128)(2,1)}), bf16[2,48,768]{2,1,0:T(8,128)(2,1)S(1)}, u32[]{:S(2)}, u32[]{:S(2)}) async-start(bf16[2,48,768]{2,1,0:T(8,128)(2,1)} %reduce_sum.61), calls=%async_computation.2 | async-start | bytes 294912 | tf_op jit(solution)/shard_map/all_to_all | solution.py:61
  265.9 1.1 constant_dynamic-slice_fusion
  267.0 0.7 copy.56
  267.7 1.0 constant_dynamic-slice_fusion.1
  268.7 0.7 copy.55
  269.5 4.9 %all-to-all-done.2 = bf16[2,48,768]{2,1,0:T(8,128)(2,1)S(1)} async-done(((bf16[2,48,768]{2,1,0:T(8,128)(2,1)}), bf16[2,48,768]{2,1,0:T(8,128)(2,1)S(1)}, u32[]{:S(2)}, u32[]{:S(2)}) %all-to-all-start.2) | async-done | bytes 147488 | tf_op jit(solution)/shard_map/all_to_all | solution.py:61
  274.4 1.5 fusion.39
  (58 shorter events, 1.5 us)
Async XLA Ops:
  7.2 64.5 %copy-start = (bf16[768,768]{1,0:T(8,128)(2,1)S(1)}, bf16[768,768]{1,0:T(8,128)(2,1)}, u32[]{:S(2)}) copy-start(bf16[768,768]{1,0:T(8,128)(2,1)} %param.24) | copy-start | bytes 3538948
  7.2 172.9 %all-reduce.2.cloned.1.call-start = ((), (), s32[]{:S(2)}) async-start(), calls=%async_computation.3 | async-start | bytes 8257536 | tf_op jit(solution)/shard_map/psum | solution.py:105
  7.2 20.0 %collective-permute-start = (bf16[48,768]{1,0:T(8,128)(2,1)}, bf16[48,768]{1,0:T(8,128)(2,1)S(1)}, u32[]{:S(2)}, u32[]{:S(2)}) collective-permute-start(bf16[48,768]{1,0:T(8,128)(2,1)} %param.14), channel_id=1, source_target_pairs={{0,128},{128,0},{1,129},{129,1},{2,130},{130,2},{3,131},{131,3},{4... | collective-permute-start | bytes 221192 | tf_op jit(solution)/shard_map/ppermute | solution.py:84
  68.2 0.7 copy-start.6
  68.2 0.7 copy-start.7
  68.2 0.7 copy-start.8
  68.2 0.7 copy-start.9
  68.9 1.2 copy-start.15
  73.8 2.3 copy-start.5
  73.8 106.3 %copy-start.10 = (f32[576]{0:T(1024)S(1)}, f32[576]{0:T(1024)}, u32[]{:S(2)}) copy-start(f32[576]{0:T(1024)} %param.21) | copy-start | bytes 6916
  76.0 107.8 %copy-start.13 = (f32[768]{0:T(1024)S(1)}, f32[768]{0:T(1024)}, u32[]{:S(2)}) copy-start(f32[768]{0:T(1024)} %param.25) | copy-start | bytes 9220
  180.1 3.8 %copy-start.2 = (bf16[1536,1344]{0,1:T(8,128)(2,1)S(1)}, bf16[1536,1344]{0,1:T(8,128)(2,1)}, u32[]{:S(2)}) copy-start(bf16[1536,1344]{0,1:T(8,128)(2,1)} %all-reduce.2.cloned.1.call-done) | copy-start | bytes 12386308
  182.0 1.8 copy-start.1
  196.3 0.8 copy-start.3
  198.0 18.6 %copy-start.14 = (bf16[768,768]{1,0:T(8,128)(2,1)S(1)}, bf16[768,768]{1,0:T(8,128)(2,1)}, u32[]{:S(2)}) copy-start(bf16[768,768]{1,0:T(8,128)(2,1)} %param.26) | copy-start | bytes 3538948
  216.6 3.8 %copy-start.4 = (bf16[192,768]{1,0:T(8,128)(2,1)S(1)}, bf16[192,768]{1,0:T(8,128)(2,1)}, u32[]{:S(2)}) copy-start(bf16[192,768]{1,0:T(8,128)(2,1)} %param.22) | copy-start | bytes 884740
  221.4 52.9 %copy-start.11 = (f32[768]{0:T(1024)S(1)}, f32[768]{0:T(1024)}, u32[]{:S(2)}) copy-start(f32[768]{0:T(1024)} %param.27) | copy-start | bytes 9220
  221.5 52.9 %copy-start.12 = (f32[768]{0:T(1024)S(1)}, f32[768]{0:T(1024)}, u32[]{:S(2)}) copy-start(f32[768]{0:T(1024)} %param.23) | copy-start | bytes 9220
  260.8 13.6 %all-to-all-start.2 = ((bf16[2,48,768]{2,1,0:T(8,128)(2,1)}), bf16[2,48,768]{2,1,0:T(8,128)(2,1)S(1)}, u32[]{:S(2)}, u32[]{:S(2)}) async-start(bf16[2,48,768]{2,1,0:T(8,128)(2,1)} %reduce_sum.61), calls=%async_computation.2 | async-start | bytes 294912 | tf_op jit(solution)/shard_map/all_to_all | solution.py:61
Sparse Core Ops, SparseCore 0:
  76.2 103.8 all-reduce.1

commit v9 on v8

--- a/solution.py
+++ b/solution.py
@@ -83,16 +83,19 @@
     z = lax.axis_index("hz")
     swaps = [lax.ppermute(states, "hz", [(i, (i + k) % nz) for i in range(nz)]) for k in range(1, nz)]
     local = jnp.stack([jnp.sum(floats, -1), jnp.sum(floats * floats, -1)])
-    every = lax.all_gather(local, ("hz",) + WIDTH, axis=0, tiled=False)
-    stats = jnp.sum(every.reshape(nz, -1, 2, local.shape[1]), 1)
+    every = lax.all_gather(local, HEADS + WIDTH, axis=0, tiled=False)
+    heads_total = every.shape[0] // lax.axis_size(WIDTH)
+    stats = jnp.sum(every.reshape(heads_total, -1, 2, local.shape[1]), 1)
+    stats = stats.transpose(1, 0, 2).reshape(2, -1)
     pair = jnp.stack([states] + swaps)
-    by_z = jnp.take(pair, (z - jnp.arange(nz)) % nz, axis=0).astype(jnp.float32)
-    row_mean = (stats[:, 0] / D)[..., None]
-    row_var = (stats[:, 1] / D)[..., None] - row_mean * row_mean
-    normed = ((by_z - row_mean) * lax.rsqrt(row_var + norm_epsilon)).astype(jnp.bfloat16)
+    by_z = jnp.take(pair, (z - jnp.arange(nz)) % nz, axis=0)
     qkv_cols = qkv_weight.shape[1]
     heads_dev = qkv_cols // (3 * HD)
-    block_f = gather_heads(normed.reshape(-1, normed.shape[2])).astype(jnp.float32)
+    raw_rows = gather_heads(by_z.reshape(-1, by_z.shape[2])).astype(jnp.float32)
+    row_mean = (stats[0] / D)[:, None]
+    row_var = (stats[1] / D)[:, None] - row_mean * row_mean
+    normed = ((raw_rows - row_mean) * lax.rsqrt(row_var + norm_epsilon)).astype(jnp.bfloat16)
+    block_f = normed.astype(jnp.float32)
     attn_in = (block_f * attn_gain + attn_shift).astype(jnp.bfloat16)
     mlp_in = (block_f * mlp_gain + mlp_shift).astype(jnp.bfloat16)
     projected = jnp.concatenate(

time: 286 us -> 594 us (2.08)
  blocking collectives: 107 us -> 393 us
  waiting for transfers between devices: 107 us -> 116 us
  starting transfers between devices: 9.71 us -> 16.8 us
    all_gather x1, blocking collectives: 13.9 us -> 339 us  [on_device(): every = lax.all_gather(local, HEADS + WIDTH, axis=0, tiled=False)]
    all_to_all x1 -> x0, blocking collectives: 38.6 us -> none  [gather_heads(): block = lax.all_to_all(spread, ('hy', 'hx'), 0, 0, tiled=False)]
    all_to_all x0 -> x1, starting transfers between devices: none -> 7.03 us  [gather_heads(): block = lax.all_to_all(spread, ('hy', 'hx'), 0, 0, tiled=False)]
    psum x1, waiting for transfers between devices: 102 us -> 108 us  [on_device(): summed_proj = lax.psum(projected.astype(jnp.bfloat16), WIDTH)]
  transfers between devices with their start and end apart: 3 -> 4, of which waited for: 2 -> 3; matrix products, arithmetic and copies ran while one was open for 3% -> 2% of each run, Pallas kernels for 0% -> 0%
where the time goes in v9:
time: 594 us; the launch traced here: 591 us
  blocking collectives  393 us (66%)
  waiting for transfers between devices  116 us (20%)
  other arithmetic  25.9 us (4%)
  starting transfers between devices  16.8 us (3%)
  between operations  14.4 us (2%)
  local copies, waits for them, and re-layouts  13.1 us (2%)
  matrix products  11.3 us (2%)
    all_gather x1, blocking collectives, on_device(): every = lax.all_gather(local, HEADS + WIDTH, axis=0, tiled=False)  339 us
    psum x1, waiting for transfers between devices, on_device(): summed_proj = lax.psum(projected.astype(jnp.bfloat16), WIDTH)  108 us
    all_to_all x1, blocking collectives, reduce_heads(): part = lax.all_to_all(part, ('hy', 'hx'), 0, 0, tiled=False)  38.3 us
    all_gather x1, blocking collectives, on_device(): lax.all_gather(attended, WIDTH, axis=0, tiled=True)  15.6 us
    convert_element_type x1, other arithmetic, on_device(): jax.nn.gelu(summed_proj[:, qkv_cols:].astype(jnp.float32) + up_bias, appr...  12.1 us
  transfers between devices with their start and end apart: 4, of which 3 were waited for; matrix products, arithmetic and copies ran while one was open for 2% of the time, Pallas kernels for 0%

profile of v9, /device:TPU:96, one launch (start us, length us, event | category | flops | bytes accessed | tf_op | source)
XLA Modules:
  0.0 590.8 jit_solution(8561434616024383900)
XLA Ops:
  7.2 4.6 collective-permute-start
  12.0 3.8 collective-permute-done
  15.7 0.9 pad_maximum_fusion.2
  16.6 0.6 gather_fusion
  17.3 1.6 broadcast_in_dim.45
  18.9 7.0 %all-to-all-start = ((bf16[16,96,768]{2,1,0:T(8,128)(2,1)}), bf16[16,96,768]{2,1,0:T(8,128)(2,1)S(1)}, u32[]{:S(2)}, u32[]{:S(2)}) async-start(bf16[16,96,768]{2,1,0:T(8,128)(2,1)} %broadcast_in_dim.45), calls=%async_computation | async-start | bytes 4718592 | tf_op jit(solution)/shard_map/all_to_all | solution.py:48
  26.0 1.0 convert_reduce_fusion.1
  27.1 338.9 %all-gather.1 = f32[256,2,48]{2,1,0:T(2,128)S(1)} all-gather(f32[1,2,48]{2,1,0:T(2,128)S(1)} %maximum_bitcast_fusion), channel_id=2, replica_groups=mesh['hz'=2,'hy'=4,'hx'=4,'wz'=4,'wc'=2] {'hz','hy','hx','wz','wc'}, dimensions={0}, use_global_device_ids=true | all-gather | bytes 98688 | tf_op jit(solution)/shard_map/all_gather | solution.py:86
  366.1 0.7 fusion.54
  366.8 0.8 div.30
  367.6 1.4 div.32
  369.0 0.7 add_rsqrt_fusion
  369.7 0.6 convert_bitcast_fusion
  370.3 0.4 copy.47
  370.7 0.5 fusion.8
  371.2 0.6 copy-done.10
  371.9 1.6 convolution_convert_fusion.1
  373.5 2.1 convolution_convert_fusion
  375.6 2.2 pad_maximum_fusion
  378.1 0.3 reduce-window.9
  378.5 0.1 slice_reduce_fusion
  378.7 0.2 multiply_cosine_fusion.1
  379.1 0.4 multiply_cosine_fusion
  379.6 0.5 fusion.32
  380.0 107.7 %all-reduce.2.cloned.1.call-done = bf16[1536,1344]{0,1:T(8,128)(2,1)} async-done(((bf16[1536,1344]{0,1:T(8,128)(2,1)}), bf16[1536,1344]{0,1:T(8,128)(2,1)}) %all-reduce.2.cloned.1.call-update) | async-done | bytes 4128784 | tf_op jit(solution)/shard_map/psum | solution.py:108
  487.8 1.9 convert_add_fusion.1
  489.7 0.1 constant_dynamic-slice_fusion.2
  489.8 1.7 copy-done.1
  491.6 12.1 %fusion.6 = bf16[1536,768]{0,1:T(8,128)(2,1)} fusion(bf16[1536,1344]{0,1:T(8,128)(2,1)S(1)} %copy-done.2, f32[768]{0:T(1024)S(1)} %copy-done.9), kind=kLoop, calls=%fused_computation.10 | loop fusion | flops 79036416 | bytes 4721664 | tf_op jit(solution)/shard_map/convert_element_type | solution.py:156
  503.7 0.1 copy.58
  504.0 0.1 subtract_convert_fusion.1
  504.2 0.8 copy-done.3
  505.1 0.8 fusion.61
  505.9 0.7 fusion.26
  506.6 2.0 fusion.40
  508.7 15.6 %all_gather.11 = bf16[1536,192]{1,0:T(8,128)(2,1)S(1)} all-gather(bf16[192,192]{1,0:T(8,128)(2,1)S(1)} %copy.53), channel_id=1, replica_groups=mesh['hz'=2,'hy'=4,'hx'=4,'wz'=4,'wc'=2] {'wz','wc'}, dimensions={0}, use_global_device_ids=true | all-gather | bytes 663552 | tf_op jit(solution)/shard_map/all_gather | solution.py:152
  524.3 4.1 fusion.63
  528.4 0.8 add_convert_fusion
  529.2 0.2 copy.71
  529.5 38.3 %all_to_all.15 = bf16[16,2,48,768]{3,2,1,0:T(8,128)(2,1)S(1)} all-to-all(bf16[16,2,48,768]{3,2,1,0:T(8,128)(2,1)S(1)} %bitcast.60), channel_id=1, replica_groups=mesh['hz'=2,'hy'=4,'hx'=4,'wz'=4,'wc'=2] {'hy','hx'}, dimensions={0} | all-to-all | bytes 4718592 | tf_op jit(solution)/shard_map/all_to_all | solution.py:59
  567.8 1.0 reduce_sum.61
  568.8 5.1 all-to-all-start.2
  573.9 1.1 constant_dynamic-slice_fusion
  575.0 0.7 copy.56
  575.7 1.0 constant_dynamic-slice_fusion.1
  576.7 0.7 copy.55
  577.5 4.9 all-to-all-done.2
  582.4 1.5 fusion.47
  (57 shorter events, 1.7 us)
Async XLA Ops:
  7.2 366.3 %copy-start = (bf16[768,768]{1,0:T(8,128)(2,1)S(1)}, bf16[768,768]{1,0:T(8,128)(2,1)}, u32[]{:S(2)}) copy-start(bf16[768,768]{1,0:T(8,128)(2,1)} %param.24) | copy-start | bytes 3538948
  7.2 8.6 %collective-permute-start = (bf16[48,768]{1,0:T(8,128)(2,1)}, bf16[48,768]{1,0:T(8,128)(2,1)S(1)}, u32[]{:S(2)}, u32[]{:S(2)}) collective-permute-start(bf16[48,768]{1,0:T(8,128)(2,1)} %param.14), channel_id=1, source_target_pairs={{0,128},{128,0},{1,129},{129,1},{2,130},{130,2},{3,131},{131,3},{4... | collective-permute-start | bytes 221192 | tf_op jit(solution)/shard_map/ppermute | solution.py:84
  18.9 350.7 %all-to-all-start = ((bf16[16,96,768]{2,1,0:T(8,128)(2,1)}), bf16[16,96,768]{2,1,0:T(8,128)(2,1)S(1)}, u32[]{:S(2)}, u32[]{:S(2)}) async-start(bf16[16,96,768]{2,1,0:T(8,128)(2,1)} %broadcast_in_dim.45), calls=%async_computation | async-start | bytes 4718592 | tf_op jit(solution)/shard_map/all_to_all | solution.py:48
  26.0 461.8 %all-reduce.2.cloned.1.call-start = ((), (), s32[]{:S(2)}) async-start(), calls=%async_computation.3 | async-start | bytes 8257536 | tf_op jit(solution)/shard_map/psum | solution.py:108
  370.7 1.2 copy-start.10
  370.7 1.2 copy-start.11
  370.7 1.2 copy-start.12
  371.8 1.6 copy-start.13
  371.9 1.6 copy-start.14
  375.6 2.3 copy-start.5
  375.6 112.2 %copy-start.6 = (f32[576]{0:T(1024)S(1)}, f32[576]{0:T(1024)}, u32[]{:S(2)}) copy-start(f32[576]{0:T(1024)} %param.21) | copy-start | bytes 6916
  377.8 113.8 %copy-start.9 = (f32[768]{0:T(1024)S(1)}, f32[768]{0:T(1024)}, u32[]{:S(2)}) copy-start(f32[768]{0:T(1024)} %param.25) | copy-start | bytes 9220
  487.8 3.8 copy-start.2
  489.7 1.8 copy-start.1
  504.2 0.8 copy-start.3
  524.3 4.1 copy-start.4
  529.5 52.9 %copy-start.7 = (f32[768]{0:T(1024)S(1)}, f32[768]{0:T(1024)}, u32[]{:S(2)}) copy-start(f32[768]{0:T(1024)} %param.27) | copy-start | bytes 9220
  529.5 52.9 %copy-start.8 = (f32[768]{0:T(1024)S(1)}, f32[768]{0:T(1024)}, u32[]{:S(2)}) copy-start(f32[768]{0:T(1024)} %param.23) | copy-start | bytes 9220
  568.8 13.6 %all-to-all-start.2 = ((bf16[2,48,768]{2,1,0:T(8,128)(2,1)}), bf16[2,48,768]{2,1,0:T(8,128)(2,1)S(1)}, u32[]{:S(2)}, u32[]{:S(2)}) async-start(bf16[2,48,768]{2,1,0:T(8,128)(2,1)} %reduce_sum.61), calls=%async_computation.2 | async-start | bytes 294912 | tf_op jit(solution)/shard_map/all_to_all | solution.py:61
Sparse Core Ops, SparseCore 0:
  377.9 109.8 all-reduce.1

commit v10 on v8

--- a/solution.py
+++ b/solution.py
@@ -146,7 +146,13 @@
         .astype(jnp.bfloat16)
     )
     attn_part = jnp.dot(
-        lax.all_gather(attended, WIDTH, axis=0, tiled=True),
+        lax.all_to_all(
+            jnp.broadcast_to(attended[None], (lax.axis_size(WIDTH),) + attended.shape),
+            WIDTH,
+            0,
+            0,
+            tiled=False,
+        ).reshape(-1, attended.shape[1]),
         dense_weight,
         preferred_element_type=jnp.float32,
     )

time: 286 us -> 282 us (0.986)
  blocking collectives: 107 us -> 90.6 us
  starting transfers between devices: 9.71 us -> 16.1 us
    all_gather x1 -> x0, blocking collectives: 15.8 us -> none  [on_device(): lax.all_gather(attended, WIDTH, axis=0, tiled=True)]
    all_to_all x0 -> x1, starting transfers between devices: none -> 6.41 us  [on_device(): lax.all_to_all(jnp.broadcast_to(attended[None], (lax.axis_size(WIDTH),) +...]
  transfers between devices with their start and end apart: 3 -> 4, of which waited for: 2 -> 3; matrix products, arithmetic and copies ran while one was open for 3% -> 8% of each run, Pallas kernels for 0% -> 0%
where the time goes in v10:
time: 282 us; the launch traced here: 279 us
  waiting for transfers between devices  109 us (39%)
  blocking collectives  90.6 us (32%)
  other arithmetic  25 us (9%)
  starting transfers between devices  16.1 us (6%)
  between operations  14.4 us (5%)
  matrix products  13.7 us (5%)
  local copies, waits for them, and re-layouts  10.4 us (4%)
    psum x1, waiting for transfers between devices, on_device(): summed_proj = lax.psum(projected.astype(jnp.bfloat16), WIDTH)  102 us
    all_to_all x1, blocking collectives, gather_heads(): block = lax.all_to_all(spread, ('hy', 'hx'), 0, 0, tiled=False)  38.6 us
    all_to_all x1, blocking collectives, reduce_heads(): part = lax.all_to_all(part, ('hy', 'hx'), 0, 0, tiled=False)  38 us
    all_gather x1, blocking collectives, on_device(): every = lax.all_gather(local, ('hz',) + WIDTH, axis=0, tiled=False)  13.9 us
    convert_element_type x1, other arithmetic, on_device(): jax.nn.gelu(summed_proj[:, qkv_cols:].astype(jnp.float32) + up_bias, appr...  12.1 us
    all_to_all x1, starting transfers between devices, on_device(): lax.all_to_all(jnp.broadcast_to(attended[None], (lax.axis_size(WIDTH),) +...  6.41 us
  transfers between devices with their start and end apart: 4, of which 3 were waited for; matrix products, arithmetic and copies ran while one was open for 8% of the time, Pallas kernels for 0%

profile of v10, /device:TPU:96, one launch (start us, length us, event | category | flops | bytes accessed | tf_op | source)
XLA Modules:
  0.0 279.0 jit_solution(4430219106729832107)
XLA Ops:
  7.2 4.6 %collective-permute-start = (bf16[48,768]{1,0:T(8,128)(2,1)}, bf16[48,768]{1,0:T(8,128)(2,1)S(1)}, u32[]{:S(2)}, u32[]{:S(2)}) collective-permute-start(bf16[48,768]{1,0:T(8,128)(2,1)} %param.14), channel_id=1, source_target_pairs={{0,128},{128,0},{1,129},{129,1},{2,130},{130,2},{3,131},{131,3},{4... | collective-permute-start | bytes 221192 | tf_op jit(solution)/shard_map/ppermute | solution.py:84
  11.8 1.0 convert_reduce_fusion.1
  13.0 13.9 %all-gather.1 = f32[16,2,48]{2,1,0:T(2,128)S(1)} all-gather(f32[1,2,48]{2,1,0:T(2,128)S(1)} %maximum_bitcast_fusion), channel_id=2, replica_groups=mesh['hz'=2,'hy'=4,'hx'=4,'wz'=4,'wc'=2] {'hz','wz','wc'}, dimensions={0}, use_global_device_ids=true | all-gather | bytes 6528 | tf_op jit(solution)/shard_map/all_gather | solution.py:86
  27.2 0.9 pad_maximum_fusion.2
  28.1 0.6 gather_fusion
  28.7 0.1 multiply_convert_fusion
  28.8 0.2 broadcast_in_dim.47
  29.0 38.6 %all_to_all.20 = bf16[16,96,768]{2,1,0:T(8,128)(2,1)S(1)} all-to-all(bf16[16,96,768]{2,1,0:T(8,128)(2,1)S(1)} %broadcast_in_dim.47), channel_id=1, replica_groups=mesh['hz'=2,'hy'=4,'hx'=4,'wz'=4,'wc'=2] {'hy','hx'}, dimensions={0} | all-to-all | bytes 4718592 | tf_op jit(solution)/shard_map/all_to_all | solution.py:48
  67.6 0.6 convert_bitcast_fusion
  68.2 0.4 copy.50
  68.7 0.2 copy-done.5
  68.9 1.1 fusion.4
  70.1 1.6 convolution_convert_fusion.1
  71.7 2.1 convolution_convert_fusion
  73.8 2.2 pad_maximum_fusion
  76.3 0.3 reduce-window.9
  76.7 0.1 slice_reduce_fusion
  77.0 0.2 multiply_cosine_fusion.1
  77.1 0.1 copy.52
  77.2 0.1 copy.53
  77.4 0.4 multiply_cosine_fusion
  77.8 0.5 fusion.24
  78.3 101.8 %all-reduce.2.cloned.1.call-done = bf16[1536,1344]{0,1:T(8,128)(2,1)} async-done(((bf16[1536,1344]{0,1:T(8,128)(2,1)}), bf16[1536,1344]{0,1:T(8,128)(2,1)}) %all-reduce.2.cloned.1.call-update) | async-done | bytes 4128784 | tf_op jit(solution)/shard_map/psum | solution.py:105
  180.1 1.8 convert_add_fusion.1
  181.9 0.1 constant_dynamic-slice_fusion.2
  182.0 1.6 copy-done.1
  183.7 0.1 copy.61
  184.0 0.1 subtract_convert_fusion.1
  184.2 0.9 copy-done.2
  185.1 0.8 fusion.53
  185.9 0.7 fusion.18
  186.7 2.0 fusion.32
  188.7 1.0 broadcast_in_dim.86
  189.7 6.4 %all-to-all-start.1 = ((bf16[8,192,192]{2,1,0:T(8,128)(2,1)}), bf16[8,192,192]{2,1,0:T(8,128)(2,1)S(1)}, u32[]{:S(2)}, u32[]{:S(2)}) async-start(bf16[8,192,192]{2,1,0:T(8,128)(2,1)} %broadcast_in_dim.86), calls=%async_computation.1 | async-start | bytes 1572864 | tf_op jit(solution)/shard_map/all_to_all | solution.py:149
  196.2 12.1 %fusion.2 = bf16[1536,768]{0,1:T(8,128)(2,1)S(1)} fusion(bf16[1536,1344]{0,1:T(8,128)(2,1)} %all-reduce.2.cloned.1.call-done, f32[768]{0:T(1024)S(1)} %copy-done.12), kind=kLoop, calls=%fused_computation.4 | loop fusion | flops 79036416 | bytes 4721664 | tf_op jit(solution)/shard_map/convert_element_type | solution.py:159
  208.3 4.2 %fusion.55 = f32[1536,768]{1,0:T(8,128)} fusion(bf16[1536,768]{0,1:T(8,128)(2,1)S(1)} %fusion.2, bf16[768,768]{1,0:T(8,128)(2,1)S(1)} %copy-done.13), kind=kOutput, calls=%fused_computation.116 | convolution fusion | flops 1811939328 | bytes 8257536 | tf_op jit(solution)/shard_map/dot_general | solution.py:163
  212.5 2.0 all-to-all-done.1
  214.5 3.1 %add_convert_fusion = bf16[1536,768]{1,0:T(8,128)(2,1)S(1)} fusion(f32[1536,768]{1,0:T(8,128)} %fusion.55, bf16[1536,192]{1,0:T(8,128)(2,1)S(1)} %bitcast.75, bf16[192,768]{1,0:T(8,128)(2,1)S(1)} %copy-done.3), kind=kOutput, calls=%fused_computation.12 | convolution fusion | flops 455344128 | bytes 7962624 | tf_op jit(solution)/shard_map/dot_general | solution.py:148
  217.6 0.2 copy.74
  217.9 38.0 %all_to_all.21 = bf16[16,2,48,768]{3,2,1,0:T(8,128)(2,1)S(1)} all-to-all(bf16[16,2,48,768]{3,2,1,0:T(8,128)(2,1)S(1)} %bitcast.69), channel_id=1, replica_groups=mesh['hz'=2,'hy'=4,'hx'=4,'wz'=4,'wc'=2] {'hy','hx'}, dimensions={0} | all-to-all | bytes 4718592 | tf_op jit(solution)/shard_map/all_to_all | solution.py:59
  256.0 1.0 reduce_sum.61
  257.0 5.1 %all-to-all-start.3 = ((bf16[2,48,768]{2,1,0:T(8,128)(2,1)}), bf16[2,48,768]{2,1,0:T(8,128)(2,1)S(1)}, u32[]{:S(2)}, u32[]{:S(2)}) async-start(bf16[2,48,768]{2,1,0:T(8,128)(2,1)} %reduce_sum.61), calls=%async_computation.3 | async-start | bytes 294912 | tf_op jit(solution)/shard_map/all_to_all | solution.py:61
  262.1 1.1 constant_dynamic-slice_fusion
  263.1 0.7 copy.59
  263.9 1.0 constant_dynamic-slice_fusion.1
  264.9 0.7 copy.58
  265.6 4.9 %all-to-all-done.3 = bf16[2,48,768]{2,1,0:T(8,128)(2,1)S(1)} async-done(((bf16[2,48,768]{2,1,0:T(8,128)(2,1)}), bf16[2,48,768]{2,1,0:T(8,128)(2,1)S(1)}, u32[]{:S(2)}, u32[]{:S(2)}) %all-to-all-start.3) | async-done | bytes 147488 | tf_op jit(solution)/shard_map/all_to_all | solution.py:61
  270.6 1.5 fusion.39
  (58 shorter events, 1.7 us)
Async XLA Ops:
  7.2 64.5 %copy-start = (bf16[768,768]{1,0:T(8,128)(2,1)S(1)}, bf16[768,768]{1,0:T(8,128)(2,1)}, u32[]{:S(2)}) copy-start(bf16[768,768]{1,0:T(8,128)(2,1)} %param.24) | copy-start | bytes 3538948
  7.2 172.9 %all-reduce.2.cloned.1.call-start = ((), (), s32[]{:S(2)}) async-start(), calls=%async_computation.4 | async-start | bytes 8257536 | tf_op jit(solution)/shard_map/psum | solution.py:105
  7.2 20.0 %collective-permute-start = (bf16[48,768]{1,0:T(8,128)(2,1)}, bf16[48,768]{1,0:T(8,128)(2,1)S(1)}, u32[]{:S(2)}, u32[]{:S(2)}) collective-permute-start(bf16[48,768]{1,0:T(8,128)(2,1)} %param.14), channel_id=1, source_target_pairs={{0,128},{128,0},{1,129},{129,1},{2,130},{130,2},{3,131},{131,3},{4... | collective-permute-start | bytes 221192 | tf_op jit(solution)/shard_map/ppermute | solution.py:84
  68.2 0.7 copy-start.5
  68.2 0.7 copy-start.6
  68.2 0.7 copy-start.7
  68.2 0.7 copy-start.8
  68.9 1.2 copy-start.14
  73.8 2.3 copy-start.4
  73.8 106.3 %copy-start.9 = (f32[576]{0:T(1024)S(1)}, f32[576]{0:T(1024)}, u32[]{:S(2)}) copy-start(f32[576]{0:T(1024)} %param.21) | copy-start | bytes 6916
  181.8 1.8 copy-start.1
  184.2 0.9 copy-start.2
  185.9 10.2 %copy-start.12 = (f32[768]{0:T(1024)S(1)}, f32[768]{0:T(1024)}, u32[]{:S(2)}) copy-start(f32[768]{0:T(1024)} %param.25) | copy-start | bytes 9220
  188.6 19.7 %copy-start.13 = (bf16[768,768]{1,0:T(8,128)(2,1)S(1)}, bf16[768,768]{1,0:T(8,128)(2,1)}, u32[]{:S(2)}) copy-start(bf16[768,768]{1,0:T(8,128)(2,1)} %param.26) | copy-start | bytes 3538948
  189.7 24.8 %all-to-all-start.1 = ((bf16[8,192,192]{2,1,0:T(8,128)(2,1)}), bf16[8,192,192]{2,1,0:T(8,128)(2,1)S(1)}, u32[]{:S(2)}, u32[]{:S(2)}) async-start(bf16[8,192,192]{2,1,0:T(8,128)(2,1)} %broadcast_in_dim.86), calls=%async_computation.1 | async-start | bytes 1572864 | tf_op jit(solution)/shard_map/all_to_all | solution.py:149
  208.3 6.2 %copy-start.3 = (bf16[192,768]{1,0:T(8,128)(2,1)S(1)}, bf16[192,768]{1,0:T(8,128)(2,1)}, u32[]{:S(2)}) copy-start(bf16[192,768]{1,0:T(8,128)(2,1)} %param.22) | copy-start | bytes 884740
  217.9 52.7 %copy-start.10 = (f32[768]{0:T(1024)S(1)}, f32[768]{0:T(1024)}, u32[]{:S(2)}) copy-start(f32[768]{0:T(1024)} %param.27) | copy-start | bytes 9220
  217.9 52.6 %copy-start.11 = (f32[768]{0:T(1024)S(1)}, f32[768]{0:T(1024)}, u32[]{:S(2)}) copy-start(f32[768]{0:T(1024)} %param.23) | copy-start | bytes 9220
  257.0 13.5 %all-to-all-start.3 = ((bf16[2,48,768]{2,1,0:T(8,128)(2,1)}), bf16[2,48,768]{2,1,0:T(8,128)(2,1)S(1)}, u32[]{:S(2)}, u32[]{:S(2)}) async-start(bf16[2,48,768]{2,1,0:T(8,128)(2,1)} %reduce_sum.61), calls=%async_computation.3 | async-start | bytes 294912 | tf_op jit(solution)/shard_map/all_to_all | solution.py:61
Sparse Core Ops, SparseCore 0:
  76.2 103.8 all-reduce.1

commit v11 on v10

--- a/solution.py
+++ b/solution.py
@@ -83,7 +83,10 @@
     z = lax.axis_index("hz")
     swaps = [lax.ppermute(states, "hz", [(i, (i + k) % nz) for i in range(nz)]) for k in range(1, nz)]
     local = jnp.stack([jnp.sum(floats, -1), jnp.sum(floats * floats, -1)])
-    every = lax.all_gather(local, ("hz",) + WIDTH, axis=0, tiled=False)
+    group = nz * lax.axis_size(WIDTH)
+    every = lax.all_to_all(
+        jnp.broadcast_to(local[None], (group,) + local.shape), ("hz",) + WIDTH, 0, 0, tiled=False
+    )
     stats = jnp.sum(every.reshape(nz, -1, 2, local.shape[1]), 1)
     pair = jnp.stack([states] + swaps)
     by_z = jnp.take(pair, (z - jnp.arange(nz)) % nz, axis=0).astype(jnp.float32)

time: 282 us -> 275 us (0.975)
  blocking collectives: 90.6 us -> 76.3 us
  starting transfers between devices: 16.1 us -> 21.3 us
    all_gather x1 -> x0, blocking collectives: 13.9 us -> none  [on_device(): every = lax.all_gather(local, ('hz',) + WIDTH, axis=0, tiled=False)]
    all_to_all x0 -> x1, starting transfers between devices: none -> 5.21 us  [on_device(): lax.all_to_all(jnp.broadcast_to(local[None], (group,) + local.shape), ('h...]
    all_to_all x0 -> x1, waiting for transfers between devices: none -> 4.26 us  [on_device(): lax.all_to_all(jnp.broadcast_to(local[None], (group,) + local.shape), ('h...]
    psum x1, waiting for transfers between devices: 102 us -> 98.9 us  [on_device(): summed_proj = lax.psum(projected.astype(jnp.bfloat16), WIDTH)]
  transfers between devices with their start and end apart: 4 -> 5, of which waited for: 3 -> 4; matrix products, arithmetic and copies ran while one was open for 8% -> 9% of each run, Pallas kernels for 0% -> 0%
where the time goes in v11:
time: 275 us; the launch traced here: 272 us
  waiting for transfers between devices  110 us (40%)
  blocking collectives  76.3 us (28%)
  other arithmetic  25.1 us (9%)
  starting transfers between devices  21.3 us (8%)
  between operations  14.4 us (5%)
  matrix products  13.7 us (5%)
  local copies, waits for them, and re-layouts  11 us (4%)
    psum x1, waiting for transfers between devices, on_device(): summed_proj = lax.psum(projected.astype(jnp.bfloat16), WIDTH)  98.9 us
    all_to_all x1, blocking collectives, gather_heads(): block = lax.all_to_all(spread, ('hy', 'hx'), 0, 0, tiled=False)  38.3 us
    all_to_all x1, blocking collectives, reduce_heads(): part = lax.all_to_all(part, ('hy', 'hx'), 0, 0, tiled=False)  38 us
    convert_element_type x1, other arithmetic, on_device(): jax.nn.gelu(summed_proj[:, qkv_cols:].astype(jnp.float32) + up_bias, appr...  12.1 us
    all_to_all x1, starting transfers between devices, on_device(): lax.all_to_all(jnp.broadcast_to(attended[None], (lax.axis_size(WIDTH),) +...  6.42 us
  transfers between devices with their start and end apart: 5, of which 4 were waited for; matrix products, arithmetic and copies ran while one was open for 9% of the time, Pallas kernels for 0%

profile of v11, /device:TPU:96, one launch (start us, length us, event | category | flops | bytes accessed | tf_op | source)
XLA Modules:
  0.0 271.9 jit_solution(16590568960911276245)
XLA Ops:
  7.2 4.6 %collective-permute-start = (bf16[48,768]{1,0:T(8,128)(2,1)}, bf16[48,768]{1,0:T(8,128)(2,1)S(1)}, u32[]{:S(2)}, u32[]{:S(2)}) collective-permute-start(bf16[48,768]{1,0:T(8,128)(2,1)} %param.14), channel_id=1, source_target_pairs={{0,128},{128,0},{1,129},{129,1},{2,130},{130,2},{3,131},{131,3},{4... | collective-permute-start | bytes 221192 | tf_op jit(solution)/shard_map/ppermute | solution.py:84
  11.8 1.0 convert_reduce_fusion.1
  12.8 0.6 broadcast_in_dim.49
  13.4 5.2 %all-to-all-start = ((f32[16,2,48]{2,1,0:T(2,128)}), f32[16,2,48]{2,1,0:T(2,128)S(1)}, u32[]{:S(2)}, u32[]{:S(2)}) async-start(f32[16,2,48]{2,1,0:T(2,128)} %broadcast_in_dim.49), calls=%async_computation | async-start | bytes 32768 | tf_op jit(solution)/shard_map/all_to_all | solution.py:87
  18.9 4.3 %all-to-all-done = f32[16,2,48]{2,1,0:T(2,128)S(1)} async-done(((f32[16,2,48]{2,1,0:T(2,128)}), f32[16,2,48]{2,1,0:T(2,128)S(1)}, u32[]{:S(2)}, u32[]{:S(2)}) %all-to-all-start) | async-done | bytes 6176 | tf_op jit(solution)/shard_map/all_to_all | solution.py:87
  23.4 0.9 pad_maximum_fusion.2
  24.3 0.6 gather_fusion
  24.9 0.1 multiply_convert_fusion
  25.0 0.2 broadcast_in_dim.50
  25.2 38.3 %all_to_all.25 = bf16[16,96,768]{2,1,0:T(8,128)(2,1)S(1)} all-to-all(bf16[16,96,768]{2,1,0:T(8,128)(2,1)S(1)} %broadcast_in_dim.50), channel_id=1, replica_groups=mesh['hz'=2,'hy'=4,'hx'=4,'wz'=4,'wc'=2] {'hy','hx'}, dimensions={0} | all-to-all | bytes 4718592 | tf_op jit(solution)/shard_map/all_to_all | solution.py:48
  63.5 0.6 convert_bitcast_fusion
  64.2 0.4 copy.71
  64.6 0.2 copy-done.5
  64.9 1.1 fusion.4
  66.0 1.6 convolution_convert_fusion.1
  67.6 2.1 convolution_convert_fusion
  69.7 2.2 pad_maximum_fusion
  72.2 0.3 reduce-window.9
  72.6 0.1 slice_reduce_fusion
  72.9 0.2 multiply_cosine_fusion.1
  73.3 0.4 multiply_cosine_fusion
  73.7 0.5 fusion.24
  74.2 98.9 %all-reduce.2.cloned.1.call-done = bf16[1536,1344]{0,1:T(8,128)(2,1)} async-done(((bf16[1536,1344]{0,1:T(8,128)(2,1)}), bf16[1536,1344]{0,1:T(8,128)(2,1)}) %all-reduce.2.cloned.1.call-update) | async-done | bytes 4128784 | tf_op jit(solution)/shard_map/psum | solution.py:108
  173.0 1.8 convert_add_fusion.1
  174.8 0.1 constant_dynamic-slice_fusion.2
  175.0 1.6 copy-done.1
  176.7 0.1 copy.87
  177.0 0.1 subtract_convert_fusion.1
  177.2 0.9 copy-done.2
  178.1 0.8 fusion.53
  178.9 0.7 fusion.18
  179.6 2.0 fusion.32
  181.7 1.0 broadcast_in_dim.93
  182.7 6.4 %all-to-all-start.2 = ((bf16[8,192,192]{2,1,0:T(8,128)(2,1)}), bf16[8,192,192]{2,1,0:T(8,128)(2,1)S(1)}, u32[]{:S(2)}, u32[]{:S(2)}) async-start(bf16[8,192,192]{2,1,0:T(8,128)(2,1)} %broadcast_in_dim.93), calls=%async_computation.2 | async-start | bytes 1572864 | tf_op jit(solution)/shard_map/all_to_all | solution.py:152
  189.1 12.1 %fusion.2 = bf16[1536,768]{0,1:T(8,128)(2,1)S(1)} fusion(bf16[1536,1344]{0,1:T(8,128)(2,1)} %all-reduce.2.cloned.1.call-done, f32[768]{0:T(1024)S(1)} %copy-done.12), kind=kLoop, calls=%fused_computation.4 | loop fusion | flops 79036416 | bytes 4721664 | tf_op jit(solution)/shard_map/convert_element_type | solution.py:162
  201.3 4.2 %fusion.55 = f32[1536,768]{1,0:T(8,128)} fusion(bf16[1536,768]{0,1:T(8,128)(2,1)S(1)} %fusion.2, bf16[768,768]{1,0:T(8,128)(2,1)S(1)} %copy-done.13), kind=kOutput, calls=%fused_computation.116 | convolution fusion | flops 1811939328 | bytes 8257536 | tf_op jit(solution)/shard_map/dot_general | solution.py:166
  205.5 2.0 all-to-all-done.2
  207.5 3.1 %add_convert_fusion = bf16[1536,768]{1,0:T(8,128)(2,1)S(1)} fusion(f32[1536,768]{1,0:T(8,128)} %fusion.55, bf16[1536,192]{1,0:T(8,128)(2,1)S(1)} %bitcast.73, bf16[192,768]{1,0:T(8,128)(2,1)S(1)} %copy-done.3), kind=kOutput, calls=%fused_computation.12 | convolution fusion | flops 455344128 | bytes 7962624 | tf_op jit(solution)/shard_map/dot_general | solution.py:151
  210.6 0.2 copy.100
  210.9 38.0 %all_to_all.26 = bf16[16,2,48,768]{3,2,1,0:T(8,128)(2,1)S(1)} all-to-all(bf16[16,2,48,768]{3,2,1,0:T(8,128)(2,1)S(1)} %bitcast.67), channel_id=1, replica_groups=mesh['hz'=2,'hy'=4,'hx'=4,'wz'=4,'wc'=2] {'hy','hx'}, dimensions={0} | all-to-all | bytes 4718592 | tf_op jit(solution)/shard_map/all_to_all | solution.py:59
  248.9 1.0 reduce_sum.61
  250.0 5.1 %all-to-all-start.4 = ((bf16[2,48,768]{2,1,0:T(8,128)(2,1)}), bf16[2,48,768]{2,1,0:T(8,128)(2,1)S(1)}, u32[]{:S(2)}, u32[]{:S(2)}) async-start(bf16[2,48,768]{2,1,0:T(8,128)(2,1)} %reduce_sum.61), calls=%async_computation.4 | async-start | bytes 294912 | tf_op jit(solution)/shard_map/all_to_all | solution.py:61
  255.0 1.1 constant_dynamic-slice_fusion
  256.1 0.7 copy.80
  256.8 1.0 constant_dynamic-slice_fusion.1
  257.9 0.7 copy.79
  258.6 4.9 %all-to-all-done.4 = bf16[2,48,768]{2,1,0:T(8,128)(2,1)S(1)} async-done(((bf16[2,48,768]{2,1,0:T(8,128)(2,1)}), bf16[2,48,768]{2,1,0:T(8,128)(2,1)S(1)}, u32[]{:S(2)}, u32[]{:S(2)}) %all-to-all-start.4) | async-done | bytes 147488 | tf_op jit(solution)/shard_map/all_to_all | solution.py:61
  263.5 1.5 fusion.39
  (60 shorter events, 1.9 us)
Async XLA Ops:
  7.2 60.4 %copy-start = (bf16[768,768]{1,0:T(8,128)(2,1)S(1)}, bf16[768,768]{1,0:T(8,128)(2,1)}, u32[]{:S(2)}) copy-start(bf16[768,768]{1,0:T(8,128)(2,1)} %param.24) | copy-start | bytes 3538948
  7.2 16.2 %collective-permute-start = (bf16[48,768]{1,0:T(8,128)(2,1)}, bf16[48,768]{1,0:T(8,128)(2,1)S(1)}, u32[]{:S(2)}, u32[]{:S(2)}) collective-permute-start(bf16[48,768]{1,0:T(8,128)(2,1)} %param.14), channel_id=1, source_target_pairs={{0,128},{128,0},{1,129},{129,1},{2,130},{130,2},{3,131},{131,3},{4... | collective-permute-start | bytes 221192 | tf_op jit(solution)/shard_map/ppermute | solution.py:84
  13.4 9.7 %all-to-all-start = ((f32[16,2,48]{2,1,0:T(2,128)}), f32[16,2,48]{2,1,0:T(2,128)S(1)}, u32[]{:S(2)}, u32[]{:S(2)}) async-start(f32[16,2,48]{2,1,0:T(2,128)} %broadcast_in_dim.49), calls=%async_computation | async-start | bytes 32768 | tf_op jit(solution)/shard_map/all_to_all | solution.py:87
  18.6 154.4 %all-reduce.2.cloned.1.call-start = ((), (), s32[]{:S(2)}) async-start(), calls=%async_computation.5 | async-start | bytes 8257536 | tf_op jit(solution)/shard_map/psum | solution.py:108
  64.1 0.7 copy-start.5
  64.1 0.7 copy-start.6
  64.1 0.7 copy-start.7
  64.1 0.7 copy-start.8
  64.8 1.2 copy-start.14
  69.7 2.3 copy-start.4
  69.7 103.3 %copy-start.9 = (f32[576]{0:T(1024)S(1)}, f32[576]{0:T(1024)}, u32[]{:S(2)}) copy-start(f32[576]{0:T(1024)} %param.21) | copy-start | bytes 6916
  174.8 1.8 copy-start.1
  177.2 0.9 copy-start.2
  178.9 10.2 %copy-start.12 = (f32[768]{0:T(1024)S(1)}, f32[768]{0:T(1024)}, u32[]{:S(2)}) copy-start(f32[768]{0:T(1024)} %param.25) | copy-start | bytes 9220
  181.6 19.7 %copy-start.13 = (bf16[768,768]{1,0:T(8,128)(2,1)S(1)}, bf16[768,768]{1,0:T(8,128)(2,1)}, u32[]{:S(2)}) copy-start(bf16[768,768]{1,0:T(8,128)(2,1)} %param.26) | copy-start | bytes 3538948
  182.7 24.8 %all-to-all-start.2 = ((bf16[8,192,192]{2,1,0:T(8,128)(2,1)}), bf16[8,192,192]{2,1,0:T(8,128)(2,1)S(1)}, u32[]{:S(2)}, u32[]{:S(2)}) async-start(bf16[8,192,192]{2,1,0:T(8,128)(2,1)} %broadcast_in_dim.93), calls=%async_computation.2 | async-start | bytes 1572864 | tf_op jit(solution)/shard_map/all_to_all | solution.py:152
  201.3 6.2 %copy-start.3 = (bf16[192,768]{1,0:T(8,128)(2,1)S(1)}, bf16[192,768]{1,0:T(8,128)(2,1)}, u32[]{:S(2)}) copy-start(bf16[192,768]{1,0:T(8,128)(2,1)} %param.22) | copy-start | bytes 884740
  210.9 52.6 %copy-start.10 = (f32[768]{0:T(1024)S(1)}, f32[768]{0:T(1024)}, u32[]{:S(2)}) copy-start(f32[768]{0:T(1024)} %param.27) | copy-start | bytes 9220
  210.9 52.6 %copy-start.11 = (f32[768]{0:T(1024)S(1)}, f32[768]{0:T(1024)}, u32[]{:S(2)}) copy-start(f32[768]{0:T(1024)} %param.23) | copy-start | bytes 9220
  250.0 13.5 %all-to-all-start.4 = ((bf16[2,48,768]{2,1,0:T(8,128)(2,1)}), bf16[2,48,768]{2,1,0:T(8,128)(2,1)S(1)}, u32[]{:S(2)}, u32[]{:S(2)}) async-start(bf16[2,48,768]{2,1,0:T(8,128)(2,1)} %reduce_sum.61), calls=%async_computation.4 | async-start | bytes 294912 | tf_op jit(solution)/shard_map/all_to_all | solution.py:61
Sparse Core Ops, SparseCore 0:
  72.1 100.9 all-reduce.1

commit v12 on v8

--- a/solution.py
+++ b/solution.py
@@ -83,7 +83,10 @@
     z = lax.axis_index("hz")
     swaps = [lax.ppermute(states, "hz", [(i, (i + k) % nz) for i in range(nz)]) for k in range(1, nz)]
     local = jnp.stack([jnp.sum(floats, -1), jnp.sum(floats * floats, -1)])
-    every = lax.all_gather(local, ("hz",) + WIDTH, axis=0, tiled=False)
+    group = nz * lax.axis_size(WIDTH)
+    every = lax.all_to_all(
+        jnp.broadcast_to(local[None], (group,) + local.shape), ("hz",) + WIDTH, 0, 0, tiled=False
+    )
     stats = jnp.sum(every.reshape(nz, -1, 2, local.shape[1]), 1)
     pair = jnp.stack([states] + swaps)
     by_z = jnp.take(pair, (z - jnp.arange(nz)) % nz, axis=0).astype(jnp.float32)
@@ -145,17 +148,24 @@
         .reshape(own_rows, heads_dev * HD)
         .astype(jnp.bfloat16)
     )
-    attn_part = jnp.dot(
-        lax.all_gather(attended, WIDTH, axis=0, tiled=True),
-        dense_weight,
-        preferred_element_type=jnp.float32,
-    )
+    gathered = lax.all_to_all(
+        jnp.broadcast_to(attended[None], (lax.axis_size(WIDTH),) + attended.shape),
+        WIDTH,
+        0,
+        0,
+        tiled=False,
+    ).reshape(-1, attended.shape[1])
     hidden = jax.nn.gelu(summed_proj[:, qkv_cols:].astype(jnp.float32) + up_bias, approximate=False).astype(
         jnp.bfloat16
     )
     hidden = lax.optimization_barrier(hidden)
-    mlp_part = jnp.dot(hidden, down_weight, preferred_element_type=jnp.float32)
-    summed = reduce_heads((attn_part + mlp_part).astype(jnp.bfloat16))
+    half = dense_weight.shape[1] // 2
+    halves = []
+    for cols in (slice(0, half), slice(half, None)):
+        attn_part = jnp.dot(gathered, dense_weight[:, cols], preferred_element_type=jnp.float32)
+        mlp_part = jnp.dot(hidden, down_weight[:, cols], preferred_element_type=jnp.float32)
+        halves.append(reduce_heads((attn_part + mlp_part).astype(jnp.bfloat16)))
+    summed = jnp.concatenate(halves, axis=1)
     layer_out = (floats + summed + dense_bias + down_bias).astype(jnp.bfloat16)
     return (layer_out, key_cache, value_cache)
 

time: 286 us -> 296 us (1.035)
  blocking collectives: 107 us -> 38.3 us
  waiting for transfers between devices: 107 us -> 151 us
  starting transfers between devices: 9.71 us -> 35.1 us
  local copies, waits for them, and re-layouts: 9.4 us -> 15.2 us
  matrix products: 11 us -> 14 us
    all_to_all x0 -> x4, waiting for transfers between devices: none -> 39.1 us  [the longest x2 29.3 us: reduce_heads(): part = lax.all_to_all(part, ('hy', 'hx'), 0, 0, tiled=False)]
    all_to_all x1 -> x0, blocking collectives: 38.3 us -> none  [reduce_heads(): part = lax.all_to_all(part, ('hy', 'hx'), 0, 0, tiled=False)]
    all_gather x2 -> x0, blocking collectives: 29.8 us -> none  [the longest x1 15.8 us: on_device(): lax.all_gather(attended, WIDTH, axis=0, tiled=True)]
    all_to_all x0 -> x4, starting transfers between devices: none -> 22.1 us  [the longest x2 10.5 us: reduce_heads(): part = lax.all_to_all(part, ('hy', 'hx'), 0, 0, tiled=False)]
    all_to_all x1 -> x2, waiting for transfers between devices: 4.9 us -> 13.6 us  [reduce_heads(): part = lax.all_to_all(total.astype(jnp.bfloat16), 'hz', 0, 0, tiled=False)]
    psum x1, waiting for transfers between devices: 102 us -> 98.3 us  [on_device(): summed_proj = lax.psum(projected.astype(jnp.bfloat16), WIDTH)]
    all_to_all x1 -> x2, starting transfers between devices: 5.1 us -> 8.35 us  [reduce_heads(): part = lax.all_to_all(total.astype(jnp.bfloat16), 'hz', 0, 0, tiled=False)]
    dot_general x2 -> x4, matrix products: 4.56 us -> 7.58 us  [the longest x2 6.46 us: on_device(): jnp.dot(hidden, down_weight[:, cols], preferred_element_type=jnp.float32)]
  transfers between devices with their start and end apart: 3 -> 8, of which waited for: 2 -> 7; matrix products, arithmetic and copies ran while one was open for 3% -> 10% of each run, Pallas kernels for 0% -> 0%
where the time goes in v12:
time: 296 us; the launch traced here: 294 us
  waiting for transfers between devices  151 us (51%)
  blocking collectives  38.3 us (13%)
  starting transfers between devices  35.1 us (12%)
  other arithmetic  26.3 us (9%)
  local copies, waits for them, and re-layouts  15.2 us (5%)
  between operations  14.4 us (5%)
  matrix products  14 us (5%)
    psum x1, waiting for transfers between devices, on_device(): summed_proj = lax.psum(projected.astype(jnp.bfloat16), WIDTH)  98.3 us
    all_to_all x1, blocking collectives, gather_heads(): block = lax.all_to_all(spread, ('hy', 'hx'), 0, 0, tiled=False)  38.3 us
    all_to_all x2, waiting for transfers between devices, reduce_heads(): part = lax.all_to_all(part, ('hy', 'hx'), 0, 0, tiled=False)  29.3 us
    all_to_all x2, waiting for transfers between devices, reduce_heads(): part = lax.all_to_all(total.astype(jnp.bfloat16), 'hz', 0, 0, tiled=False)  13.6 us
    convert_element_type x1, other arithmetic, on_device(): jax.nn.gelu(summed_proj[:, qkv_cols:].astype(jnp.float32) + up_bias, appr...  12.9 us
    all_to_all x2, starting transfers between devices, reduce_heads(): part = lax.all_to_all(part, ('hy', 'hx'), 0, 0, tiled=False)  10.5 us
    all_to_all x2, starting transfers between devices, reduce_heads(): part = lax.all_to_all(total.astype(jnp.bfloat16), 'hz', 0, 0, tiled=False)  8.35 us
    dot_general x2, matrix products, on_device(): jnp.dot(hidden, down_weight[:, cols], preferred_element_type=jnp.float32)  6.46 us
  transfers between devices with their start and end apart: 8, of which 7 were waited for; matrix products, arithmetic and copies ran while one was open for 10% of the time, Pallas kernels for 0%

profile of v12, /device:TPU:96, one launch (start us, length us, event | category | flops | bytes accessed | tf_op | source)
XLA Modules:
  0.0 294.4 jit_solution(6121722709337964476)
XLA Ops:
  7.2 4.6 %collective-permute-start = (bf16[48,768]{1,0:T(8,128)(2,1)}, bf16[48,768]{1,0:T(8,128)(2,1)S(1)}, u32[]{:S(2)}, u32[]{:S(2)}) collective-permute-start(bf16[48,768]{1,0:T(8,128)(2,1)} %param.14), channel_id=1, source_target_pairs={{0,128},{128,0},{1,129},{129,1},{2,130},{130,2},{3,131},{131,3},{4... | collective-permute-start | bytes 221192 | tf_op jit(solution)/shard_map/ppermute | solution.py:84
  11.8 1.0 convert_reduce_fusion
  12.8 0.6 broadcast_in_dim.49
  13.4 5.2 %all-to-all-start = ((f32[16,2,48]{2,1,0:T(2,128)}), f32[16,2,48]{2,1,0:T(2,128)S(1)}, u32[]{:S(2)}, u32[]{:S(2)}) async-start(f32[16,2,48]{2,1,0:T(2,128)} %broadcast_in_dim.49), calls=%async_computation | async-start | bytes 32768 | tf_op jit(solution)/shard_map/all_to_all | solution.py:87
  18.9 4.3 %all-to-all-done = f32[16,2,48]{2,1,0:T(2,128)S(1)} async-done(((f32[16,2,48]{2,1,0:T(2,128)}), f32[16,2,48]{2,1,0:T(2,128)S(1)}, u32[]{:S(2)}, u32[]{:S(2)}) %all-to-all-start) | async-done | bytes 6176 | tf_op jit(solution)/shard_map/all_to_all | solution.py:87
  23.4 0.9 pad_maximum_fusion.2
  24.3 0.6 gather_fusion
  25.2 38.3 %all_to_all.35 = bf16[16,96,768]{2,1,0:T(8,128)(2,1)S(1)} all-to-all(bf16[16,96,768]{2,1,0:T(8,128)(2,1)S(1)} %broadcast_in_dim.50), channel_id=1, replica_groups=mesh['hz'=2,'hy'=4,'hx'=4,'wz'=4,'wc'=2] {'hy','hx'}, dimensions={0} | all-to-all | bytes 4718592 | tf_op jit(solution)/shard_map/all_to_all | solution.py:48
  63.5 0.6 convert_bitcast_fusion
  64.9 1.1 fusion.4
  66.0 1.6 convolution_convert_fusion.1
  67.6 2.1 convolution_convert_fusion
  69.7 2.2 pad_maximum_fusion
  71.9 0.7 copy-done.4
  73.9 0.4 multiply_cosine_fusion
  74.3 0.5 fusion.26
  74.8 98.3 %all-reduce.2.cloned.1.call-done = bf16[1536,1344]{0,1:T(8,128)(2,1)} async-done(((bf16[1536,1344]{0,1:T(8,128)(2,1)}), bf16[1536,1344]{0,1:T(8,128)(2,1)}) %all-reduce.2.cloned.1.call-update) | async-done | bytes 4128784 | tf_op jit(solution)/shard_map/psum | solution.py:108
  173.1 1.8 convert_add_fusion.1
  175.0 1.7 copy-done.1
  177.3 0.8 copy-done.2
  178.1 0.8 fusion.61
  178.9 0.7 fusion.20
  179.7 2.0 fusion.34
  181.8 0.9 broadcast_in_dim.93
  182.7 6.4 %all-to-all-start.2 = ((bf16[8,192,192]{2,1,0:T(8,128)(2,1)}), bf16[8,192,192]{2,1,0:T(8,128)(2,1)S(1)}, u32[]{:S(2)}, u32[]{:S(2)}) async-start(bf16[8,192,192]{2,1,0:T(8,128)(2,1)} %broadcast_in_dim.93), calls=%async_computation.2 | async-start | bytes 1572864 | tf_op jit(solution)/shard_map/all_to_all | solution.py:151
  189.1 12.9 %fusion.2 = bf16[1536,768]{0,1:T(8,128)(2,1)} fusion(bf16[1536,1344]{0,1:T(8,128)(2,1)} %all-reduce.2.cloned.1.call-done, f32[768]{0:T(1024)S(1)} %copy-done.12), kind=kLoop, calls=%fused_computation.4 | loop fusion | flops 79036416 | bytes 4721664 | tf_op jit(solution)/shard_map/convert_element_type | solution.py:158
  202.0 5.5 %all-to-all-done.2 = bf16[8,192,192]{2,1,0:T(8,128)(2,1)S(1)} async-done(((bf16[8,192,192]{2,1,0:T(8,128)(2,1)}), bf16[8,192,192]{2,1,0:T(8,128)(2,1)S(1)}, u32[]{:S(2)}, u32[]{:S(2)}) %all-to-all-start.2) | async-done | bytes 589856 | tf_op jit(solution)/shard_map/all_to_all | solution.py:151
  207.5 0.6 fusion.44
  208.1 3.2 %fusion.19 = bf16[1536,384]{1,0:T(8,128)(2,1)S(1)} fusion(f32[1536,384]{1,0:T(8,128)S(1)} %fusion.44, bf16[1536,768]{0,1:T(8,128)(2,1)} %fusion.2, bf16[768,768]{1,0:T(8,128)(2,1)} %param.26), kind=kOutput, calls=%fused_computation.39 | convolution fusion | flops 907149312 | bytes 6488064 | tf_op jit(solution)/shard_map/dot_general | solution.py:166
  211.3 1.1 copy.106
  212.4 6.8 %all-to-all-start.5 = ((bf16[16,2,48,384]{3,2,1,0:T(8,128)(2,1)}), bf16[16,2,48,384]{3,2,1,0:T(8,128)(2,1)S(1)}, u32[]{:S(2)}, u32[]{:S(2)}) async-start(bf16[16,2,48,384]{3,2,1,0:T(8,128)(2,1)} %bitcast.78), calls=%async_computation.5 | async-start | bytes 2359296 | tf_op jit(solution)/shard_map/all_to_all | solution.py:59
  219.3 0.6 fusion.46
  219.8 3.2 %fusion.18 = bf16[1536,384]{1,0:T(8,128)(2,1)S(1)} fusion(f32[1536,384]{1,0:T(8,128)S(1)} %fusion.46, bf16[1536,768]{0,1:T(8,128)(2,1)} %fusion.2, bf16[768,768]{1,0:T(8,128)(2,1)} %param.26), kind=kOutput, calls=%fused_computation.38 | convolution fusion | flops 907149312 | bytes 6488064 | tf_op jit(solution)/shard_map/dot_general | solution.py:166
  223.1 1.2 copy.107
  224.3 14.5 %all-to-all-done.5 = bf16[16,2,48,384]{3,2,1,0:T(8,128)(2,1)S(1)} async-done(((bf16[16,2,48,384]{3,2,1,0:T(8,128)(2,1)}), bf16[16,2,48,384]{3,2,1,0:T(8,128)(2,1)S(1)}, u32[]{:S(2)}, u32[]{:S(2)}) %all-to-all-start.5) | async-done | bytes 1179680 | tf_op jit(solution)/shard_map/all_to_all | solution.py:59
  238.8 3.7 %all-to-all-start.3 = ((bf16[16,2,48,384]{3,2,1,0:T(8,128)(2,1)}), bf16[16,2,48,384]{3,2,1,0:T(8,128)(2,1)S(1)}, u32[]{:S(2)}, u32[]{:S(2)}) async-start(bf16[16,2,48,384]{3,2,1,0:T(8,128)(2,1)} %bitcast.77), calls=%async_computation.3 | async-start | bytes 2359296 | tf_op jit(solution)/shard_map/all_to_all | solution.py:59
  242.5 1.7 constant_dynamic-slice_fusion
  244.2 1.6 copy.85
  245.9 0.8 reduce_sum.84
  246.7 14.8 %all-to-all-done.3 = bf16[16,2,48,384]{3,2,1,0:T(8,128)(2,1)S(1)} async-done(((bf16[16,2,48,384]{3,2,1,0:T(8,128)(2,1)}), bf16[16,2,48,384]{3,2,1,0:T(8,128)(2,1)S(1)}, u32[]{:S(2)}, u32[]{:S(2)}) %all-to-all-start.3) | async-done | bytes 1179680 | tf_op jit(solution)/shard_map/all_to_all | solution.py:59
  261.4 5.0 %all-to-all-start.6 = ((bf16[2,48,384]{2,1,0:T(8,128)(2,1)}), bf16[2,48,384]{2,1,0:T(8,128)(2,1)S(1)}, u32[]{:S(2)}, u32[]{:S(2)}) async-start(bf16[2,48,384]{2,1,0:T(8,128)(2,1)} %reduce_sum.84), calls=%async_computation.6 | async-start | bytes 147456 | tf_op jit(solution)/shard_map/all_to_all | solution.py:61
  266.5 1.0 constant_dynamic-slice_fusion.1
  267.5 0.7 copy.84
  268.2 0.8 reduce_sum.82
  269.0 5.5 %all-to-all-done.6 = bf16[2,48,384]{2,1,0:T(8,128)(2,1)S(1)} async-done(((bf16[2,48,384]{2,1,0:T(8,128)(2,1)}), bf16[2,48,384]{2,1,0:T(8,128)(2,1)S(1)}, u32[]{:S(2)}, u32[]{:S(2)}) %all-to-all-start.6) | async-done | bytes 73760 | tf_op jit(solution)/shard_map/all_to_all | solution.py:61
  274.6 3.3 %all-to-all-start.4 = ((bf16[2,48,384]{2,1,0:T(8,128)(2,1)}), bf16[2,48,384]{2,1,0:T(8,128)(2,1)S(1)}, u32[]{:S(2)}, u32[]{:S(2)}) async-start(bf16[2,48,384]{2,1,0:T(8,128)(2,1)} %reduce_sum.82), calls=%async_computation.4 | async-start | bytes 147456 | tf_op jit(solution)/shard_map/all_to_all | solution.py:61
  277.9 8.0 %all-to-all-done.4 = bf16[2,48,384]{2,1,0:T(8,128)(2,1)S(1)} async-done(((bf16[2,48,384]{2,1,0:T(8,128)(2,1)}), bf16[2,48,384]{2,1,0:T(8,128)(2,1)S(1)}, u32[]{:S(2)}, u32[]{:S(2)}) %all-to-all-start.4) | async-done | bytes 73760 | tf_op jit(solution)/shard_map/all_to_all | solution.py:61
  286.0 1.5 fusion.43
  (68 shorter events, 3.8 us)
Async XLA Ops:
  7.2 60.4 %copy-start = (bf16[768,768]{1,0:T(8,128)(2,1)S(1)}, bf16[768,768]{1,0:T(8,128)(2,1)}, u32[]{:S(2)}) copy-start(bf16[768,768]{1,0:T(8,128)(2,1)} %param.24) | copy-start | bytes 3538948
  7.2 16.2 %collective-permute-start = (bf16[48,768]{1,0:T(8,128)(2,1)}, bf16[48,768]{1,0:T(8,128)(2,1)S(1)}, u32[]{:S(2)}, u32[]{:S(2)}) collective-permute-start(bf16[48,768]{1,0:T(8,128)(2,1)} %param.14), channel_id=1, source_target_pairs={{0,128},{128,0},{1,129},{129,1},{2,130},{130,2},{3,131},{131,3},{4... | collective-permute-start | bytes 221192 | tf_op jit(solution)/shard_map/ppermute | solution.py:84
  13.4 9.7 %all-to-all-start = ((f32[16,2,48]{2,1,0:T(2,128)}), f32[16,2,48]{2,1,0:T(2,128)S(1)}, u32[]{:S(2)}, u32[]{:S(2)}) async-start(f32[16,2,48]{2,1,0:T(2,128)} %broadcast_in_dim.49), calls=%async_computation | async-start | bytes 32768 | tf_op jit(solution)/shard_map/all_to_all | solution.py:87
  18.6 154.4 %all-reduce.2.cloned.1.call-start = ((), (), s32[]{:S(2)}) async-start(), calls=%async_computation.7 | async-start | bytes 8257536 | tf_op jit(solution)/shard_map/psum | solution.py:108
  64.1 0.7 copy-start.5
  64.1 0.7 copy-start.6
  64.1 0.7 copy-start.7
  64.1 0.7 copy-start.8
  64.8 1.2 copy-start.13
  71.9 0.7 copy-start.4
  71.9 101.2 %copy-start.9 = (f32[576]{0:T(1024)S(1)}, f32[576]{0:T(1024)}, u32[]{:S(2)}) copy-start(f32[576]{0:T(1024)} %param.21) | copy-start | bytes 6916
  174.9 1.8 copy-start.1
  177.3 0.8 copy-start.2
  179.7 9.4 %copy-start.12 = (f32[768]{0:T(1024)S(1)}, f32[768]{0:T(1024)}, u32[]{:S(2)}) copy-start(f32[768]{0:T(1024)} %param.25) | copy-start | bytes 9220
  181.6 25.9 %copy-start.3 = (bf16[192,768]{1,0:T(8,128)(2,1)S(1)}, bf16[192,768]{1,0:T(8,128)(2,1)}, u32[]{:S(2)}) copy-start(bf16[192,768]{1,0:T(8,128)(2,1)} %param.22) | copy-start | bytes 884740
  182.7 24.8 %all-to-all-start.2 = ((bf16[8,192,192]{2,1,0:T(8,128)(2,1)}), bf16[8,192,192]{2,1,0:T(8,128)(2,1)S(1)}, u32[]{:S(2)}, u32[]{:S(2)}) async-start(bf16[8,192,192]{2,1,0:T(8,128)(2,1)} %broadcast_in_dim.93), calls=%async_computation.2 | async-start | bytes 1572864 | tf_op jit(solution)/shard_map/all_to_all | solution.py:151
  212.4 26.4 %all-to-all-start.5 = ((bf16[16,2,48,384]{3,2,1,0:T(8,128)(2,1)}), bf16[16,2,48,384]{3,2,1,0:T(8,128)(2,1)S(1)}, u32[]{:S(2)}, u32[]{:S(2)}) async-start(bf16[16,2,48,384]{3,2,1,0:T(8,128)(2,1)} %bitcast.78), calls=%async_computation.5 | async-start | bytes 2359296 | tf_op jit(solution)/shard_map/all_to_all | solution.py:59
  223.1 62.9 %copy-start.10 = (f32[768]{0:T(1024)S(1)}, f32[768]{0:T(1024)}, u32[]{:S(2)}) copy-start(f32[768]{0:T(1024)} %param.27) | copy-start | bytes 9220
  223.1 62.9 %copy-start.11 = (f32[768]{0:T(1024)S(1)}, f32[768]{0:T(1024)}, u32[]{:S(2)}) copy-start(f32[768]{0:T(1024)} %param.23) | copy-start | bytes 9220
  238.8 22.6 %all-to-all-start.3 = ((bf16[16,2,48,384]{3,2,1,0:T(8,128)(2,1)}), bf16[16,2,48,384]{3,2,1,0:T(8,128)(2,1)S(1)}, u32[]{:S(2)}, u32[]{:S(2)}) async-start(bf16[16,2,48,384]{3,2,1,0:T(8,128)(2,1)} %bitcast.77), calls=%async_computation.3 | async-start | bytes 2359296 | tf_op jit(solution)/shard_map/all_to_all | solution.py:59
  261.4 13.1 %all-to-all-start.6 = ((bf16[2,48,384]{2,1,0:T(8,128)(2,1)}), bf16[2,48,384]{2,1,0:T(8,128)(2,1)S(1)}, u32[]{:S(2)}, u32[]{:S(2)}) async-start(bf16[2,48,384]{2,1,0:T(8,128)(2,1)} %reduce_sum.84), calls=%async_computation.6 | async-start | bytes 147456 | tf_op jit(solution)/shard_map/all_to_all | solution.py:61
  274.6 11.4 %all-to-all-start.4 = ((bf16[2,48,384]{2,1,0:T(8,128)(2,1)}), bf16[2,48,384]{2,1,0:T(8,128)(2,1)S(1)}, u32[]{:S(2)}, u32[]{:S(2)}) async-start(bf16[2,48,384]{2,1,0:T(8,128)(2,1)} %reduce_sum.82), calls=%async_computation.4 | async-start | bytes 147456 | tf_op jit(solution)/shard_map/all_to_all | solution.py:61
Sparse Core Ops, SparseCore 0:
  72.1 100.9 all-reduce.1

commit v13 on v11

--- a/solution.py
+++ b/solution.py
@@ -98,15 +98,14 @@
     block_f = gather_heads(normed.reshape(-1, normed.shape[2])).astype(jnp.float32)
     attn_in = (block_f * attn_gain + attn_shift).astype(jnp.bfloat16)
     mlp_in = (block_f * mlp_gain + mlp_shift).astype(jnp.bfloat16)
-    projected = jnp.concatenate(
-        [
-            jnp.dot(attn_in, qkv_weight, preferred_element_type=jnp.float32),
-            jnp.dot(mlp_in, up_weight, preferred_element_type=jnp.float32),
-        ],
-        axis=1,
+    qkv_sum, up_sum = lax.psum(
+        (
+            jnp.dot(attn_in, qkv_weight, preferred_element_type=jnp.float32).astype(jnp.bfloat16),
+            jnp.dot(mlp_in, up_weight, preferred_element_type=jnp.float32).astype(jnp.bfloat16),
+        ),
+        WIDTH,
     )
-    summed_proj = lax.psum(projected.astype(jnp.bfloat16), WIDTH)
-    all_tokens = projected.shape[0]
+    all_tokens = qkv_sum.shape[0]
     own_rows = all_tokens // lax.axis_size(WIDTH)
     row_zero = lax.axis_index(WIDTH) * own_rows
     positions = positions_of(segment_ids)
@@ -114,7 +113,7 @@
     own_index = row_zero + jnp.arange(own_rows, dtype=jnp.int32)
     score_scale = 1.0 / HD**0.5
     own_positions = lax.dynamic_slice_in_dim(positions, row_zero, own_rows)
-    shaped = (summed_proj[:, :qkv_cols].astype(jnp.float32) + qkv_bias).reshape(all_tokens, heads_dev, 3, HD)
+    shaped = (qkv_sum.astype(jnp.float32) + qkv_bias).reshape(all_tokens, heads_dev, 3, HD)
     own_shaped = lax.dynamic_slice_in_dim(shaped, row_zero, own_rows)
     queries = rotary(own_shaped[:, :, 0, :], own_positions).astype(jnp.bfloat16)
     key_heads = rotary(shaped[:, :, 1, :], positions).astype(jnp.bfloat16)
@@ -159,7 +158,7 @@
         dense_weight,
         preferred_element_type=jnp.float32,
     )
-    hidden = jax.nn.gelu(summed_proj[:, qkv_cols:].astype(jnp.float32) + up_bias, approximate=False).astype(
+    hidden = jax.nn.gelu(up_sum.astype(jnp.float32) + up_bias, approximate=False).astype(
         jnp.bfloat16
     )
     hidden = lax.optimization_barrier(hidden)

time: 275 us -> 283 us (1.029)
  blocking collectives: 76.3 us -> 38.3 us
  waiting for transfers between devices: 110 us -> 144 us
  starting transfers between devices: 21.3 us -> 28.2 us
  local copies, waits for them, and re-layouts: 11 us -> 15.2 us
    all_to_all x1 -> x0, blocking collectives: 38 us -> none  [reduce_heads(): part = lax.all_to_all(part, ('hy', 'hx'), 0, 0, tiled=False)]
    all_to_all x0 -> x1, waiting for transfers between devices: none -> 33.4 us  [reduce_heads(): part = lax.all_to_all(part, ('hy', 'hx'), 0, 0, tiled=False)]
    all_to_all x0 -> x1, starting transfers between devices: none -> 6.95 us  [reduce_heads(): part = lax.all_to_all(part, ('hy', 'hx'), 0, 0, tiled=False)]
  transfers between devices with their start and end apart: 5 -> 6, of which waited for: 4 -> 5; matrix products, arithmetic and copies ran while one was open for 9% -> 10% of each run, Pallas kernels for 0% -> 0%
where the time goes in v13:
time: 283 us; the launch traced here: 281 us
  waiting for transfers between devices  144 us (51%)
  blocking collectives  38.3 us (14%)
  starting transfers between devices  28.2 us (10%)
  other arithmetic  24.7 us (9%)
  matrix products  16.3 us (6%)
  local copies, waits for them, and re-layouts  15.2 us (5%)
  between operations  14.4 us (5%)
    psum x1, waiting for transfers between devices, on_device(): lax.psum((jnp.dot(attn_in, qkv_weight, preferred_element_type=jnp.float32...  97 us
    all_to_all x1, blocking collectives, gather_heads(): block = lax.all_to_all(spread, ('hy', 'hx'), 0, 0, tiled=False)  38.3 us
    all_to_all x1, waiting for transfers between devices, reduce_heads(): part = lax.all_to_all(part, ('hy', 'hx'), 0, 0, tiled=False)  33.4 us
    convert_element_type x1, other arithmetic, on_device(): jax.nn.gelu(up_sum.astype(jnp.float32) + up_bias, approximate=False)  11.5 us
    all_to_all x1, starting transfers between devices, reduce_heads(): part = lax.all_to_all(part, ('hy', 'hx'), 0, 0, tiled=False)  6.95 us
    all_to_all x1, waiting for transfers between devices, reduce_heads(): part = lax.all_to_all(total.astype(jnp.bfloat16), 'hz', 0, 0, tiled=False)  6.66 us
    all_to_all x1, starting transfers between devices, on_device(): lax.all_to_all(jnp.broadcast_to(attended[None], (lax.axis_size(WIDTH),) +...  6.4 us
  transfers between devices with their start and end apart: 6, of which 5 were waited for; matrix products, arithmetic and copies ran while one was open for 10% of the time, Pallas kernels for 0%

profile of v13, /device:TPU:96, one launch (start us, length us, event | category | flops | bytes accessed | tf_op | source)
XLA Modules:
  0.0 281.1 jit_solution(2169615749002579688)
XLA Ops:
  7.2 4.6 %collective-permute-start = (bf16[48,768]{1,0:T(8,128)(2,1)}, bf16[48,768]{1,0:T(8,128)(2,1)S(1)}, u32[]{:S(2)}, u32[]{:S(2)}) collective-permute-start(bf16[48,768]{1,0:T(8,128)(2,1)} %param.14), channel_id=1, source_target_pairs={{0,128},{128,0},{1,129},{129,1},{2,130},{130,2},{3,131},{131,3},{4... | collective-permute-start | bytes 221192 | tf_op jit(solution)/shard_map/ppermute | solution.py:84
  11.8 1.0 convert_reduce_fusion.1
  12.8 0.6 broadcast_in_dim.49
  13.4 5.2 %all-to-all-start = ((f32[16,2,48]{2,1,0:T(2,128)}), f32[16,2,48]{2,1,0:T(2,128)S(1)}, u32[]{:S(2)}, u32[]{:S(2)}) async-start(f32[16,2,48]{2,1,0:T(2,128)} %broadcast_in_dim.49), calls=%async_computation | async-start | bytes 32768 | tf_op jit(solution)/shard_map/all_to_all | solution.py:87
  18.9 4.3 %all-to-all-done = f32[16,2,48]{2,1,0:T(2,128)S(1)} async-done(((f32[16,2,48]{2,1,0:T(2,128)}), f32[16,2,48]{2,1,0:T(2,128)S(1)}, u32[]{:S(2)}, u32[]{:S(2)}) %all-to-all-start) | async-done | bytes 6176 | tf_op jit(solution)/shard_map/all_to_all | solution.py:87
  23.4 0.9 pad_maximum_fusion.1
  24.3 0.6 gather_fusion
  25.0 0.2 broadcast_in_dim.50
  25.2 38.3 %all_to_all.25 = bf16[16,96,768]{2,1,0:T(8,128)(2,1)S(1)} all-to-all(bf16[16,96,768]{2,1,0:T(8,128)(2,1)S(1)} %broadcast_in_dim.50), channel_id=1, replica_groups=mesh['hz'=2,'hy'=4,'hx'=4,'wz'=4,'wc'=2] {'hy','hx'}, dimensions={0} | all-to-all | bytes 4718592 | tf_op jit(solution)/shard_map/all_to_all | solution.py:48
  63.5 0.6 convert_bitcast_fusion
  64.2 0.4 copy.71
  64.6 0.2 copy-done.5
  64.8 1.1 fusion.4
  65.9 3.4 %convolution_convert_fusion = bf16[1536,768]{1,0:T(8,128)(2,1)} fusion(bf16[1536,768]{1,0:T(8,128)(2,1)S(1)} %get-tuple-element.31, bf16[768,768]{1,0:T(8,128)(2,1)S(1)} %copy-done), kind=kOutput, calls=%fused_computation.32 | convolution fusion | flops 1813118976 | bytes 5898240 | tf_op jit(solution)/shard_map/dot_general | solution.py:104
  69.4 2.8 convolution_convert_fusion.1
  72.4 0.3 reduce-window.9
  73.1 0.1 multiply_cosine_fusion.1
  73.3 0.8 copy.73
  74.0 0.8 copy.74
  74.8 1.1 multiply_cosine_fusion
  75.9 0.5 fusion.24
  76.4 97.0 %all-reduce.3.cloned.1.call-done = (bf16[1536,768]{1,0:T(8,128)(2,1)}, bf16[1536,576]{0,1:T(8,128)(2,1)}) async-done(((bf16[1536,768]{1,0:T(8,128)(2,1)}, bf16[1536,576]{0,1:T(8,128)(2,1)}), (bf16[1536,768]{1,0:T(8,128)(2,1)}, bf16[1536,576]{0,1:T(8,128)(2,1)})) %all-reduce.3.cloned.1.call-update) | async-done | bytes 4128784 | tf_op jit(solution)/shard_map/psum | solution.py:101
  173.4 1.8 convert_add_fusion.1
  175.3 1.7 copy-done.1
  177.1 0.1 copy.87
  177.3 1.0 subtract_convert_fusion
  178.3 1.1 subtract_convert_fusion.1
  179.5 0.9 copy-done.2
  180.3 0.8 fusion.53
  181.2 0.7 fusion.18
  181.9 2.0 fusion.32
  184.0 1.0 broadcast_in_dim.93
  185.0 6.4 %all-to-all-start.2 = ((bf16[8,192,192]{2,1,0:T(8,128)(2,1)}), bf16[8,192,192]{2,1,0:T(8,128)(2,1)S(1)}, u32[]{:S(2)}, u32[]{:S(2)}) async-start(bf16[8,192,192]{2,1,0:T(8,128)(2,1)} %broadcast_in_dim.93), calls=%async_computation.2 | async-start | bytes 1572864 | tf_op jit(solution)/shard_map/all_to_all | solution.py:151
  191.4 11.5 %fusion.2 = bf16[1536,768]{1,0:T(8,128)(2,1)S(1)} fusion(bf16[1536,768]{1,0:T(8,128)(2,1)} %get-tuple-element.28, f32[768]{0:T(1024)S(1)} %copy-done.12), kind=kLoop, calls=%fused_computation.4 | loop fusion | flops 79036416 | bytes 4721664 | tf_op jit(solution)/shard_map/convert_element_type | solution.py:161
  202.9 4.2 %fusion.55 = f32[1536,768]{1,0:T(8,128)} fusion(bf16[1536,768]{1,0:T(8,128)(2,1)S(1)} %fusion.2, bf16[768,768]{1,0:T(8,128)(2,1)S(1)} %copy-done.13), kind=kOutput, calls=%fused_computation.115 | convolution fusion | flops 1811939328 | bytes 8257536 | tf_op jit(solution)/shard_map/dot_general | solution.py:165
  207.1 2.7 all-to-all-done.2
  209.8 3.1 %add_convert_fusion = bf16[1536,768]{1,0:T(8,128)(2,1)S(1)} fusion(f32[1536,768]{1,0:T(8,128)} %fusion.55, bf16[1536,192]{1,0:T(8,128)(2,1)S(1)} %bitcast.73, bf16[192,768]{1,0:T(8,128)(2,1)S(1)} %copy-done.3), kind=kOutput, calls=%fused_computation.12 | convolution fusion | flops 455344128 | bytes 7962624 | tf_op jit(solution)/shard_map/dot_general | solution.py:150
  212.9 1.6 copy.100
  214.5 6.9 %all-to-all-start.3 = ((bf16[16,2,48,768]{3,2,1,0:T(8,128)(2,1)}), bf16[16,2,48,768]{3,2,1,0:T(8,128)(2,1)S(1)}, u32[]{:S(2)}, u32[]{:S(2)}) async-start(bf16[16,2,48,768]{3,2,1,0:T(8,128)(2,1)} %bitcast.67), calls=%async_computation.3 | async-start | bytes 4718592 | tf_op jit(solution)/shard_map/all_to_all | solution.py:59
  221.5 1.7 constant_dynamic-slice_fusion.1
  223.1 1.6 copy.79
  224.8 33.4 %all-to-all-done.3 = bf16[16,2,48,768]{3,2,1,0:T(8,128)(2,1)S(1)} async-done(((bf16[16,2,48,768]{3,2,1,0:T(8,128)(2,1)}), bf16[16,2,48,768]{3,2,1,0:T(8,128)(2,1)S(1)}, u32[]{:S(2)}, u32[]{:S(2)}) %all-to-all-start.3) | async-done | bytes 2359328 | tf_op jit(solution)/shard_map/all_to_all | solution.py:59
  258.2 1.0 reduce_sum.61
  259.2 5.0 %all-to-all-start.4 = ((bf16[2,48,768]{2,1,0:T(8,128)(2,1)}), bf16[2,48,768]{2,1,0:T(8,128)(2,1)S(1)}, u32[]{:S(2)}, u32[]{:S(2)}) async-start(bf16[2,48,768]{2,1,0:T(8,128)(2,1)} %reduce_sum.61), calls=%async_computation.4 | async-start | bytes 294912 | tf_op jit(solution)/shard_map/all_to_all | solution.py:61
  264.2 1.1 constant_dynamic-slice_fusion
  265.3 0.7 copy.80
  266.1 6.7 %all-to-all-done.4 = bf16[2,48,768]{2,1,0:T(8,128)(2,1)S(1)} async-done(((bf16[2,48,768]{2,1,0:T(8,128)(2,1)}), bf16[2,48,768]{2,1,0:T(8,128)(2,1)S(1)}, u32[]{:S(2)}, u32[]{:S(2)}) %all-to-all-start.4) | async-done | bytes 147488 | tf_op jit(solution)/shard_map/all_to_all | solution.py:61
  272.8 1.5 fusion.39
  (60 shorter events, 1.8 us)
Async XLA Ops:
  7.2 58.7 %copy-start = (bf16[768,768]{1,0:T(8,128)(2,1)S(1)}, bf16[768,768]{1,0:T(8,128)(2,1)}, u32[]{:S(2)}) copy-start(bf16[768,768]{1,0:T(8,128)(2,1)} %param.24) | copy-start | bytes 3538948
  7.2 16.2 %collective-permute-start = (bf16[48,768]{1,0:T(8,128)(2,1)}, bf16[48,768]{1,0:T(8,128)(2,1)S(1)}, u32[]{:S(2)}, u32[]{:S(2)}) collective-permute-start(bf16[48,768]{1,0:T(8,128)(2,1)} %param.14), channel_id=1, source_target_pairs={{0,128},{128,0},{1,129},{129,1},{2,130},{130,2},{3,131},{131,3},{4... | collective-permute-start | bytes 221192 | tf_op jit(solution)/shard_map/ppermute | solution.py:84
  13.4 9.7 %all-to-all-start = ((f32[16,2,48]{2,1,0:T(2,128)}), f32[16,2,48]{2,1,0:T(2,128)S(1)}, u32[]{:S(2)}, u32[]{:S(2)}) async-start(f32[16,2,48]{2,1,0:T(2,128)} %broadcast_in_dim.49), calls=%async_computation | async-start | bytes 32768 | tf_op jit(solution)/shard_map/all_to_all | solution.py:87
  18.6 154.7 %all-reduce.3.cloned.1.call-start = ((), (), s32[]{:S(2)}) async-start(), calls=%async_computation.5 | async-start | bytes 8257536 | tf_op jit(solution)/shard_map/psum | solution.py:101
  64.1 0.7 copy-start.5
  64.1 0.7 copy-start.6
  64.1 0.7 copy-start.7
  64.1 0.7 copy-start.8
  65.9 3.4 %copy-start.14 = (bf16[768,576]{0,1:T(8,128)(2,1)S(1)}, bf16[768,576]{0,1:T(8,128)(2,1)}, u32[]{:S(2)}) copy-start(bf16[768,576]{0,1:T(8,128)(2,1)} %param.20) | copy-start | bytes 2654212
  69.4 2.8 %copy-start.4 = (s32[1536]{0:T(1024)S(1)}, s32[1536]{0:T(1024)}, u32[]{:S(2)}) copy-start(s32[1536]{0:T(1024)} %param.15) | copy-start | bytes 18436
  72.2 101.2 %copy-start.9 = (f32[576]{0:T(1024)S(1)}, f32[576]{0:T(1024)}, u32[]{:S(2)}) copy-start(f32[576]{0:T(1024)} %param.21) | copy-start | bytes 6916
  175.2 1.8 copy-start.1
  179.5 0.9 copy-start.2
  181.2 10.2 %copy-start.12 = (f32[768]{0:T(1024)S(1)}, f32[768]{0:T(1024)}, u32[]{:S(2)}) copy-start(f32[768]{0:T(1024)} %param.25) | copy-start | bytes 9220
  183.9 19.0 %copy-start.13 = (bf16[768,768]{1,0:T(8,128)(2,1)S(1)}, bf16[768,768]{1,0:T(8,128)(2,1)}, u32[]{:S(2)}) copy-start(bf16[768,768]{1,0:T(8,128)(2,1)} %param.26) | copy-start | bytes 3538948
  185.0 24.8 %all-to-all-start.2 = ((bf16[8,192,192]{2,1,0:T(8,128)(2,1)}), bf16[8,192,192]{2,1,0:T(8,128)(2,1)S(1)}, u32[]{:S(2)}, u32[]{:S(2)}) async-start(bf16[8,192,192]{2,1,0:T(8,128)(2,1)} %broadcast_in_dim.93), calls=%async_computation.2 | async-start | bytes 1572864 | tf_op jit(solution)/shard_map/all_to_all | solution.py:151
  202.9 6.9 %copy-start.3 = (bf16[192,768]{1,0:T(8,128)(2,1)S(1)}, bf16[192,768]{1,0:T(8,128)(2,1)}, u32[]{:S(2)}) copy-start(bf16[192,768]{1,0:T(8,128)(2,1)} %param.22) | copy-start | bytes 884740
  214.5 58.2 %copy-start.10 = (f32[768]{0:T(1024)S(1)}, f32[768]{0:T(1024)}, u32[]{:S(2)}) copy-start(f32[768]{0:T(1024)} %param.27) | copy-start | bytes 9220
  214.5 58.2 %copy-start.11 = (f32[768]{0:T(1024)S(1)}, f32[768]{0:T(1024)}, u32[]{:S(2)}) copy-start(f32[768]{0:T(1024)} %param.23) | copy-start | bytes 9220
  214.5 43.7 %all-to-all-start.3 = ((bf16[16,2,48,768]{3,2,1,0:T(8,128)(2,1)}), bf16[16,2,48,768]{3,2,1,0:T(8,128)(2,1)S(1)}, u32[]{:S(2)}, u32[]{:S(2)}) async-start(bf16[16,2,48,768]{3,2,1,0:T(8,128)(2,1)} %bitcast.67), calls=%async_computation.3 | async-start | bytes 4718592 | tf_op jit(solution)/shard_map/all_to_all | solution.py:59
  259.2 13.5 %all-to-all-start.4 = ((bf16[2,48,768]{2,1,0:T(8,128)(2,1)}), bf16[2,48,768]{2,1,0:T(8,128)(2,1)S(1)}, u32[]{:S(2)}, u32[]{:S(2)}) async-start(bf16[2,48,768]{2,1,0:T(8,128)(2,1)} %reduce_sum.61), calls=%async_computation.4 | async-start | bytes 294912 | tf_op jit(solution)/shard_map/all_to_all | solution.py:61
Sparse Core Ops, SparseCore 0:
  72.3 101.0 all-reduce.2

commit v14 on v11

--- a/solution.py
+++ b/solution.py
@@ -58,8 +58,15 @@
     part = partial.reshape(nz, ny * nx, rows, cols).transpose(1, 0, 2, 3)
     part = lax.all_to_all(part, ("hy", "hx"), 0, 0, tiled=False)
     total = jnp.sum(part.astype(jnp.float32), 0)
-    part = lax.all_to_all(total.astype(jnp.bfloat16), "hz", 0, 0, tiled=False)
-    return jnp.sum(part.astype(jnp.float32), 0)
+    z = lax.axis_index("hz")
+    result = lax.dynamic_index_in_dim(total, z, 0, keepdims=False)
+    for k in range(1, nz):
+        outgoing = lax.dynamic_index_in_dim(total, (z + k) % nz, 0, keepdims=False)
+        incoming = lax.ppermute(
+            outgoing.astype(jnp.bfloat16), "hz", [(i, (i + k) % nz) for i in range(nz)]
+        )
+        result = result + incoming.astype(jnp.float32)
+    return result
 
 
 def on_device(

time: 275 us -> 275 us (level)
  blocking collectives: 76.3 us -> 38.3 us
  waiting for transfers between devices: 110 us -> 142 us
  starting transfers between devices: 21.3 us -> 27.1 us
  local copies, waits for them, and re-layouts: 11 us -> 14.7 us
    all_to_all x1 -> x0, blocking collectives: 38 us -> none  [reduce_heads(): part = lax.all_to_all(part, ('hy', 'hx'), 0, 0, tiled=False)]
    all_to_all x1, waiting for transfers between devices: 4.9 us -> 33.3 us  [reduce_heads(): part = lax.all_to_all(part, ('hy', 'hx'), 0, 0, tiled=False)]
    ppermute x0 -> x1, starting transfers between devices: none -> 3.88 us  [reduce_heads(): lax.ppermute(outgoing.astype(jnp.bfloat16), 'hz', [(i, (i + k) % nz) for...]
    ppermute x0 -> x1, waiting for transfers between devices: none -> 3.5 us  [reduce_heads(): lax.ppermute(outgoing.astype(jnp.bfloat16), 'hz', [(i, (i + k) % nz) for...]
    unnamed x33 -> x35, local copies, waits for them, and re-layouts: 4.54 us -> 6.13 us
  transfers between devices with their start and end apart: 5 -> 6, of which waited for: 4 -> 5; matrix products, arithmetic and copies ran while one was open for 9% -> 9% of each run, Pallas kernels for 0% -> 0%
where the time goes in v14:
time: 275 us
  waiting for transfers between devices  142 us (52%)
  blocking collectives  38.3 us (14%)
  starting transfers between devices  27.1 us (10%)
  other arithmetic  24.4 us (9%)
  local copies, waits for them, and re-layouts  14.7 us (5%)
  between operations  14.4 us (5%)
  matrix products  13.7 us (5%)
    psum x1, waiting for transfers between devices, on_device(): summed_proj = lax.psum(projected.astype(jnp.bfloat16), WIDTH)  98.9 us
    all_to_all x1, blocking collectives, gather_heads(): block = lax.all_to_all(spread, ('hy', 'hx'), 0, 0, tiled=False)  38.3 us
    all_to_all x1, waiting for transfers between devices, reduce_heads(): part = lax.all_to_all(part, ('hy', 'hx'), 0, 0, tiled=False)  33.3 us
    convert_element_type x1, other arithmetic, on_device(): jax.nn.gelu(summed_proj[:, qkv_cols:].astype(jnp.float32) + up_bias, appr...  12.1 us
    all_to_all x1, starting transfers between devices, reduce_heads(): part = lax.all_to_all(part, ('hy', 'hx'), 0, 0, tiled=False)  6.94 us
    all_to_all x1, starting transfers between devices, on_device(): lax.all_to_all(jnp.broadcast_to(attended[None], (lax.axis_size(WIDTH),) +...  6.42 us
    unnamed x35, local copies, waits for them, and re-layouts  6.13 us
  transfers between devices with their start and end apart: 6, of which 5 were waited for; matrix products, arithmetic and copies ran while one was open for 9% of the time, Pallas kernels for 0%

profile of v14, /device:TPU:96, one launch (start us, length us, event | category | flops | bytes accessed | tf_op | source)
XLA Modules:
  0.0 274.6 jit_solution(1816100779812883587)
XLA Ops:
  7.2 4.6 %collective-permute-start = (bf16[48,768]{1,0:T(8,128)(2,1)}, bf16[48,768]{1,0:T(8,128)(2,1)S(1)}, u32[]{:S(2)}, u32[]{:S(2)}) collective-permute-start(bf16[48,768]{1,0:T(8,128)(2,1)} %param.14), channel_id=1, source_target_pairs={{0,128},{128,0},{1,129},{129,1},{2,130},{130,2},{3,131},{131,3},{4... | collective-permute-start | bytes 221192 | tf_op jit(solution)/shard_map/ppermute | solution.py:91
  11.8 1.0 convert_reduce_fusion.1
  12.8 0.6 broadcast_in_dim.49
  13.4 5.2 %all-to-all-start = ((f32[16,2,48]{2,1,0:T(2,128)}), f32[16,2,48]{2,1,0:T(2,128)S(1)}, u32[]{:S(2)}, u32[]{:S(2)}) async-start(f32[16,2,48]{2,1,0:T(2,128)} %broadcast_in_dim.49), calls=%async_computation | async-start | bytes 32768 | tf_op jit(solution)/shard_map/all_to_all | solution.py:94
  18.9 4.3 %all-to-all-done = f32[16,2,48]{2,1,0:T(2,128)S(1)} async-done(((f32[16,2,48]{2,1,0:T(2,128)}), f32[16,2,48]{2,1,0:T(2,128)S(1)}, u32[]{:S(2)}, u32[]{:S(2)}) %all-to-all-start) | async-done | bytes 6176 | tf_op jit(solution)/shard_map/all_to_all | solution.py:94
  23.4 0.9 pad_maximum_fusion.2
  24.3 0.6 gather_fusion
  25.0 0.2 broadcast_in_dim.50
  25.2 38.3 %all_to_all.20 = bf16[16,96,768]{2,1,0:T(8,128)(2,1)S(1)} all-to-all(bf16[16,96,768]{2,1,0:T(8,128)(2,1)S(1)} %broadcast_in_dim.50), channel_id=1, replica_groups=mesh['hz'=2,'hy'=4,'hx'=4,'wz'=4,'wc'=2] {'hy','hx'}, dimensions={0} | all-to-all | bytes 4718592 | tf_op jit(solution)/shard_map/all_to_all | solution.py:48
  63.5 0.6 convert_bitcast_fusion
  64.2 0.4 copy.71
  64.6 0.2 copy-done.6
  64.9 1.1 fusion.4
  66.0 1.6 convolution_convert_fusion.1
  67.6 2.1 convolution_convert_fusion
  69.7 2.2 pad_maximum_fusion
  72.2 0.3 reduce-window.9
  72.9 0.2 multiply_cosine_fusion.1
  73.3 0.4 multiply_cosine_fusion
  73.7 0.5 fusion.24
  74.2 98.9 %all-reduce.2.cloned.1.call-done = bf16[1536,1344]{0,1:T(8,128)(2,1)} async-done(((bf16[1536,1344]{0,1:T(8,128)(2,1)}), bf16[1536,1344]{0,1:T(8,128)(2,1)}) %all-reduce.2.cloned.1.call-update) | async-done | bytes 4128784 | tf_op jit(solution)/shard_map/psum | solution.py:115
  173.0 1.8 convert_add_fusion.1
  174.8 0.1 constant_dynamic-slice_fusion.2
  175.0 1.6 copy-done.1
  176.7 0.1 copy.87
  177.0 0.1 subtract_convert_fusion.1
  177.2 0.9 copy-done.2
  178.1 0.8 fusion.54
  178.9 0.7 fusion.18
  179.6 2.0 fusion.32
  181.7 1.0 broadcast_in_dim.93
  182.7 6.4 %all-to-all-start.2 = ((bf16[8,192,192]{2,1,0:T(8,128)(2,1)}), bf16[8,192,192]{2,1,0:T(8,128)(2,1)S(1)}, u32[]{:S(2)}, u32[]{:S(2)}) async-start(bf16[8,192,192]{2,1,0:T(8,128)(2,1)} %broadcast_in_dim.93), calls=%async_computation.2 | async-start | bytes 1572864 | tf_op jit(solution)/shard_map/all_to_all | solution.py:159
  189.1 12.1 %fusion.2 = bf16[1536,768]{0,1:T(8,128)(2,1)S(1)} fusion(bf16[1536,1344]{0,1:T(8,128)(2,1)} %all-reduce.2.cloned.1.call-done, f32[768]{0:T(1024)S(1)} %copy-done.13), kind=kLoop, calls=%fused_computation.4 | loop fusion | flops 79036416 | bytes 4721664 | tf_op jit(solution)/shard_map/convert_element_type | solution.py:169
  201.3 4.2 %fusion.56 = f32[1536,768]{1,0:T(8,128)} fusion(bf16[1536,768]{0,1:T(8,128)(2,1)S(1)} %fusion.2, bf16[768,768]{1,0:T(8,128)(2,1)S(1)} %copy-done.14), kind=kOutput, calls=%fused_computation.119 | convolution fusion | flops 1811939328 | bytes 8257536 | tf_op jit(solution)/shard_map/dot_general | solution.py:173
  205.5 2.0 all-to-all-done.2
  207.5 3.1 %add_convert_fusion = bf16[1536,768]{1,0:T(8,128)(2,1)S(1)} fusion(f32[1536,768]{1,0:T(8,128)} %fusion.56, bf16[1536,192]{1,0:T(8,128)(2,1)S(1)} %bitcast.79, bf16[192,768]{1,0:T(8,128)(2,1)S(1)} %copy-done.4), kind=kOutput, calls=%fused_computation.13 | convolution fusion | flops 455344128 | bytes 7962624 | tf_op jit(solution)/shard_map/dot_general | solution.py:158
  210.6 1.6 copy.100
  212.3 6.9 %all-to-all-start.3 = ((bf16[16,2,48,768]{3,2,1,0:T(8,128)(2,1)}), bf16[16,2,48,768]{3,2,1,0:T(8,128)(2,1)S(1)}, u32[]{:S(2)}, u32[]{:S(2)}) async-start(bf16[16,2,48,768]{3,2,1,0:T(8,128)(2,1)} %bitcast.73), calls=%async_computation.3 | async-start | bytes 4718592 | tf_op jit(solution)/shard_map/all_to_all | solution.py:59
  219.2 1.7 constant_dynamic-slice_fusion
  221.0 1.6 copy.80
  222.6 33.3 %all-to-all-done.3 = bf16[16,2,48,768]{3,2,1,0:T(8,128)(2,1)S(1)} async-done(((bf16[16,2,48,768]{3,2,1,0:T(8,128)(2,1)}), bf16[16,2,48,768]{3,2,1,0:T(8,128)(2,1)S(1)}, u32[]{:S(2)}, u32[]{:S(2)}) %all-to-all-start.3) | async-done | bytes 2359328 | tf_op jit(solution)/shard_map/all_to_all | solution.py:59
  255.9 0.3 convert_reduce_fusion
  256.3 0.7 copy-done.3
  257.0 3.9 %collective-permute-start.1 = (bf16[48,768]{1,0:T(8,128)(2,1)S(1)}, bf16[48,768]{1,0:T(8,128)(2,1)S(1)}, u32[]{:S(2)}, u32[]{:S(2)}) collective-permute-start(bf16[48,768]{1,0:T(8,128)(2,1)S(1)} %fusion.45), channel_id=1, source_target_pairs={{0,128},{128,0},{1,129},{129,1},{2,130},{130,2},{3,131},{131,3},{4... | collective-permute-start | bytes 221192 | tf_op jit(solution)/shard_map/ppermute | solution.py:65
  260.9 1.0 constant_dynamic-slice_fusion.1
  261.9 0.7 copy.79
  262.6 3.5 %collective-permute-done.1 = bf16[48,768]{1,0:T(8,128)(2,1)S(1)} collective-permute-done((bf16[48,768]{1,0:T(8,128)(2,1)S(1)}, bf16[48,768]{1,0:T(8,128)(2,1)S(1)}, u32[]{:S(2)}, u32[]{:S(2)}) %collective-permute-start.1) | collective-permute-done | bytes 73760 | tf_op jit(solution)/shard_map/ppermute | solution.py:65
  266.1 1.6 fusion.39
  (63 shorter events, 2.1 us)
Async XLA Ops:
  7.2 60.4 %copy-start = (bf16[768,768]{1,0:T(8,128)(2,1)S(1)}, bf16[768,768]{1,0:T(8,128)(2,1)}, u32[]{:S(2)}) copy-start(bf16[768,768]{1,0:T(8,128)(2,1)} %param.24) | copy-start | bytes 3538948
  7.2 16.2 %collective-permute-start = (bf16[48,768]{1,0:T(8,128)(2,1)}, bf16[48,768]{1,0:T(8,128)(2,1)S(1)}, u32[]{:S(2)}, u32[]{:S(2)}) collective-permute-start(bf16[48,768]{1,0:T(8,128)(2,1)} %param.14), channel_id=1, source_target_pairs={{0,128},{128,0},{1,129},{129,1},{2,130},{130,2},{3,131},{131,3},{4... | collective-permute-start | bytes 221192 | tf_op jit(solution)/shard_map/ppermute | solution.py:91
  13.4 9.7 %all-to-all-start = ((f32[16,2,48]{2,1,0:T(2,128)}), f32[16,2,48]{2,1,0:T(2,128)S(1)}, u32[]{:S(2)}, u32[]{:S(2)}) async-start(f32[16,2,48]{2,1,0:T(2,128)} %broadcast_in_dim.49), calls=%async_computation | async-start | bytes 32768 | tf_op jit(solution)/shard_map/all_to_all | solution.py:94
  18.6 154.4 %all-reduce.2.cloned.1.call-start = ((), (), s32[]{:S(2)}) async-start(), calls=%async_computation.4 | async-start | bytes 8257536 | tf_op jit(solution)/shard_map/psum | solution.py:115
  64.1 0.7 copy-start.6
  64.1 0.7 copy-start.7
  64.1 0.7 copy-start.8
  64.1 0.7 copy-start.9
  64.8 1.2 copy-start.15
  69.7 2.3 copy-start.5
  69.7 103.3 %copy-start.10 = (f32[576]{0:T(1024)S(1)}, f32[576]{0:T(1024)}, u32[]{:S(2)}) copy-start(f32[576]{0:T(1024)} %param.21) | copy-start | bytes 6916
  174.8 1.8 copy-start.1
  177.2 0.9 copy-start.2
  178.9 10.2 %copy-start.13 = (f32[768]{0:T(1024)S(1)}, f32[768]{0:T(1024)}, u32[]{:S(2)}) copy-start(f32[768]{0:T(1024)} %param.25) | copy-start | bytes 9220
  181.6 19.7 %copy-start.14 = (bf16[768,768]{1,0:T(8,128)(2,1)S(1)}, bf16[768,768]{1,0:T(8,128)(2,1)}, u32[]{:S(2)}) copy-start(bf16[768,768]{1,0:T(8,128)(2,1)} %param.26) | copy-start | bytes 3538948
  182.7 24.8 %all-to-all-start.2 = ((bf16[8,192,192]{2,1,0:T(8,128)(2,1)}), bf16[8,192,192]{2,1,0:T(8,128)(2,1)S(1)}, u32[]{:S(2)}, u32[]{:S(2)}) async-start(bf16[8,192,192]{2,1,0:T(8,128)(2,1)} %broadcast_in_dim.93), calls=%async_computation.2 | async-start | bytes 1572864 | tf_op jit(solution)/shard_map/all_to_all | solution.py:159
  201.3 6.2 %copy-start.4 = (bf16[192,768]{1,0:T(8,128)(2,1)S(1)}, bf16[192,768]{1,0:T(8,128)(2,1)}, u32[]{:S(2)}) copy-start(bf16[192,768]{1,0:T(8,128)(2,1)} %param.22) | copy-start | bytes 884740
  212.3 53.9 %copy-start.11 = (f32[768]{0:T(1024)S(1)}, f32[768]{0:T(1024)}, u32[]{:S(2)}) copy-start(f32[768]{0:T(1024)} %param.27) | copy-start | bytes 9220
  212.3 53.9 %copy-start.12 = (f32[768]{0:T(1024)S(1)}, f32[768]{0:T(1024)}, u32[]{:S(2)}) copy-start(f32[768]{0:T(1024)} %param.23) | copy-start | bytes 9220
  212.3 43.7 %all-to-all-start.3 = ((bf16[16,2,48,768]{3,2,1,0:T(8,128)(2,1)}), bf16[16,2,48,768]{3,2,1,0:T(8,128)(2,1)S(1)}, u32[]{:S(2)}, u32[]{:S(2)}) async-start(bf16[16,2,48,768]{3,2,1,0:T(8,128)(2,1)} %bitcast.73), calls=%async_computation.3 | async-start | bytes 4718592 | tf_op jit(solution)/shard_map/all_to_all | solution.py:59
  256.3 0.7 copy-start.3
  257.0 9.1 %collective-permute-start.1 = (bf16[48,768]{1,0:T(8,128)(2,1)S(1)}, bf16[48,768]{1,0:T(8,128)(2,1)S(1)}, u32[]{:S(2)}, u32[]{:S(2)}) collective-permute-start(bf16[48,768]{1,0:T(8,128)(2,1)S(1)} %fusion.45), channel_id=1, source_target_pairs={{0,128},{128,0},{1,129},{129,1},{2,130},{130,2},{3,131},{131,3},{4... | collective-permute-start | bytes 221192 | tf_op jit(solution)/shard_map/ppermute | solution.py:65
Sparse Core Ops, SparseCore 0:
  72.1 100.9 all-reduce.1
